TPU v7x, 128 devices: a whole 4x4x4 slice. The times are simulated.
128 devices in a mesh: wl: 8 (over x, z_hi), tile: 16 (over z_lo, y, core).
Axes of the slice: x: 4, y: 4, z: 4 (z_hi: 2, z_lo: 2; z = z_hi * 2 + z_lo), core: 2. Of those that a mesh axis runs over, the one named last changes fastest.
Arguments:
- density: float32 [32, 1024], P('tile', 'wl'), may hold values from 0 to 1
- foot_index: int32 [4, 128, 4096], P(None, 'tile'), may hold values from 0 to 2047, as said below
- foot_weight: bfloat16 [4, 128, 4096], P(None, 'tile'), may hold values from 0.099609375 to 0.3984375
- source_fwd: float32 [16, 128, 4096], P('wl', 'tile'), may hold values from -6 to 6
- source_adj: float32 [16, 128, 4096], P('wl', 'tile'), may hold values from -6 to 6
- omega: float32 [16], P('wl'), may hold values from 0.2 to 1.5
Outputs:
- forward_field: float32 [16, 128, 4096], P('wl', 'tile')
- density_grad: float32 [32, 1024], P('tile', 'wl')
Inputs may be any that keep to these rules, and one draw needn't show every extreme that they name: foot_index[f, x, y] = r * 1024 + c names coarse row r and column c of the strip of the tile holding row x, with r within one of (x mod 8) // 4 and c within two of y // 4; entry f = 0 is the cell's own block.
All inputs are finite; a program needn't handle non-finite values.
Results may differ from a plain program's by a relative error of at most 0.0003.
Values sent between devices are 32-bit elements; how exact they have to be, the bound alone decides.
No kernel may reach another device: no remote copies, remote signals or barrier semaphores. Data moves between devices by JAX's collectives and lax.ppermute only.
A program may use at most 192 MiB of HBM per device.

v0:
```python
import jax
import jax.numpy as jnp
from jax import lax
from jax.sharding import PartitionSpec as P

ITERS = 4
HALO = 4
SHIFTS = (-2, -1, 0, 1, 2)


time_step = 0.5
high_contrast = 4.0
drude_decay = 0.9
drude_gain = 0.5


def from_behind(value, axis, steps):
    count = lax.axis_size(axis)
    first, last = (max(0, -steps), min(count, count - steps))
    return lax.ppermute(value, axis, [(source, source + steps) for source in range(first, last)])


def with_halo(value, axis):
    above = from_behind(value[..., -HALO:, :], axis, 1)
    below = from_behind(value[..., :HALO, :], axis, -1)
    return jnp.concatenate([above, value, below], axis=-2)


def lane_shift(vector, shift):
    width = vector.shape[-1]
    pad = [(0, 0)] * (vector.ndim - 1) + [(abs(shift), abs(shift))]
    padded = jnp.pad(vector, pad)
    start = abs(shift) - shift
    return lax.slice_in_dim(padded, start, start + width, axis=vector.ndim - 1)


def march(source, drive, density_cell, inverse, valid):
    field_e = jnp.zeros_like(source)
    field_hx = jnp.zeros_like(source)
    field_hy = jnp.zeros_like(source)
    current = jnp.zeros_like(source)
    rows = source.shape[2]
    history = []
    for turn in range(ITERS):
        row_zero = jnp.zeros_like(source[:, :, :1, :])
        col_zero = jnp.zeros_like(source[:, :, :, :1])
        e_up = jnp.concatenate([field_e[:, :, 1:, :], row_zero], 2)
        e_right = jnp.concatenate([field_e[:, :, :, 1:], col_zero], 3)
        field_hx = field_hx - time_step * (e_right - field_e)
        field_hy = (field_hy + time_step * (e_up - field_e)) * valid
        current = drude_decay * current + drude_gain * density_cell * field_e
        hy_down = jnp.concatenate([row_zero, field_hy[:, :, :-1, :]], 2)
        hx_left = jnp.concatenate([col_zero, field_hx[:, :, :, :-1]], 3)
        field_e = (
            field_e
            + inverse * (field_hy - hy_down - (field_hx - hx_left) - current)
            + drive[turn] * source
        ) * valid
        history.append(field_e[:, :, HALO : rows - HALO, :])
    return history


def shards(density, foot_index, foot_weight, source_fwd, source_adj, omega):
    sources = jnp.stack([source_fwd, source_adj])
    sources_ext = with_halo(sources, "tile")
    strip = lax.all_gather(density, "wl", axis=1, tiled=True)
    block_rows, block_cols = strip.shape
    cells_x, cells_y = foot_index.shape[1:]
    factor = cells_y // block_cols
    weights = foot_weight.astype(jnp.float32)
    col_block = lax.broadcasted_iota(jnp.int32, (1, cells_y), 1) // factor
    key = (foot_index // block_cols) * len(SHIFTS) + (foot_index % block_cols - col_block[None]) + 2
    upsampled = jnp.repeat(strip, factor, axis=1)
    matched = []
    density_cell = jnp.zeros((cells_x, cells_y), jnp.float32)
    for row in range(block_rows):
        for slot, shift in enumerate(SHIFTS):
            code = row * len(SHIFTS) + slot
            weight_sum = jnp.sum(jnp.where(key == code, weights, 0.0), axis=0)
            matched.append(weight_sum)
            density_cell = density_cell + weight_sum * lane_shift(upsampled[row], -factor * shift)[None]
    density_ext = with_halo(density_cell, "tile")
    inverse_ext = time_step / (1.0 + high_contrast * density_ext)
    rows_ext = cells_x + 2 * HALO
    global_row = lax.axis_index("tile") * cells_x - HALO + lax.broadcasted_iota(jnp.int32, (rows_ext, 1), 0)
    valid = ((global_row >= 0) & (global_row < cells_x * lax.axis_size("tile"))).astype(jnp.float32)
    drive = [jnp.sin(omega * (turn + 1.0))[None, :, None, None] for turn in range(ITERS)]
    history = march(sources_ext, drive, density_ext, inverse_ext, valid)
    sense = jnp.zeros((cells_x, cells_y), jnp.float32)
    for turn in range(ITERS):
        sense = sense + jnp.sum(history[turn][1] * history[ITERS - 1 - turn][0], axis=0)
    total_waves = source_fwd.shape[0] * lax.axis_size("wl")
    scaled = high_contrast / total_waves * sense
    pooled_rows = []
    for row in range(block_rows):
        acc = jnp.zeros((cells_y,), jnp.float32)
        for slot, shift in enumerate(SHIFTS):
            per_col = jnp.sum(matched[row * len(SHIFTS) + slot] * scaled, axis=0)
            acc = acc + lane_shift(per_col, factor * shift)
        pooled_rows.append(acc.reshape(block_cols, factor).sum(axis=1))
    partial_grad = jnp.stack(pooled_rows)
    density_grad = lax.psum_scatter(partial_grad, "wl", scatter_dimension=1, tiled=True)
    return (history[ITERS - 1][0], density_grad)


def solution(mesh):
    in_specs = (
        P("tile", "wl"),
        P(None, "tile", None),
        P(None, "tile", None),
        P("wl", "tile", None),
        P("wl", "tile", None),
        P("wl"),
    )
    out_specs = (P("wl", "tile", None), P("tile", "wl"))
    return jax.shard_map(shards, mesh=mesh, in_specs=in_specs, out_specs=out_specs, check_vma=False)
```

profile of v0, /device:TPU:25, one launch (start us, length us, event | category | flops | bytes accessed | tf_op | source)
XLA Modules:
  0.0 136.1 jit_solution(15025737107666634582)
XLA Ops:
  7.2 0.6 copy-done.4
  7.8 20.4 %all_gather.3 = f32[2,1024]{1,0:T(2,128)S(1)} all-gather(f32[2,128]{1,0:T(2,128)S(1)} %copy-done.4), channel_id=1, replica_groups=mesh['wl'=8,'tile'=16] {'wl'}, dimensions={1}, use_global_device_ids=true | all-gather | bytes 9216 | tf_op jit(solution)/shard_map/all_gather | solution.py:66
  28.4 0.3 broadcast_in_dim.25
  28.9 0.3 broadcast_in_dim.23
  29.3 0.5 copy-done.2
  29.9 1.1 fusion.4
  31.2 6.5 %collective-permute-start.1 = (f32[4,4096]{1,0:T(4,128)S(1)}, f32[4,4096]{1,0:T(4,128)S(1)}, u32[]{:S(2)}, u32[]{:S(2)}) collective-permute-start(f32[4,4096]{1,0:T(4,128)S(1)} %get-tuple-element.38), channel_id=1, source_target_pairs={{1,0},{2,1},{3,2},{4,3},{5,4},{6,5},{7,6},{8,7},{9,8},{10,9},{11,1... | collective-permute-start | bytes 196616 | tf_op jit(solution)/shard_map/ppermute | solution.py:20
  37.7 2.2 %collective-permute-start = (f32[4,4096]{1,0:T(4,128)S(1)}, f32[4,4096]{1,0:T(4,128)S(1)}, u32[]{:S(2)}, u32[]{:S(2)}) collective-permute-start(f32[4,4096]{1,0:T(4,128)S(1)} %get-tuple-element.37), channel_id=1, source_target_pairs={{0,1},{1,2},{2,3},{3,4},{4,5},{5,6},{6,7},{7,8},{8,9},{9,10},{10,1... | collective-permute-start | bytes 196616 | tf_op jit(solution)/shard_map/ppermute | solution.py:20
  40.0 2.1 %collective-permute-start.3 = (f32[2,2,4,4096]{3,2,1,0:T(4,128)S(1)}, f32[2,2,4,4096]{3,2,1,0:T(4,128)S(1)}, u32[]{:S(2)}, u32[]{:S(2)}) collective-permute-start(f32[2,2,4,4096]{3,2,1,0:T(4,128)S(1)} %get-tuple-element.33), channel_id=1, source_target_pairs={{1,0},{2,1},{3,2},{4,3},{5,4},{6,5},{7,6},{8,7},{9,8},{10,9},{11,1... | collective-permute-start | bytes 786440 | tf_op jit(solution)/shard_map/ppermute | solution.py:20
  42.1 5.5 %collective-permute-start.2 = (f32[2,2,4,4096]{3,2,1,0:T(4,128)S(1)}, f32[2,2,4,4096]{3,2,1,0:T(4,128)S(1)}, u32[]{:S(2)}, u32[]{:S(2)}) collective-permute-start(f32[2,2,4,4096]{3,2,1,0:T(4,128)S(1)} %get-tuple-element.32), channel_id=1, source_target_pairs={{0,1},{1,2},{2,3},{3,4},{4,5},{5,6},{6,7},{7,8},{8,9},{9,10},{10,1... | collective-permute-start | bytes 786440 | tf_op jit(solution)/shard_map/ppermute | solution.py:20
  47.7 0.6 copy-done.5
  48.7 1.1 collective-permute-done.3
  49.8 1.2 collective-permute-done.2
  51.0 0.3 add_multiply_fusion.6
  51.4 0.3 slice.290
  51.7 0.6 add_multiply_fusion.5
  52.3 0.9 add_multiply_fusion.4
  53.3 0.3 slice.294
  53.6 0.4 add_multiply_fusion.3
  54.1 1.0 add_multiply_fusion.2
  55.1 0.3 slice.298
  55.5 0.4 add_multiply_fusion.1
  55.9 1.1 add_multiply_fusion
  57.0 0.8 fusion.23
  58.0 0.4 multiply_reduce_fusion.5
  58.5 0.5 add.288
  59.0 0.2 reduce_sum.259
  59.3 0.5 add.283
  59.9 0.2 reduce_sum.253
  60.1 1.0 copy.8
  61.2 66.6 %reduce-scatter.4.cloned.1.call-done = f32[128,2]{1,0:T(8,128)} async-done(((f32[1024,2]{1,0:T(8,128)}), f32[128,2]{1,0:T(8,128)}) %reduce-scatter.4.cloned.1.call-update) | async-done | bytes 1040
  127.8 1.5 %copy.9 = f32[2,128]{1,0:T(2,128)} copy(f32[2,128]{0,1:T(8,128)} %bitcast.45) | data formatting | bytes 2048
  (38 shorter events, 2.0 us)
Async XLA Ops:
  7.2 0.7 copy-start.4
  7.2 120.6 %reduce-scatter.4.cloned.1.call-start = ((), (), s32[]{:S(2)}) async-start(), calls=%async_computation.1 | async-start | bytes 589824
  28.7 1.0 copy-start.2
  28.9 1.0 copy-start.3
  31.0 8.9 %copy-start.1 = (f32[2,8,4096]{2,1,0:T(8,128)S(1)}, f32[2,8,4096]{2,1,0:T(8,128)}, u32[]{:S(2)}) copy-start(f32[2,8,4096]{2,1,0:T(8,128)} %param.10) | copy-start | bytes 786436
  31.1 8.7 %copy-start = (f32[2,8,4096]{2,1,0:T(8,128)S(1)}, f32[2,8,4096]{2,1,0:T(8,128)}, u32[]{:S(2)}) copy-start(f32[2,8,4096]{2,1,0:T(8,128)} %param.9) | copy-start | bytes 786436
  31.2 17.4 %collective-permute-start.1 = (f32[4,4096]{1,0:T(4,128)S(1)}, f32[4,4096]{1,0:T(4,128)S(1)}, u32[]{:S(2)}, u32[]{:S(2)}) collective-permute-start(f32[4,4096]{1,0:T(4,128)S(1)} %get-tuple-element.38), channel_id=1, source_target_pairs={{1,0},{2,1},{3,2},{4,3},{5,4},{6,5},{7,6},{8,7},{9,8},{10,9},{11,1... | collective-permute-start | bytes 196616 | tf_op jit(solution)/shard_map/ppermute | solution.py:20
  37.7 10.9 %collective-permute-start = (f32[4,4096]{1,0:T(4,128)S(1)}, f32[4,4096]{1,0:T(4,128)S(1)}, u32[]{:S(2)}, u32[]{:S(2)}) collective-permute-start(f32[4,4096]{1,0:T(4,128)S(1)} %get-tuple-element.37), channel_id=1, source_target_pairs={{0,1},{1,2},{2,3},{3,4},{4,5},{5,6},{6,7},{7,8},{8,9},{9,10},{10,1... | collective-permute-start | bytes 196616 | tf_op jit(solution)/shard_map/ppermute | solution.py:20
  40.0 9.8 %collective-permute-start.3 = (f32[2,2,4,4096]{3,2,1,0:T(4,128)S(1)}, f32[2,2,4,4096]{3,2,1,0:T(4,128)S(1)}, u32[]{:S(2)}, u32[]{:S(2)}) collective-permute-start(f32[2,2,4,4096]{3,2,1,0:T(4,128)S(1)} %get-tuple-element.33), channel_id=1, source_target_pairs={{1,0},{2,1},{3,2},{4,3},{5,4},{6,5},{7,6},{8,7},{9,8},{10,9},{11,1... | collective-permute-start | bytes 786440 | tf_op jit(solution)/shard_map/ppermute | solution.py:20
  42.1 8.9 %collective-permute-start.2 = (f32[2,2,4,4096]{3,2,1,0:T(4,128)S(1)}, f32[2,2,4,4096]{3,2,1,0:T(4,128)S(1)}, u32[]{:S(2)}, u32[]{:S(2)}) collective-permute-start(f32[2,2,4,4096]{3,2,1,0:T(4,128)S(1)} %get-tuple-element.32), channel_id=1, source_target_pairs={{0,1},{1,2},{2,3},{3,4},{4,5},{5,6},{6,7},{7,8},{8,9},{9,10},{10,1... | collective-permute-start | bytes 786440 | tf_op jit(solution)/shard_map/ppermute | solution.py:20
  47.7 0.7 copy-start.5
Sparse Core Ops, SparseCore 0:
  61.3 66.4 reduce-scatter.3
where the time goes:
time: 139 us; the launch traced here: 136 us
  waiting for transfers between devices  68.9 us (50%)
  blocking collectives  20.4 us (15%)
  starting transfers between devices  16.4 us (12%)
  between operations  14.3 us (10%)
  other arithmetic  8.32 us (6%)
  local copies, waits for them, and re-layouts  7.76 us (6%)
    unnamed x2, waiting for transfers between devices  66.6 us
    all_gather x1, blocking collectives, shards(): strip = lax.all_gather(density, 'wl', axis=1, tiled=True)  20.4 us
    ppermute x4, starting transfers between devices, from_behind(): lax.ppermute(value, axis, [(source, source + steps) for source in range(f...  16.3 us
    unnamed x14, local copies, waits for them, and re-layouts  4.38 us
    mul x4, other arithmetic, march(): (field_e + inverse * (field_hy - hy_down - (field_hx - hx_left) - current...  3.26 us
  transfers between devices with their start and end apart: 5, of which 3 were waited for; matrix products, arithmetic and copies ran while one was open for 0% of the time, Pallas kernels for 0%

commit v1 on v0

--- a/solution.py
+++ b/solution.py
@@ -24,6 +24,20 @@
     above = from_behind(value[..., -HALO:, :], axis, 1)
     below = from_behind(value[..., :HALO, :], axis, -1)
     return jnp.concatenate([above, value, below], axis=-2)
+
+
+def gather_columns(value, axis):
+    count = lax.axis_size(axis)
+    copies = jnp.broadcast_to(value[None], (count,) + value.shape)
+    pieces = lax.all_to_all(copies, axis, 0, 0, tiled=True)
+    return pieces.transpose(1, 0, 2).reshape(value.shape[0], count * value.shape[1])
+
+
+def scatter_sum_columns(value, axis):
+    count = lax.axis_size(axis)
+    rows, cols = value.shape
+    pieces = value.reshape(rows, count, cols // count).transpose(1, 0, 2)
+    return lax.all_to_all(pieces, axis, 0, 0, tiled=True).sum(axis=0)
 
 
 def lane_shift(vector, shift):
@@ -63,7 +77,7 @@
 def shards(density, foot_index, foot_weight, source_fwd, source_adj, omega):
     sources = jnp.stack([source_fwd, source_adj])
     sources_ext = with_halo(sources, "tile")
-    strip = lax.all_gather(density, "wl", axis=1, tiled=True)
+    strip = gather_columns(density, "wl")
     block_rows, block_cols = strip.shape
     cells_x, cells_y = foot_index.shape[1:]
     factor = cells_y // block_cols
@@ -99,7 +113,7 @@
             acc = acc + lane_shift(per_col, factor * shift)
         pooled_rows.append(acc.reshape(block_cols, factor).sum(axis=1))
     partial_grad = jnp.stack(pooled_rows)
-    density_grad = lax.psum_scatter(partial_grad, "wl", scatter_dimension=1, tiled=True)
+    density_grad = scatter_sum_columns(partial_grad, "wl")
     return (history[ITERS - 1][0], density_grad)
 
 

time: 139 us -> 57.1 us (0.41)
  the two profiles are of different devices: /device:TPU:25 before, /device:TPU:32 now
where the time goes in v1:
time: 57.1 us; the launch traced here: 56.8 us
  starting transfers between devices  20.8 us (36%)
  blocking collectives  13.8 us (24%)
  other arithmetic  10.2 us (18%)
  waiting for transfers between devices  5.69 us (10%)
  local copies, waits for them, and re-layouts  5.32 us (9%)
  between operations  0.96 us (2%)
    ppermute x4, starting transfers between devices, from_behind(): lax.ppermute(value, axis, [(source, source + steps) for source in range(f...  14.1 us
    all_to_all x1, blocking collectives, scatter_sum_columns(): return lax.all_to_all(pieces, axis, 0, 0, tiled=True).sum(axis=0)  13.8 us
    all_to_all x1, starting transfers between devices, gather_columns(): pieces = lax.all_to_all(copies, axis, 0, 0, tiled=True)  6.71 us
    ppermute x4, waiting for transfers between devices, from_behind(): lax.ppermute(value, axis, [(source, source + steps) for source in range(f...  5.69 us
    mul x4, other arithmetic, march(): (field_e + inverse * (field_hy - hy_down - (field_hx - hx_left) - current...  3.29 us
    mul x4, other arithmetic, march(): field_hy = (field_hy + time_step * (e_up - field_e)) * valid  1.5 us
    another operation x1, other arithmetic, shards(): sources = jnp.stack([source_fwd, source_adj])  1.35 us
    broadcast_in_dim x1, local copies, waits for them, and re-layouts, gather_columns(): copies = jnp.broadcast_to(value[None], (count,) + value.shape)  1.28 us
  transfers between devices with their start and end apart: 5, of which 1 were waited for; matrix products, arithmetic and copies ran while one was open for 7% of the time, Pallas kernels for 0%

profile of v1, /device:TPU:32, one launch (start us, length us, event | category | flops | bytes accessed | tf_op | source)
XLA Modules:
  0.0 56.8 jit_solution(1772204601077161621)
XLA Ops:
  0.6 1.3 %broadcast_in_dim.24 = f32[8,2,128]{2,1,0:T(2,128)} broadcast(f32[2,128]{1,0:T(2,128)} %param.6), dimensions={1,2} | broadcast | bytes 9216 | tf_op jit(solution)/shard_map/broadcast_in_dim | solution.py:31
  1.9 6.7 %all-to-all-start = ((f32[8,2,128]{2,1,0:T(2,128)}), f32[8,2,128]{2,1,0:T(2,128)S(1)}, u32[]{:S(2)}, u32[]{:S(2)}) async-start(f32[8,2,128]{2,1,0:T(2,128)} %broadcast_in_dim.24), calls=%async_computation | async-start | bytes 16384 | tf_op jit(solution)/shard_map/all_to_all | solution.py:32
  8.6 1.4 %fusion.18 = (f32[2,2,4,4096]{3,2,1,0:T(4,128)S(1)}, f32[2,2,4,4096]{3,2,1,0:T(4,128)S(1)}) fusion(f32[1,2,8,4096]{3,2,1,0:T(8,128)} %bitcast.32, f32[1,2,8,4096]{3,2,1,0:T(8,128)} %bitcast.38), kind=kLoop, calls=%fused_computation.49 | loop fusion | flops 131072 | bytes 1048576 | tf_op jit(solution)/shard_map/stack | solution.py:78
  10.0 4.5 %collective-permute-start.3 = (f32[2,2,4,4096]{3,2,1,0:T(4,128)S(1)}, f32[2,2,4,4096]{3,2,1,0:T(4,128)S(1)}, u32[]{:S(2)}, u32[]{:S(2)}) collective-permute-start(f32[2,2,4,4096]{3,2,1,0:T(4,128)S(1)} %get-tuple-element.33), channel_id=1, source_target_pairs={{1,0},{2,1},{3,2},{4,3},{5,4},{6,5},{7,6},{8,7},{9,8},{10,9},{11,1... | collective-permute-start | bytes 786440 | tf_op jit(solution)/shard_map/ppermute | solution.py:20
  14.5 1.9 %collective-permute-start.2 = (f32[2,2,4,4096]{3,2,1,0:T(4,128)S(1)}, f32[2,2,4,4096]{3,2,1,0:T(4,128)S(1)}, u32[]{:S(2)}, u32[]{:S(2)}) collective-permute-start(f32[2,2,4,4096]{3,2,1,0:T(4,128)S(1)} %get-tuple-element.32), channel_id=1, source_target_pairs={{0,1},{1,2},{2,3},{3,4},{4,5},{5,6},{6,7},{7,8},{8,9},{9,10},{10,1... | collective-permute-start | bytes 786440 | tf_op jit(solution)/shard_map/ppermute | solution.py:20
  16.5 0.6 %copy-done.4 = f32[2]{0:T(128)S(1)} copy-done((f32[2]{0:T(128)S(1)}, f32[2]{0:T(128)}, u32[]{:S(2)}) %copy-start.4) | copy-done | bytes 32
  17.3 1.1 %fusion.4 = (f32[8,4096]{1,0:T(8,128)S(1)}, f32[8,4096]{1,0:T(8,128)S(1)}, f32[8,4096]{1,0:T(8,128)S(1)}, f32[8,4096]{1,0:T(8,128)S(1)}, f32[8,4096]{1,0:T(8,128...) fusion(bf16[4,8,4096]{2,1,0:T(8,128)(2,1)S(1)} %copy-done.3, ...), kind=kLoop, calls=%fused_computation.32 | loop fusion | flops 6750208 | bytes 2113536 | tf_op jit(solution)/shard_map/reduce_sum | solution.py:93
  18.4 0.2 broadcast_in_dim.27
  18.6 0.3 broadcast_in_dim.28
  18.9 0.2 broadcast_in_dim.25
  19.1 0.3 broadcast_in_dim.26
  19.6 5.8 %collective-permute-start.1 = (f32[4,4096]{1,0:T(4,128)S(1)}, f32[4,4096]{1,0:T(4,128)S(1)}, u32[]{:S(2)}, u32[]{:S(2)}) collective-permute-start(f32[4,4096]{1,0:T(4,128)S(1)} %get-tuple-element.38), channel_id=1, source_target_pairs={{1,0},{2,1},{3,2},{4,3},{5,4},{6,5},{7,6},{8,7},{9,8},{10,9},{11,1... | collective-permute-start | bytes 196616 | tf_op jit(solution)/shard_map/ppermute | solution.py:20
  25.4 1.9 %collective-permute-start = (f32[4,4096]{1,0:T(4,128)S(1)}, f32[4,4096]{1,0:T(4,128)S(1)}, u32[]{:S(2)}, u32[]{:S(2)}) collective-permute-start(f32[4,4096]{1,0:T(4,128)S(1)} %get-tuple-element.37), channel_id=1, source_target_pairs={{0,1},{1,2},{2,3},{3,4},{4,5},{5,6},{6,7},{7,8},{8,9},{9,10},{10,1... | collective-permute-start | bytes 196616 | tf_op jit(solution)/shard_map/ppermute | solution.py:20
  27.4 5.7 %collective-permute-done = f32[4,4096]{1,0:T(4,128)S(1)} collective-permute-done((f32[4,4096]{1,0:T(4,128)S(1)}, f32[4,4096]{1,0:T(4,128)S(1)}, u32[]{:S(2)}, u32[]{:S(2)}) %collective-permute-start) | collective-permute-done | bytes 65568 | tf_op jit(solution)/shard_map/ppermute | solution.py:20
  33.2 0.3 add_multiply_fusion.6
  33.7 0.3 slice.292
  34.0 0.6 %add_multiply_fusion.5 = (f32[2,2,16,4096]{3,2,1,0:T(8,128)S(1)}, f32[2,2,16,4096]{3,2,1,0:T(8,128)S(1)}) fusion(f32[2,2,15,4096]{3,2,1,0:T(8,128)S(1)} %slice.290, f32[16]{0:T(128)S(1)} %select_multiply_fusion, f32[16]{0:T(128)S(1)} %fusion.35, f32[2,2,4,4096]{3,2,1,0:T(4,128)S(1)} %collective-permute-done.3, f32[1,2,8,4096]{3,2,1,0:T(8,128)S(1)} %bitcast.40, ...), kind=kLoop, calls=%fused_computation.21 | loop fusion | flops 4194304 | bytes 5734344 | tf_op jit(solution)/shard_map/mul | solution.py:64
  34.6 0.9 %add_multiply_fusion.4 = f32[2,2,16,4096]{3,2,1,0:T(8,128)S(1)} fusion(f32[2,2,16,4096]{3,2,1,0:T(8,128)S(1)} %get-tuple-element.27, f32[2,2,16,4095]{3,2,1,0:T(8,128)S(1)} %bitcast.29, f32[2,2,16,4096]{3,2,1,0:T(8,128)S(1)} %get-tuple-element.26, f32[2,2,15,4096]{3,2,1,0:T(8,128)S(1)} %bitcast.28, f32[2]{0:T(128)S(1)} %get-tuple-element.50, ...), kind=kLoop, calls=%fused_computation.18 | loop fusion | flops 5242880 | bytes 7028624 | tf_op jit(solution)/shard_map/mul | solution.py:68
  35.6 0.3 slice.296
  35.9 0.4 add_multiply_fusion.3
  36.4 1.0 %add_multiply_fusion.2 = f32[2,2,16,4096]{3,2,1,0:T(8,128)S(1)} fusion(f32[2,2,16,4096]{3,2,1,0:T(8,128)S(1)} %add_multiply_fusion.4, f32[2,2,16,4096]{3,2,1,0:T(8,128)S(1)} %get-tuple-element.31, f32[2,2,16,4095]{3,2,1,0:T(8,128)S(1)} %bitcast.27, f32[2,2,16,4096]{3,2,1,0:T(8,128)S(1)} %get-tuple-element.30, f32[2,2,15,4096]{3,2,1,0:T(8,128)S(1)} %bitcast.26, ...), kind=kLoop, calls=%fused_computation.14 | loop fusion | flops 6029312 | bytes 8077200 | tf_op jit(solution)/shard_map/mul | solution.py:68
  37.5 0.3 slice.300
  37.8 0.4 add_multiply_fusion.1
  38.2 1.1 %add_multiply_fusion = f32[2,2,16,4096]{3,2,1,0:T(8,128)S(1)} fusion(f32[2,2,16,4096]{3,2,1,0:T(8,128)S(1)} %add_multiply_fusion.2, f32[2,2,16,4096]{3,2,1,0:T(8,128)S(1)} %get-tuple-element.29, f32[2,2,16,4095]{3,2,1,0:T(8,128)S(1)} %bitcast.31, f32[2,2,16,4096]{3,2,1,0:T(8,128)S(1)} %get-tuple-element.28, f32[2,2,15,4096]{3,2,1,0:T(8,128)S(1)} %bitcast.30, ...), kind=kLoop, calls=%fused_computation.11 | loop fusion | flops 6815744 | bytes 9125776 | tf_op jit(solution)/shard_map/mul | solution.py:68
  39.3 0.8 %fusion.23 = (f32[8,4096]{1,0:T(8,128)S(1)}, f32[2,8,4096]{2,1,0:T(8,128)}) fusion(f32[2,2,16,4096]{3,2,1,0:T(8,128)S(1)} %add_multiply_fusion.6, f32[2,2,16,4096]{3,2,1,0:T(8,128)S(1)} %add_multiply_fusion), kind=kLoop, calls=%fused_computation.58 | loop fusion | flops 98304 | bytes 917504 | tf_op jit(solution)/shard_map/reduce_sum | solution.py:105
  40.3 0.4 multiply_reduce_fusion.5
  40.8 0.5 add.286
  41.4 0.2 reduce_sum.268
  41.7 0.5 add.281
  42.2 0.2 reduce_sum.262
  42.4 13.8 %all_to_all.10 = f32[8,2,128]{2,1,0:T(2,128)S(1)} all-to-all(f32[8,2,128]{2,1,0:T(2,128)S(1)} %maximum_bitcast_fusion), channel_id=1, replica_groups=mesh['wl'=8,'tile'=16] {'wl'}, dimensions={0} | all-to-all | bytes 16384 | tf_op jit(solution)/shard_map/all_to_all | solution.py:40
  56.2 0.6 %reduce_sum.269 = f32[2,128]{1,0:T(2,128)} reduce(f32[8,2,128]{2,1,0:T(2,128)S(1)} %all_to_all.10, f32[]{:T(128)} %constant.82.clone.1), dimensions={0}, to_apply=%region_26.27 | reduce | flops 1792 | bytes 9220 | tf_op jit(solution)/shard_map/reduce_sum | solution.py:40
  (35 shorter events, 1.3 us)
Async XLA Ops:
  1.9 16.5 %all-to-all-start = ((f32[8,2,128]{2,1,0:T(2,128)}), f32[8,2,128]{2,1,0:T(2,128)S(1)}, u32[]{:S(2)}, u32[]{:S(2)}) async-start(f32[8,2,128]{2,1,0:T(2,128)} %broadcast_in_dim.24), calls=%async_computation | async-start | bytes 16384 | tf_op jit(solution)/shard_map/all_to_all | solution.py:32
  8.6 8.7 %copy-start.2 = (s32[4,8,4096]{2,1,0:T(8,128)S(1)}, s32[4,8,4096]{2,1,0:T(8,128)}, u32[]{:S(2)}) copy-start(s32[4,8,4096]{2,1,0:T(8,128)} %param.7) | copy-start | bytes 1572868
  8.6 8.7 %copy-start.3 = (bf16[4,8,4096]{2,1,0:T(8,128)(2,1)S(1)}, bf16[4,8,4096]{2,1,0:T(8,128)(2,1)}, u32[]{:S(2)}) copy-start(bf16[4,8,4096]{2,1,0:T(8,128)(2,1)} %param.8) | copy-start | bytes 786436
  10.0 23.2 %collective-permute-start.3 = (f32[2,2,4,4096]{3,2,1,0:T(4,128)S(1)}, f32[2,2,4,4096]{3,2,1,0:T(4,128)S(1)}, u32[]{:S(2)}, u32[]{:S(2)}) collective-permute-start(f32[2,2,4,4096]{3,2,1,0:T(4,128)S(1)} %get-tuple-element.33), channel_id=1, source_target_pairs={{1,0},{2,1},{3,2},{4,3},{5,4},{6,5},{7,6},{8,7},{9,8},{10,9},{11,1... | collective-permute-start | bytes 786440 | tf_op jit(solution)/shard_map/ppermute | solution.py:20
  14.5 18.7 %collective-permute-start.2 = (f32[2,2,4,4096]{3,2,1,0:T(4,128)S(1)}, f32[2,2,4,4096]{3,2,1,0:T(4,128)S(1)}, u32[]{:S(2)}, u32[]{:S(2)}) collective-permute-start(f32[2,2,4,4096]{3,2,1,0:T(4,128)S(1)} %get-tuple-element.32), channel_id=1, source_target_pairs={{0,1},{1,2},{2,3},{3,4},{4,5},{5,6},{6,7},{7,8},{8,9},{9,10},{10,1... | collective-permute-start | bytes 786440 | tf_op jit(solution)/shard_map/ppermute | solution.py:20
  16.5 0.7 %copy-start.4 = (f32[2]{0:T(128)S(1)}, f32[2]{0:T(128)}, u32[]{:S(2)}) copy-start(f32[2]{0:T(128)} %param.11) | copy-start | bytes 28
  19.6 7.8 %collective-permute-start.1 = (f32[4,4096]{1,0:T(4,128)S(1)}, f32[4,4096]{1,0:T(4,128)S(1)}, u32[]{:S(2)}, u32[]{:S(2)}) collective-permute-start(f32[4,4096]{1,0:T(4,128)S(1)} %get-tuple-element.38), channel_id=1, source_target_pairs={{1,0},{2,1},{3,2},{4,3},{5,4},{6,5},{7,6},{8,7},{9,8},{10,9},{11,1... | collective-permute-start | bytes 196616 | tf_op jit(solution)/shard_map/ppermute | solution.py:20
  25.4 7.7 %collective-permute-start = (f32[4,4096]{1,0:T(4,128)S(1)}, f32[4,4096]{1,0:T(4,128)S(1)}, u32[]{:S(2)}, u32[]{:S(2)}) collective-permute-start(f32[4,4096]{1,0:T(4,128)S(1)} %get-tuple-element.37), channel_id=1, source_target_pairs={{0,1},{1,2},{2,3},{3,4},{4,5},{5,6},{6,7},{7,8},{8,9},{9,10},{10,1... | collective-permute-start | bytes 196616 | tf_op jit(solution)/shard_map/ppermute | solution.py:20
  27.4 5.8 %copy-start = (f32[2,8,4096]{2,1,0:T(8,128)S(1)}, f32[2,8,4096]{2,1,0:T(8,128)}, u32[]{:S(2)}) copy-start(f32[2,8,4096]{2,1,0:T(8,128)} %param.9) | copy-start | bytes 786436
  27.4 5.8 %copy-start.1 = (f32[2,8,4096]{2,1,0:T(8,128)S(1)}, f32[2,8,4096]{2,1,0:T(8,128)}, u32[]{:S(2)}) copy-start(f32[2,8,4096]{2,1,0:T(8,128)} %param.10) | copy-start | bytes 786436

commit v2 on v1

--- a/solution.py
+++ b/solution.py
@@ -48,12 +48,11 @@
     return lax.slice_in_dim(padded, start, start + width, axis=vector.ndim - 1)
 
 
-def march(source, drive, density_cell, inverse, valid):
+def march(source, drive, density_cell, inverse, hy_step):
     field_e = jnp.zeros_like(source)
     field_hx = jnp.zeros_like(source)
     field_hy = jnp.zeros_like(source)
     current = jnp.zeros_like(source)
-    rows = source.shape[2]
     history = []
     for turn in range(ITERS):
         row_zero = jnp.zeros_like(source[:, :, :1, :])
@@ -61,7 +60,7 @@
         e_up = jnp.concatenate([field_e[:, :, 1:, :], row_zero], 2)
         e_right = jnp.concatenate([field_e[:, :, :, 1:], col_zero], 3)
         field_hx = field_hx - time_step * (e_right - field_e)
-        field_hy = (field_hy + time_step * (e_up - field_e)) * valid
+        field_hy = field_hy + hy_step * (e_up - field_e)
         current = drude_decay * current + drude_gain * density_cell * field_e
         hy_down = jnp.concatenate([row_zero, field_hy[:, :, :-1, :]], 2)
         hx_left = jnp.concatenate([col_zero, field_hx[:, :, :, :-1]], 3)
@@ -69,8 +68,8 @@
             field_e
             + inverse * (field_hy - hy_down - (field_hx - hx_left) - current)
             + drive[turn] * source
-        ) * valid
-        history.append(field_e[:, :, HALO : rows - HALO, :])
+        )
+        history.append(field_e)
     return history
 
 
@@ -84,37 +83,39 @@
     weights = foot_weight.astype(jnp.float32)
     col_block = lax.broadcasted_iota(jnp.int32, (1, cells_y), 1) // factor
     key = (foot_index // block_cols) * len(SHIFTS) + (foot_index % block_cols - col_block[None]) + 2
+    codes = lax.broadcasted_iota(jnp.int32, (block_rows * len(SHIFTS), 1, 1), 0)
+    matched = jnp.zeros((block_rows * len(SHIFTS), cells_x, cells_y), jnp.float32)
+    for entry in range(foot_index.shape[0]):
+        matched = matched + jnp.where(key[entry][None] == codes, weights[entry][None], 0.0)
     upsampled = jnp.repeat(strip, factor, axis=1)
-    matched = []
-    density_cell = jnp.zeros((cells_x, cells_y), jnp.float32)
-    for row in range(block_rows):
-        for slot, shift in enumerate(SHIFTS):
-            code = row * len(SHIFTS) + slot
-            weight_sum = jnp.sum(jnp.where(key == code, weights, 0.0), axis=0)
-            matched.append(weight_sum)
-            density_cell = density_cell + weight_sum * lane_shift(upsampled[row], -factor * shift)[None]
-    density_ext = with_halo(density_cell, "tile")
-    inverse_ext = time_step / (1.0 + high_contrast * density_ext)
+    candidates = jnp.stack(
+        [lane_shift(upsampled[row], -factor * shift) for row in range(block_rows) for shift in SHIFTS]
+    )
+    density_cell = jnp.sum(matched * candidates[:, None, :], axis=0)
+    reach = 2
+    above = from_behind(density_cell[-reach:], "tile", 1)
+    below = from_behind(density_cell[:reach], "tile", -1)
+    pad = jnp.zeros((HALO - reach, cells_y), jnp.float32)
+    density_ext = jnp.concatenate([pad, above, density_cell, below, pad], axis=0)
     rows_ext = cells_x + 2 * HALO
     global_row = lax.axis_index("tile") * cells_x - HALO + lax.broadcasted_iota(jnp.int32, (rows_ext, 1), 0)
-    valid = ((global_row >= 0) & (global_row < cells_x * lax.axis_size("tile"))).astype(jnp.float32)
+    valid = (global_row >= 0) & (global_row < cells_x * lax.axis_size("tile"))
+    inverse_ext = jnp.where(valid, time_step / (1.0 + high_contrast * density_ext), 0.0)
+    hy_step = jnp.where(valid, time_step, 0.0)
     drive = [jnp.sin(omega * (turn + 1.0))[None, :, None, None] for turn in range(ITERS)]
-    history = march(sources_ext, drive, density_ext, inverse_ext, valid)
-    sense = jnp.zeros((cells_x, cells_y), jnp.float32)
+    history = march(sources_ext, drive, density_ext, inverse_ext, hy_step)
+    sense = jnp.zeros((rows_ext, cells_y), jnp.float32)
     for turn in range(ITERS):
         sense = sense + jnp.sum(history[turn][1] * history[ITERS - 1 - turn][0], axis=0)
     total_waves = source_fwd.shape[0] * lax.axis_size("wl")
-    scaled = high_contrast / total_waves * sense
-    pooled_rows = []
-    for row in range(block_rows):
-        acc = jnp.zeros((cells_y,), jnp.float32)
-        for slot, shift in enumerate(SHIFTS):
-            per_col = jnp.sum(matched[row * len(SHIFTS) + slot] * scaled, axis=0)
-            acc = acc + lane_shift(per_col, factor * shift)
-        pooled_rows.append(acc.reshape(block_cols, factor).sum(axis=1))
-    partial_grad = jnp.stack(pooled_rows)
+    scaled = high_contrast / total_waves * sense[HALO : HALO + cells_x]
+    per_col = jnp.sum(matched * scaled[None], axis=1)
+    pooled = per_col.reshape(block_rows, len(SHIFTS), block_cols, factor).sum(axis=3)
+    partial_grad = jnp.zeros((block_rows, block_cols), jnp.float32)
+    for slot, shift in enumerate(SHIFTS):
+        partial_grad = partial_grad + lane_shift(pooled[:, slot], shift)
     density_grad = scatter_sum_columns(partial_grad, "wl")
-    return (history[ITERS - 1][0], density_grad)
+    return (history[ITERS - 1][0, :, HALO : HALO + cells_x], density_grad)
 
 
 def solution(mesh):

time: 57.1 us -> 66.3 us (1.16)
  blocking collectives: 13.8 us -> 0 us
  local copies, waits for them, and re-layouts: 5.32 us -> 12.5 us
  waiting for transfers between devices: 5.69 us -> 11.7 us
  starting transfers between devices: 20.8 us -> 26.2 us
  other arithmetic: 10.2 us -> 14.5 us
    all_to_all x1 -> x0, blocking collectives: 13.8 us -> none  [scatter_sum_columns(): return lax.all_to_all(pieces, axis, 0, 0, tiled=True).sum(axis=0)]
    all_to_all x0 -> x1, starting transfers between devices: none -> 7.21 us  [scatter_sum_columns(): return lax.all_to_all(pieces, axis, 0, 0, tiled=True).sum(axis=0)]
    all_to_all x0 -> x1, waiting for transfers between devices: none -> 6.95 us  [scatter_sum_columns(): return lax.all_to_all(pieces, axis, 0, 0, tiled=True).sum(axis=0)]
    reshape x0 -> x1, local copies, waits for them, and re-layouts: none -> 6.65 us  [shards(): per_col.reshape(block_rows, len(SHIFTS), block_cols, factor).sum(axis=3)]
    add x3 -> x8, other arithmetic: 0.3 us -> 5.26 us  [the longest x4 3.39 us: march(): field_e + inverse * (field_hy - hy_down - (field_hx - hx_left) - current)]
    mul x8 -> x2, other arithmetic: 4.79 us -> 0.07 us  [the longest x1 0.06 us: shards(): scaled = high_contrast / total_waves * sense[HALO:HALO + cells_x]]
    reduce_sum x4 -> x3, other arithmetic: 1.87 us -> 5.27 us  [the longest x1 3.9 us: shards(): per_col.reshape(block_rows, len(SHIFTS), block_cols, factor).sum(axis=3)]
    ppermute x4, starting transfers between devices: 14.1 us -> 12.3 us  [from_behind(): lax.ppermute(value, axis, [(source, source + steps) for source in range(f...]
  transfers between devices with their start and end apart: 5 -> 6, of which waited for: 1 -> 2; matrix products, arithmetic and copies ran while one was open for 7% -> 10% of each run, Pallas kernels for 0% -> 0%
where the time goes in v2:
time: 66.3 us; the launch traced here: 65.9 us
  starting transfers between devices  26.2 us (40%)
  other arithmetic  14.5 us (22%)
  local copies, waits for them, and re-layouts  12.5 us (19%)
  waiting for transfers between devices  11.7 us (18%)
  between operations  1.02 us (2%)
    ppermute x4, starting transfers between devices, from_behind(): lax.ppermute(value, axis, [(source, source + steps) for source in range(f...  12.3 us
    all_to_all x1, starting transfers between devices, scatter_sum_columns(): return lax.all_to_all(pieces, axis, 0, 0, tiled=True).sum(axis=0)  7.21 us
    all_to_all x1, waiting for transfers between devices, scatter_sum_columns(): return lax.all_to_all(pieces, axis, 0, 0, tiled=True).sum(axis=0)  6.95 us
    all_to_all x1, starting transfers between devices, gather_columns(): pieces = lax.all_to_all(copies, axis, 0, 0, tiled=True)  6.71 us
    reshape x1, local copies, waits for them, and re-layouts, shards(): per_col.reshape(block_rows, len(SHIFTS), block_cols, factor).sum(axis=3)  6.65 us
    ppermute x4, waiting for transfers between devices, from_behind(): lax.ppermute(value, axis, [(source, source + steps) for source in range(f...  4.73 us
    reduce_sum x1, other arithmetic, shards(): per_col.reshape(block_rows, len(SHIFTS), block_cols, factor).sum(axis=3)  3.9 us
    add x4, other arithmetic, march(): field_e + inverse * (field_hy - hy_down - (field_hx - hx_left) - current)  3.39 us
  transfers between devices with their start and end apart: 6, of which 2 were waited for; matrix products, arithmetic and copies ran while one was open for 10% of the time, Pallas kernels for 0%

profile of v2, /device:TPU:32, one launch (start us, length us, event | category | flops | bytes accessed | tf_op | source)
XLA Modules:
  0.0 65.9 jit_solution(15478586800851084667)
XLA Ops:
  0.6 1.3 %broadcast_in_dim.110 = f32[8,2,128]{2,1,0:T(2,128)} broadcast(f32[2,128]{1,0:T(2,128)} %param.6), dimensions={1,2} | broadcast | bytes 9216 | tf_op jit(solution)/shard_map/broadcast_in_dim | solution.py:31
  2.0 6.7 %all-to-all-start = ((f32[8,2,128]{2,1,0:T(2,128)}), f32[8,2,128]{2,1,0:T(2,128)S(1)}, u32[]{:S(2)}, u32[]{:S(2)}) async-start(f32[8,2,128]{2,1,0:T(2,128)} %broadcast_in_dim.110), calls=%async_computation | async-start | bytes 16384 | tf_op jit(solution)/shard_map/all_to_all | solution.py:32
  8.7 1.3 %fusion.12 = (f32[2,2,4,4096]{3,2,1,0:T(4,128)S(1)}, f32[2,2,4,4096]{3,2,1,0:T(4,128)S(1)}) fusion(f32[1,2,8,4096]{3,2,1,0:T(8,128)} %bitcast.65, f32[1,2,8,4096]{3,2,1,0:T(8,128)} %bitcast.71), kind=kLoop, calls=%fused_computation.44 | loop fusion | flops 131072 | bytes 1048576 | tf_op jit(solution)/shard_map/stack | solution.py:77
  10.0 2.1 %collective-permute-start.2 = (f32[2,2,4,4096]{3,2,1,0:T(4,128)S(1)}, f32[2,2,4,4096]{3,2,1,0:T(4,128)S(1)}, u32[]{:S(2)}, u32[]{:S(2)}) collective-permute-start(f32[2,2,4,4096]{3,2,1,0:T(4,128)S(1)} %get-tuple-element.12), channel_id=1, source_target_pairs={{0,1},{1,2},{2,3},{3,4},{4,5},{5,6},{6,7},{7,8},{8,9},{9,10},{10,1... | collective-permute-start | bytes 786440 | tf_op jit(solution)/shard_map/ppermute | solution.py:20
  12.1 5.8 %collective-permute-start.3 = (f32[2,2,4,4096]{3,2,1,0:T(4,128)S(1)}, f32[2,2,4,4096]{3,2,1,0:T(4,128)S(1)}, u32[]{:S(2)}, u32[]{:S(2)}) collective-permute-start(f32[2,2,4,4096]{3,2,1,0:T(4,128)S(1)} %get-tuple-element.13), channel_id=1, source_target_pairs={{1,0},{2,1},{3,2},{4,3},{5,4},{6,5},{7,6},{8,7},{9,8},{10,9},{11,1... | collective-permute-start | bytes 786440 | tf_op jit(solution)/shard_map/ppermute | solution.py:20
  17.9 0.7 %multiply_sine_fusion = (f32[2]{0:T(128)S(1)}, f32[2]{0:T(128)S(1)}, f32[2]{0:T(128)S(1)}, f32[2]{0:T(128)S(1)}) fusion(f32[2]{0:T(128)} %param.11), kind=kLoop, calls=%fused_computation.94 | loop fusion | flops 6 | bytes 40 | tf_op jit(solution)/shard_map/sin | solution.py:105
  18.7 0.5 fusion.2
  19.7 0.3 broadcast_in_dim.113
  20.5 0.3 broadcast_in_dim.116
  21.6 0.6 multiply_reduce_fusion.1
  22.1 1.9 %collective-permute-start.1 = (f32[2,4096]{1,0:T(2,128)S(1)}, f32[2,4096]{1,0:T(2,128)S(1)}, u32[]{:S(2)}, u32[]{:S(2)}) collective-permute-start(f32[2,4096]{1,0:T(2,128)S(1)} %get-tuple-element.25), channel_id=1, source_target_pairs={{1,0},{2,1},{3,2},{4,3},{5,4},{6,5},{7,6},{8,7},{9,8},{10,9},{11,1... | collective-permute-start | bytes 98312 | tf_op jit(solution)/shard_map/ppermute | solution.py:20
  24.1 2.6 %collective-permute-start = (f32[2,4096]{1,0:T(2,128)S(1)}, f32[2,4096]{1,0:T(2,128)S(1)}, u32[]{:S(2)}, u32[]{:S(2)}) collective-permute-start(f32[2,4096]{1,0:T(2,128)S(1)} %get-tuple-element.26), channel_id=1, source_target_pairs={{0,1},{1,2},{2,3},{3,4},{4,5},{5,6},{6,7},{7,8},{8,9},{9,10},{10,1... | collective-permute-start | bytes 98312 | tf_op jit(solution)/shard_map/ppermute | solution.py:20
  26.7 4.7 %collective-permute-done = f32[2,4096]{1,0:T(2,128)S(1)} collective-permute-done((f32[2,4096]{1,0:T(2,128)S(1)}, f32[2,4096]{1,0:T(2,128)S(1)}, u32[]{:S(2)}, u32[]{:S(2)}) %collective-permute-start) | collective-permute-done | bytes 32800 | tf_op jit(solution)/shard_map/ppermute | solution.py:20
  31.4 0.3 concatenate.66
  31.9 0.3 multiply_add_fusion.8
  32.2 0.3 slice.267
  32.6 0.5 multiply_add_fusion.7
  33.2 0.8 %multiply_add_fusion.5 = f32[2,2,16,4096]{3,2,1,0:T(8,128)S(1)} fusion(f32[2,2,16,4096]{3,2,1,0:T(8,128)S(1)} %get-tuple-element.7, f32[2,2,16,4095]{3,2,1,0:T(8,128)S(1)} %bitcast.64, f32[2,2,16,4096]{3,2,1,0:T(8,128)S(1)} %get-tuple-element.6, f32[2,2,15,4096]{3,2,1,0:T(8,128)S(1)} %bitcast.63, f32[2]{0:T(128)S(1)} %get-tuple-element.43, ...), kind=kLoop, calls=%fused_computation.15 | loop fusion | flops 4718592 | bytes 7028560 | tf_op jit(solution)/shard_map/add | solution.py:68
  34.0 0.3 slice.271
  34.4 0.4 multiply_add_fusion.4
  34.8 0.9 %multiply_add_fusion.2 = f32[2,2,16,4096]{3,2,1,0:T(8,128)S(1)} fusion(f32[2,2,16,4096]{3,2,1,0:T(8,128)S(1)} %multiply_add_fusion.5, f32[2,2,16,4096]{3,2,1,0:T(8,128)S(1)} %get-tuple-element.11, f32[2,2,16,4095]{3,2,1,0:T(8,128)S(1)} %bitcast.62, f32[2,2,16,4096]{3,2,1,0:T(8,128)S(1)} %get-tuple-element.10, f32[2,2,15,4096]{3,2,1,0:T(8,128)S(1)} %bitcast.61, ...), kind=kLoop, calls=%fused_computation.11 | loop fusion | flops 5505024 | bytes 8077136 | tf_op jit(solution)/shard_map/add | solution.py:68
  35.9 0.3 slice.275
  36.3 0.4 multiply_add_fusion.1
  36.7 1.4 %multiply_add_fusion = f32[2,2,16,4096]{3,2,1,0:T(8,128)S(1)} fusion(f32[2,2,16,4096]{3,2,1,0:T(8,128)S(1)} %multiply_add_fusion.2, f32[2,2,16,4095]{3,2,1,0:T(8,128)S(1)} %bitcast.78, f32[2,2,15,4096]{3,2,1,0:T(8,128)S(1)} %bitcast.77, f32[2,2,16,4096]{3,2,1,0:T(8,128)S(1)} %multiply_add_fusion.5, f32[2]{0:T(128)S(1)} %get-tuple-element.42, ...), kind=kLoop, calls=%fused_computation.8 | loop fusion | flops 7864320 | bytes 11157136 | tf_op jit(solution)/shard_map/add | solution.py:68
  38.3 0.8 %multiply_reduce_fusion = f32[10,4096]{1,0:T(8,128)S(1)} fusion(f32[8,4096]{1,0:T(8,128)S(1)} %fusion.13, f32[8,4096]{1,0:T(8,128)S(1)} %get-tuple-element.19, s32[8,4096]{1,0:T(8,128)S(1)} %get-tuple-element.15, f32[8,4096]{1,0:T(8,128)S(1)} %get-tuple-element.20, s32[8,4096]{1,0:T(8,128)S(1)} %get-tuple-element.16, f32[8,4096]{1,0:T(8,128)S(1)} %get-tuple-element.21, ...), kind=kLoop, calls=%fused_computation | loop fusion | flops 4218880 | bytes 1343488 | tf_op jit(solution)/shard_map/reduce_sum | solution.py:112
  39.1 6.7 %reshape.174 = f32[2,5,1024,4]{3,2,1,0:T(8,128)} reshape(f32[10,4096]{1,0:T(8,128)S(1)} %multiply_reduce_fusion) | data formatting | bytes 327680 | tf_op jit(solution)/shard_map/reshape | solution.py:113
  45.8 3.9 %reduce_sum.78 = f32[2,5,1024]{2,1,0:T(8,128)S(1)} reduce(f32[2,5,1024,4]{3,2,1,0:T(8,128)} %reshape.174, f32[]{:T(128)} %constant.71.clone.1), dimensions={3}, to_apply=%region_6.7 | reduce | flops 30720 | bytes 204804 | tf_op jit(solution)/shard_map/reduce_sum | solution.py:113
  49.8 0.7 %fusion.21 = f32[8,2,128]{2,1,0:T(2,128)} fusion(f32[2,1024]{1,0:T(2,128)S(1)} %bitcast.91, f32[2,1024]{1,0:T(2,128)S(1)} %bitcast.92, f32[2,1,1024]{2,1,0:T(1,128)S(1)} %get-tuple-element.28, f32[2,1024]{1,0:T(2,128)S(1)} %bitcast.90, f32[2,1024]{1,0:T(2,128)S(1)} %bitcast.89), kind=kLoop, calls=%fused_computation.92 | loop fusion | flops 8192 | bytes 49152 | tf_op jit(solution)/shard_map/transpose | solution.py:39
  50.5 7.2 %all-to-all-start.1 = ((f32[8,2,128]{2,1,0:T(2,128)}), f32[8,2,128]{2,1,0:T(2,128)S(1)}, u32[]{:S(2)}, u32[]{:S(2)}) async-start(f32[8,2,128]{2,1,0:T(2,128)} %fusion.21), calls=%async_computation.1 | async-start | bytes 16384 | tf_op jit(solution)/shard_map/all_to_all | solution.py:40
  57.7 0.7 %slice_bitcast_fusion = f32[2,8,4096]{2,1,0:T(8,128)} fusion(f32[2,2,16,4096]{3,2,1,0:T(8,128)S(1)} %multiply_add_fusion), kind=kLoop, calls=%fused_computation.45 | loop fusion | bytes 524288 | tf_op jit(solution)/shard_map/squeeze | solution.py:118
  58.4 7.0 %all-to-all-done.1 = f32[8,2,128]{2,1,0:T(2,128)S(1)} async-done(((f32[8,2,128]{2,1,0:T(2,128)}), f32[8,2,128]{2,1,0:T(2,128)S(1)}, u32[]{:S(2)}, u32[]{:S(2)}) %all-to-all-start.1) | async-done | bytes 8224 | tf_op jit(solution)/shard_map/all_to_all | solution.py:40
  65.4 0.6 reduce_sum.79
  (45 shorter events, 2.4 us)
Async XLA Ops:
  0.6 18.1 %copy-start.2 = (s32[4,8,4096]{2,1,0:T(8,128)S(1)}, s32[4,8,4096]{2,1,0:T(8,128)}, u32[]{:S(2)}) copy-start(s32[4,8,4096]{2,1,0:T(8,128)} %param.7) | copy-start | bytes 1572868
  2.0 17.5 %all-to-all-start = ((f32[8,2,128]{2,1,0:T(2,128)}), f32[8,2,128]{2,1,0:T(2,128)S(1)}, u32[]{:S(2)}, u32[]{:S(2)}) async-start(f32[8,2,128]{2,1,0:T(2,128)} %broadcast_in_dim.110), calls=%async_computation | async-start | bytes 16384 | tf_op jit(solution)/shard_map/all_to_all | solution.py:32
  10.0 9.2 %copy-start.3 = (bf16[4,8,4096]{2,1,0:T(8,128)(2,1)S(1)}, bf16[4,8,4096]{2,1,0:T(8,128)(2,1)}, u32[]{:S(2)}) copy-start(bf16[4,8,4096]{2,1,0:T(8,128)(2,1)} %param.8) | copy-start | bytes 786436
  10.0 21.8 %collective-permute-start.2 = (f32[2,2,4,4096]{3,2,1,0:T(4,128)S(1)}, f32[2,2,4,4096]{3,2,1,0:T(4,128)S(1)}, u32[]{:S(2)}, u32[]{:S(2)}) collective-permute-start(f32[2,2,4,4096]{3,2,1,0:T(4,128)S(1)} %get-tuple-element.12), channel_id=1, source_target_pairs={{0,1},{1,2},{2,3},{3,4},{4,5},{5,6},{6,7},{7,8},{8,9},{9,10},{10,1... | collective-permute-start | bytes 786440 | tf_op jit(solution)/shard_map/ppermute | solution.py:20
  12.1 19.8 %collective-permute-start.3 = (f32[2,2,4,4096]{3,2,1,0:T(4,128)S(1)}, f32[2,2,4,4096]{3,2,1,0:T(4,128)S(1)}, u32[]{:S(2)}, u32[]{:S(2)}) collective-permute-start(f32[2,2,4,4096]{3,2,1,0:T(4,128)S(1)} %get-tuple-element.13), channel_id=1, source_target_pairs={{1,0},{2,1},{3,2},{4,3},{5,4},{6,5},{7,6},{8,7},{9,8},{10,9},{11,1... | collective-permute-start | bytes 786440 | tf_op jit(solution)/shard_map/ppermute | solution.py:20
  21.5 10.3 %copy-start = (f32[2,8,4096]{2,1,0:T(8,128)S(1)}, f32[2,8,4096]{2,1,0:T(8,128)}, u32[]{:S(2)}) copy-start(f32[2,8,4096]{2,1,0:T(8,128)} %param.9) | copy-start | bytes 786436
  21.5 10.3 %copy-start.1 = (f32[2,8,4096]{2,1,0:T(8,128)S(1)}, f32[2,8,4096]{2,1,0:T(8,128)}, u32[]{:S(2)}) copy-start(f32[2,8,4096]{2,1,0:T(8,128)} %param.10) | copy-start | bytes 786436
  22.1 4.5 %collective-permute-start.1 = (f32[2,4096]{1,0:T(2,128)S(1)}, f32[2,4096]{1,0:T(2,128)S(1)}, u32[]{:S(2)}, u32[]{:S(2)}) collective-permute-start(f32[2,4096]{1,0:T(2,128)S(1)} %get-tuple-element.25), channel_id=1, source_target_pairs={{1,0},{2,1},{3,2},{4,3},{5,4},{6,5},{7,6},{8,7},{9,8},{10,9},{11,1... | collective-permute-start | bytes 98312 | tf_op jit(solution)/shard_map/ppermute | solution.py:20
  24.1 7.3 %collective-permute-start = (f32[2,4096]{1,0:T(2,128)S(1)}, f32[2,4096]{1,0:T(2,128)S(1)}, u32[]{:S(2)}, u32[]{:S(2)}) collective-permute-start(f32[2,4096]{1,0:T(2,128)S(1)} %get-tuple-element.26), channel_id=1, source_target_pairs={{0,1},{1,2},{2,3},{3,4},{4,5},{5,6},{6,7},{7,8},{8,9},{9,10},{10,1... | collective-permute-start | bytes 98312 | tf_op jit(solution)/shard_map/ppermute | solution.py:20
  50.5 14.9 %all-to-all-start.1 = ((f32[8,2,128]{2,1,0:T(2,128)}), f32[8,2,128]{2,1,0:T(2,128)S(1)}, u32[]{:S(2)}, u32[]{:S(2)}) async-start(f32[8,2,128]{2,1,0:T(2,128)} %fusion.21), calls=%async_computation.1 | async-start | bytes 16384 | tf_op jit(solution)/shard_map/all_to_all | solution.py:40

commit v3 on v2

--- a/solution.py
+++ b/solution.py
@@ -87,10 +87,16 @@
     matched = jnp.zeros((block_rows * len(SHIFTS), cells_x, cells_y), jnp.float32)
     for entry in range(foot_index.shape[0]):
         matched = matched + jnp.where(key[entry][None] == codes, weights[entry][None], 0.0)
-    upsampled = jnp.repeat(strip, factor, axis=1)
-    candidates = jnp.stack(
-        [lane_shift(upsampled[row], -factor * shift) for row in range(block_rows) for shift in SHIFTS]
-    )
+    span = 128
+    chunks = block_cols // span
+    spread = (
+        lax.broadcasted_iota(jnp.int32, (span, span * factor), 1) // factor
+        == lax.broadcasted_iota(jnp.int32, (span, span * factor), 0)
+    ).astype(jnp.float32)
+    shifted = jnp.stack([lane_shift(strip[row], -shift) for row in range(block_rows) for shift in SHIFTS])
+    candidates = jnp.dot(
+        shifted.reshape(-1, span), spread, precision=lax.Precision.HIGHEST
+    ).reshape(block_rows * len(SHIFTS), cells_y)
     density_cell = jnp.sum(matched * candidates[:, None, :], axis=0)
     reach = 2
     above = from_behind(density_cell[-reach:], "tile", 1)
@@ -110,10 +116,13 @@
     total_waves = source_fwd.shape[0] * lax.axis_size("wl")
     scaled = high_contrast / total_waves * sense[HALO : HALO + cells_x]
     per_col = jnp.sum(matched * scaled[None], axis=1)
-    pooled = per_col.reshape(block_rows, len(SHIFTS), block_cols, factor).sum(axis=3)
-    partial_grad = jnp.zeros((block_rows, block_cols), jnp.float32)
+    per_col = per_col.reshape(block_rows, len(SHIFTS), cells_y)
+    gathered = jnp.zeros((block_rows, cells_y), jnp.float32)
     for slot, shift in enumerate(SHIFTS):
-        partial_grad = partial_grad + lane_shift(pooled[:, slot], shift)
+        gathered = gathered + lane_shift(per_col[:, slot], factor * shift)
+    partial_grad = jnp.dot(
+        gathered.reshape(-1, span * factor), spread.T, precision=lax.Precision.HIGHEST
+    ).reshape(block_rows, block_cols)
     density_grad = scatter_sum_columns(partial_grad, "wl")
     return (history[ITERS - 1][0, :, HALO : HALO + cells_x], density_grad)
 

time: 66.3 us -> 54.5 us (0.82)
  local copies, waits for them, and re-layouts: 12.5 us -> 5.41 us
  other arithmetic: 14.5 us -> 9.38 us
    reshape x1 -> x2, local copies, waits for them, and re-layouts: 6.65 us -> 0.04 us  [the longest x1 0.03 us: shards(): per_col = per_col.reshape(block_rows, len(SHIFTS), cells_y)]
    reduce_sum x1 -> x0, other arithmetic: 3.9 us -> none  [shards(): per_col.reshape(block_rows, len(SHIFTS), block_cols, factor).sum(axis=3)]
    broadcast_in_dim x6 -> x0, local copies, waits for them, and re-layouts: 1.59 us -> none  [shards(): upsampled = jnp.repeat(strip, factor, axis=1)]
    transpose x1 -> x0, other arithmetic: 0.7 us -> none  [scatter_sum_columns(): pieces = value.reshape(rows, count, cols // count).transpose(1, 0, 2)]
    transpose x0 -> x1, local copies, waits for them, and re-layouts: none -> 0.67 us  [scatter_sum_columns(): pieces = value.reshape(rows, count, cols // count).transpose(1, 0, 2)]
  transfers between devices with their start and end apart: 6 -> 6, of which waited for: 2 -> 2; matrix products, arithmetic and copies ran while one was open for 10% -> 8% of each run, Pallas kernels for 0% -> 0%
where the time goes in v3:
time: 54.5 us; the launch traced here: 54.2 us
  starting transfers between devices  26.1 us (48%)
  waiting for transfers between devices  11.9 us (22%)
  other arithmetic  9.38 us (17%)
  local copies, waits for them, and re-layouts  5.41 us (10%)
  between operations  1.03 us (2%)
    ppermute x4, starting transfers between devices, from_behind(): lax.ppermute(value, axis, [(source, source + steps) for source in range(f...  12.1 us
    all_to_all x1, starting transfers between devices, scatter_sum_columns(): return lax.all_to_all(pieces, axis, 0, 0, tiled=True).sum(axis=0)  7.21 us
    all_to_all x1, waiting for transfers between devices, scatter_sum_columns(): return lax.all_to_all(pieces, axis, 0, 0, tiled=True).sum(axis=0)  6.95 us
    all_to_all x1, starting transfers between devices, gather_columns(): pieces = lax.all_to_all(copies, axis, 0, 0, tiled=True)  6.71 us
    ppermute x4, waiting for transfers between devices, from_behind(): lax.ppermute(value, axis, [(source, source + steps) for source in range(f...  4.92 us
    add x4, other arithmetic, march(): field_e + inverse * (field_hy - hy_down - (field_hx - hx_left) - current)  3.39 us
    add x3, other arithmetic, march(): field_hy = field_hy + hy_step * (e_up - field_e)  1.36 us
    broadcast_in_dim x1, local copies, waits for them, and re-layouts, gather_columns(): copies = jnp.broadcast_to(value[None], (count,) + value.shape)  1.34 us
  transfers between devices with their start and end apart: 6, of which 2 were waited for; matrix products, arithmetic and copies ran while one was open for 8% of the time, Pallas kernels for 0%

profile of v3, /device:TPU:32, one launch (start us, length us, event | category | flops | bytes accessed | tf_op | source)
XLA Modules:
  0.0 54.2 jit_solution(14186582095642833752)
XLA Ops:
  0.6 1.3 %broadcast_in_dim.96 = f32[8,2,128]{2,1,0:T(2,128)} broadcast(f32[2,128]{1,0:T(2,128)} %param.6), dimensions={1,2} | broadcast | bytes 9216 | tf_op jit(solution)/shard_map/broadcast_in_dim | solution.py:31
  2.0 6.7 %all-to-all-start = ((f32[8,2,128]{2,1,0:T(2,128)}), f32[8,2,128]{2,1,0:T(2,128)S(1)}, u32[]{:S(2)}, u32[]{:S(2)}) async-start(f32[8,2,128]{2,1,0:T(2,128)} %broadcast_in_dim.96), calls=%async_computation | async-start | bytes 16384 | tf_op jit(solution)/shard_map/all_to_all | solution.py:32
  8.7 1.3 %fusion.12 = (f32[2,2,4,4096]{3,2,1,0:T(4,128)S(1)}, f32[2,2,4,4096]{3,2,1,0:T(4,128)S(1)}) fusion(f32[1,2,8,4096]{3,2,1,0:T(8,128)} %bitcast.73, f32[1,2,8,4096]{3,2,1,0:T(8,128)} %bitcast.79), kind=kLoop, calls=%fused_computation.45 | loop fusion | flops 131072 | bytes 1048576 | tf_op jit(solution)/shard_map/stack | solution.py:77
  10.0 1.9 %collective-permute-start.2 = (f32[2,2,4,4096]{3,2,1,0:T(4,128)S(1)}, f32[2,2,4,4096]{3,2,1,0:T(4,128)S(1)}, u32[]{:S(2)}, u32[]{:S(2)}) collective-permute-start(f32[2,2,4,4096]{3,2,1,0:T(4,128)S(1)} %get-tuple-element.12), channel_id=1, source_target_pairs={{0,1},{1,2},{2,3},{3,4},{4,5},{5,6},{6,7},{7,8},{8,9},{9,10},{10,1... | collective-permute-start | bytes 786440 | tf_op jit(solution)/shard_map/ppermute | solution.py:20
  11.9 5.8 %collective-permute-start.3 = (f32[2,2,4,4096]{3,2,1,0:T(4,128)S(1)}, f32[2,2,4,4096]{3,2,1,0:T(4,128)S(1)}, u32[]{:S(2)}, u32[]{:S(2)}) collective-permute-start(f32[2,2,4,4096]{3,2,1,0:T(4,128)S(1)} %get-tuple-element.13), channel_id=1, source_target_pairs={{1,0},{2,1},{3,2},{4,3},{5,4},{6,5},{7,6},{8,7},{9,8},{10,9},{11,1... | collective-permute-start | bytes 786440 | tf_op jit(solution)/shard_map/ppermute | solution.py:20
  18.0 0.5 fusion.2
  18.6 0.4 copy-done.3
  19.3 0.2 fusion.14
  19.6 0.6 %multiply_reduce_fusion.1 = f32[8,4096]{1,0:T(8,128)S(1)} fusion(f32[10,4096]{1,0:T(8,128)S(1)} %mul.220, f32[8,4096]{1,0:T(8,128)S(1)} %get-tuple-element.19, s32[8,4096]{1,0:T(8,128)S(1)} %get-tuple-element.15, f32[8,4096]{1,0:T(8,128)S(1)} %get-tuple-element.20, s32[8,4096]{1,0:T(8,128)S(1)} %get-tuple-element.16, f32[8,4096]{1,0:T(8,128)S(1)} %get-tuple-element.21, ...), kind=kLoop, calls=%fused_computation.1 | loop fusion | flops 4227072 | bytes 1343488 | tf_op jit(solution)/shard_map/reduce_sum | solution.py:100
  20.2 2.1 %collective-permute-start.1 = (f32[2,4096]{1,0:T(2,128)S(1)}, f32[2,4096]{1,0:T(2,128)S(1)}, u32[]{:S(2)}, u32[]{:S(2)}) collective-permute-start(f32[2,4096]{1,0:T(2,128)S(1)} %get-tuple-element.30), channel_id=1, source_target_pairs={{1,0},{2,1},{3,2},{4,3},{5,4},{6,5},{7,6},{8,7},{9,8},{10,9},{11,1... | collective-permute-start | bytes 98312 | tf_op jit(solution)/shard_map/ppermute | solution.py:20
  22.3 2.4 %collective-permute-start = (f32[2,4096]{1,0:T(2,128)S(1)}, f32[2,4096]{1,0:T(2,128)S(1)}, u32[]{:S(2)}, u32[]{:S(2)}) collective-permute-start(f32[2,4096]{1,0:T(2,128)S(1)} %get-tuple-element.31), channel_id=1, source_target_pairs={{0,1},{1,2},{2,3},{3,4},{4,5},{5,6},{6,7},{7,8},{8,9},{9,10},{10,1... | collective-permute-start | bytes 98312 | tf_op jit(solution)/shard_map/ppermute | solution.py:20
  24.7 4.9 %collective-permute-done = f32[2,4096]{1,0:T(2,128)S(1)} collective-permute-done((f32[2,4096]{1,0:T(2,128)S(1)}, f32[2,4096]{1,0:T(2,128)S(1)}, u32[]{:S(2)}, u32[]{:S(2)}) %collective-permute-start) | collective-permute-done | bytes 32800 | tf_op jit(solution)/shard_map/ppermute | solution.py:20
  29.7 0.3 concatenate.66
  30.1 0.3 multiply_add_fusion.8
  30.4 0.3 slice.263
  30.9 0.5 %multiply_add_fusion.7 = (f32[2,2,16,4096]{3,2,1,0:T(8,128)S(1)}, f32[2,2,16,4096]{3,2,1,0:T(8,128)S(1)}) fusion(f32[2,2,15,4096]{3,2,1,0:T(8,128)S(1)} %slice.261, f32[16]{0:T(128)S(1)} %get-tuple-element.51, f32[16]{0:T(128)S(1)} %pad_multiply_fusion, f32[2,2,4,4096]{3,2,1,0:T(4,128)S(1)} %collective-permute-done.3, f32[1,2,8,4096]{3,2,1,0:T(8,128)S(1)} %bitcast.81, ...), kind=kLoop, calls=%fused_computation.19 | loop fusion | flops 3670016 | bytes 5734344 | tf_op jit(solution)/shard_map/add | solution.py:63
  31.4 0.8 %multiply_add_fusion.5 = f32[2,2,16,4096]{3,2,1,0:T(8,128)S(1)} fusion(f32[2,2,16,4096]{3,2,1,0:T(8,128)S(1)} %get-tuple-element.7, f32[2,2,16,4095]{3,2,1,0:T(8,128)S(1)} %bitcast.72, f32[2,2,16,4096]{3,2,1,0:T(8,128)S(1)} %get-tuple-element.6, f32[2,2,15,4096]{3,2,1,0:T(8,128)S(1)} %bitcast.71, f32[2]{0:T(128)S(1)} %get-tuple-element.45, ...), kind=kLoop, calls=%fused_computation.16 | loop fusion | flops 4718592 | bytes 7028560 | tf_op jit(solution)/shard_map/add | solution.py:68
  32.2 0.3 slice.267
  32.6 0.4 multiply_add_fusion.4
  33.1 0.9 %multiply_add_fusion.2 = f32[2,2,16,4096]{3,2,1,0:T(8,128)S(1)} fusion(f32[2,2,16,4096]{3,2,1,0:T(8,128)S(1)} %multiply_add_fusion.5, f32[2,2,16,4096]{3,2,1,0:T(8,128)S(1)} %get-tuple-element.11, f32[2,2,16,4095]{3,2,1,0:T(8,128)S(1)} %bitcast.70, f32[2,2,16,4096]{3,2,1,0:T(8,128)S(1)} %get-tuple-element.10, f32[2,2,15,4096]{3,2,1,0:T(8,128)S(1)} %bitcast.69, ...), kind=kLoop, calls=%fused_computation.12 | loop fusion | flops 5505024 | bytes 8077136 | tf_op jit(solution)/shard_map/add | solution.py:68
  34.1 0.3 slice.271
  34.5 0.4 multiply_add_fusion.1
  34.9 1.4 %multiply_add_fusion = f32[2,2,16,4096]{3,2,1,0:T(8,128)S(1)} fusion(f32[2,2,16,4096]{3,2,1,0:T(8,128)S(1)} %multiply_add_fusion.2, f32[2,2,16,4095]{3,2,1,0:T(8,128)S(1)} %bitcast.86, f32[2,2,15,4096]{3,2,1,0:T(8,128)S(1)} %bitcast.85, f32[2,2,16,4096]{3,2,1,0:T(8,128)S(1)} %multiply_add_fusion.5, f32[2]{0:T(128)S(1)} %get-tuple-element.44, ...), kind=kLoop, calls=%fused_computation.9 | loop fusion | flops 7864320 | bytes 11157136 | tf_op jit(solution)/shard_map/add | solution.py:68
  36.3 0.1 fusion.7
  36.5 0.8 %multiply_reduce_fusion = f32[10,4096]{1,0:T(8,128)S(1)} fusion(f32[8,4096]{1,0:T(8,128)S(1)} %fusion.16, f32[8,4096]{1,0:T(8,128)S(1)} %get-tuple-element.19, s32[8,4096]{1,0:T(8,128)S(1)} %get-tuple-element.15, f32[8,4096]{1,0:T(8,128)S(1)} %get-tuple-element.20, s32[8,4096]{1,0:T(8,128)S(1)} %get-tuple-element.16, f32[8,4096]{1,0:T(8,128)S(1)} %get-tuple-element.21, ...), kind=kLoop, calls=%fused_computation | loop fusion | flops 4218880 | bytes 1343488 | tf_op jit(solution)/shard_map/reduce_sum | solution.py:118
  37.6 0.2 fusion.26
  37.8 0.2 convolution_bitcast_fusion
  38.0 0.7 %copy.21 = f32[8,2,128]{2,1,0:T(2,128)} copy(f32[8,2,128]{2,0,1:T(8,128)S(1)} %convolution_bitcast_fusion) | data formatting | bytes 16384 | tf_op jit(solution)/shard_map/transpose | solution.py:39
  38.7 7.2 %all-to-all-start.1 = ((f32[8,2,128]{2,1,0:T(2,128)}), f32[8,2,128]{2,1,0:T(2,128)S(1)}, u32[]{:S(2)}, u32[]{:S(2)}) async-start(f32[8,2,128]{2,1,0:T(2,128)} %copy.21), calls=%async_computation.1 | async-start | bytes 16384 | tf_op jit(solution)/shard_map/all_to_all | solution.py:40
  45.9 0.7 %slice_bitcast_fusion = f32[2,8,4096]{2,1,0:T(8,128)} fusion(f32[2,2,16,4096]{3,2,1,0:T(8,128)S(1)} %multiply_add_fusion), kind=kLoop, calls=%fused_computation.46 | loop fusion | bytes 524288 | tf_op jit(solution)/shard_map/squeeze | solution.py:127
  46.6 7.0 %all-to-all-done.1 = f32[8,2,128]{2,1,0:T(2,128)S(1)} async-done(((f32[8,2,128]{2,1,0:T(2,128)}), f32[8,2,128]{2,1,0:T(2,128)S(1)}, u32[]{:S(2)}, u32[]{:S(2)}) %all-to-all-start.1) | async-done | bytes 8224 | tf_op jit(solution)/shard_map/all_to_all | solution.py:40
  53.6 0.6 %reduce_sum.69 = f32[2,128]{1,0:T(2,128)} reduce(f32[8,2,128]{2,1,0:T(2,128)S(1)} %all-to-all-done.1, f32[]{:T(128)} %constant.84.clone.1), dimensions={0}, to_apply=%region_6.7 | reduce | flops 1792 | bytes 9220 | tf_op jit(solution)/shard_map/reduce_sum | solution.py:40
  (47 shorter events, 1.5 us)
Async XLA Ops:
  0.6 17.2 %copy-start.4 = (f32[2]{0:T(128)S(1)}, f32[2]{0:T(128)}, u32[]{:S(2)}) copy-start(f32[2]{0:T(128)} %param.11) | copy-start | bytes 28
  0.6 17.4 %copy-start.2 = (s32[4,8,4096]{2,1,0:T(8,128)S(1)}, s32[4,8,4096]{2,1,0:T(8,128)}, u32[]{:S(2)}) copy-start(s32[4,8,4096]{2,1,0:T(8,128)} %param.7) | copy-start | bytes 1572868
  2.0 17.1 %all-to-all-start = ((f32[8,2,128]{2,1,0:T(2,128)}), f32[8,2,128]{2,1,0:T(2,128)S(1)}, u32[]{:S(2)}, u32[]{:S(2)}) async-start(f32[8,2,128]{2,1,0:T(2,128)} %broadcast_in_dim.96), calls=%async_computation | async-start | bytes 16384 | tf_op jit(solution)/shard_map/all_to_all | solution.py:32
  10.0 20.1 %collective-permute-start.2 = (f32[2,2,4,4096]{3,2,1,0:T(4,128)S(1)}, f32[2,2,4,4096]{3,2,1,0:T(4,128)S(1)}, u32[]{:S(2)}, u32[]{:S(2)}) collective-permute-start(f32[2,2,4,4096]{3,2,1,0:T(4,128)S(1)} %get-tuple-element.12), channel_id=1, source_target_pairs={{0,1},{1,2},{2,3},{3,4},{4,5},{5,6},{6,7},{7,8},{8,9},{9,10},{10,1... | collective-permute-start | bytes 786440 | tf_op jit(solution)/shard_map/ppermute | solution.py:20
  11.9 18.2 %collective-permute-start.3 = (f32[2,2,4,4096]{3,2,1,0:T(4,128)S(1)}, f32[2,2,4,4096]{3,2,1,0:T(4,128)S(1)}, u32[]{:S(2)}, u32[]{:S(2)}) collective-permute-start(f32[2,2,4,4096]{3,2,1,0:T(4,128)S(1)} %get-tuple-element.13), channel_id=1, source_target_pairs={{1,0},{2,1},{3,2},{4,3},{5,4},{6,5},{7,6},{8,7},{9,8},{10,9},{11,1... | collective-permute-start | bytes 786440 | tf_op jit(solution)/shard_map/ppermute | solution.py:20
  18.0 1.0 %copy-start.3 = (bf16[4,8,4096]{2,1,0:T(8,128)(2,1)S(1)}, bf16[4,8,4096]{2,1,0:T(8,128)(2,1)}, u32[]{:S(2)}) copy-start(bf16[4,8,4096]{2,1,0:T(8,128)(2,1)} %param.8) | copy-start | bytes 786436
  20.2 9.9 %copy-start = (f32[2,8,4096]{2,1,0:T(8,128)S(1)}, f32[2,8,4096]{2,1,0:T(8,128)}, u32[]{:S(2)}) copy-start(f32[2,8,4096]{2,1,0:T(8,128)} %param.9) | copy-start | bytes 786436
  20.2 9.9 %copy-start.1 = (f32[2,8,4096]{2,1,0:T(8,128)S(1)}, f32[2,8,4096]{2,1,0:T(8,128)}, u32[]{:S(2)}) copy-start(f32[2,8,4096]{2,1,0:T(8,128)} %param.10) | copy-start | bytes 786436
  20.2 4.5 %collective-permute-start.1 = (f32[2,4096]{1,0:T(2,128)S(1)}, f32[2,4096]{1,0:T(2,128)S(1)}, u32[]{:S(2)}, u32[]{:S(2)}) collective-permute-start(f32[2,4096]{1,0:T(2,128)S(1)} %get-tuple-element.30), channel_id=1, source_target_pairs={{1,0},{2,1},{3,2},{4,3},{5,4},{6,5},{7,6},{8,7},{9,8},{10,9},{11,1... | collective-permute-start | bytes 98312 | tf_op jit(solution)/shard_map/ppermute | solution.py:20
  22.3 7.3 %collective-permute-start = (f32[2,4096]{1,0:T(2,128)S(1)}, f32[2,4096]{1,0:T(2,128)S(1)}, u32[]{:S(2)}, u32[]{:S(2)}) collective-permute-start(f32[2,4096]{1,0:T(2,128)S(1)} %get-tuple-element.31), channel_id=1, source_target_pairs={{0,1},{1,2},{2,3},{3,4},{4,5},{5,6},{6,7},{7,8},{8,9},{9,10},{10,1... | collective-permute-start | bytes 98312 | tf_op jit(solution)/shard_map/ppermute | solution.py:20
  38.7 14.9 %all-to-all-start.1 = ((f32[8,2,128]{2,1,0:T(2,128)}), f32[8,2,128]{2,1,0:T(2,128)S(1)}, u32[]{:S(2)}, u32[]{:S(2)}) async-start(f32[8,2,128]{2,1,0:T(2,128)} %copy.21), calls=%async_computation.1 | async-start | bytes 16384 | tf_op jit(solution)/shard_map/all_to_all | solution.py:40

commit v4 on v3

--- a/solution.py
+++ b/solution.py
@@ -48,6 +48,18 @@
     return lax.slice_in_dim(padded, start, start + width, axis=vector.ndim - 1)
 
 
+def shifted_in(value, axis, shift):
+    config = [(0, 0, 0)] * value.ndim
+    size = value.shape[axis]
+    if shift > 0:
+        config[axis] = (shift, 0, 0)
+        kept = lax.slice_in_dim(value, 0, size - shift, axis=axis)
+    else:
+        config[axis] = (0, -shift, 0)
+        kept = lax.slice_in_dim(value, -shift, size, axis=axis)
+    return lax.pad(kept, jnp.zeros((), value.dtype), config)
+
+
 def march(source, drive, density_cell, inverse, hy_step):
     field_e = jnp.zeros_like(source)
     field_hx = jnp.zeros_like(source)
@@ -55,15 +67,13 @@
     current = jnp.zeros_like(source)
     history = []
     for turn in range(ITERS):
-        row_zero = jnp.zeros_like(source[:, :, :1, :])
-        col_zero = jnp.zeros_like(source[:, :, :, :1])
-        e_up = jnp.concatenate([field_e[:, :, 1:, :], row_zero], 2)
-        e_right = jnp.concatenate([field_e[:, :, :, 1:], col_zero], 3)
+        e_up = shifted_in(field_e, 2, -1)
+        e_right = shifted_in(field_e, 3, -1)
         field_hx = field_hx - time_step * (e_right - field_e)
         field_hy = field_hy + hy_step * (e_up - field_e)
         current = drude_decay * current + drude_gain * density_cell * field_e
-        hy_down = jnp.concatenate([row_zero, field_hy[:, :, :-1, :]], 2)
-        hx_left = jnp.concatenate([col_zero, field_hx[:, :, :, :-1]], 3)
+        hy_down = shifted_in(field_hy, 2, 1)
+        hx_left = shifted_in(field_hx, 3, 1)
         field_e = (
             field_e
             + inverse * (field_hy - hy_down - (field_hx - hx_left) - current)
@@ -97,10 +107,12 @@
     candidates = jnp.dot(
         shifted.reshape(-1, span), spread, precision=lax.Precision.HIGHEST
     ).reshape(block_rows * len(SHIFTS), cells_y)
+    reach = 2
+    last_rows = jnp.sum(matched[:, -reach:] * candidates[:, None, :], axis=0)
+    first_rows = jnp.sum(matched[:, :reach] * candidates[:, None, :], axis=0)
+    above = from_behind(last_rows, "tile", 1)
+    below = from_behind(first_rows, "tile", -1)
     density_cell = jnp.sum(matched * candidates[:, None, :], axis=0)
-    reach = 2
-    above = from_behind(density_cell[-reach:], "tile", 1)
-    below = from_behind(density_cell[:reach], "tile", -1)
     pad = jnp.zeros((HALO - reach, cells_y), jnp.float32)
     density_ext = jnp.concatenate([pad, above, density_cell, below, pad], axis=0)
     rows_ext = cells_x + 2 * HALO
@@ -120,10 +132,17 @@
     gathered = jnp.zeros((block_rows, cells_y), jnp.float32)
     for slot, shift in enumerate(SHIFTS):
         gathered = gathered + lane_shift(per_col[:, slot], factor * shift)
-    partial_grad = jnp.dot(
-        gathered.reshape(-1, span * factor), spread.T, precision=lax.Precision.HIGHEST
-    ).reshape(block_rows, block_cols)
-    density_grad = scatter_sum_columns(partial_grad, "wl")
+    count = lax.axis_size("wl")
+    pooled = jnp.einsum(
+        "rky,cy->krc",
+        gathered.reshape(block_rows, chunks, span * factor),
+        spread,
+        precision=lax.Precision.HIGHEST,
+    )
+    density_grad = lax.all_to_all(
+        pooled.reshape(count, chunks // count, block_rows, span).transpose(0, 2, 1, 3).reshape(count, block_rows, -1),
+        "wl", 0, 0, tiled=True,
+    ).sum(axis=0)
     return (history[ITERS - 1][0, :, HALO : HALO + cells_x], density_grad)
 
 

time: 54.5 us -> 55.1 us (1.011)
  other arithmetic: 9.38 us -> 10.4 us
    sin x1, other arithmetic: 0.07 us -> 0.72 us  [shards(): jnp.sin(omega * (turn + 1.0))[None, :, None, None]]
    slice x9 -> x8, local copies, waits for them, and re-layouts: 1.31 us -> 1.28 us  [shifted_in(): kept = lax.slice_in_dim(value, -shift, size, axis=axis)]
  transfers between devices with their start and end apart: 6 -> 6, of which waited for: 2 -> 2; matrix products, arithmetic and copies ran while one was open for 8% -> 10% of each run, Pallas kernels for 0% -> 0%
where the time goes in v4:
time: 55.1 us; the launch traced here: 54.8 us
  starting transfers between devices  26.1 us (47%)
  waiting for transfers between devices  11.9 us (22%)
  other arithmetic  10.4 us (19%)
  local copies, waits for them, and re-layouts  5 us (9%)
  between operations  1.02 us (2%)
    ppermute x4, starting transfers between devices, from_behind(): lax.ppermute(value, axis, [(source, source + steps) for source in range(f...  12.1 us
    all_to_all x1, starting transfers between devices, shards(): lax.all_to_all(pooled.reshape(count, chunks // count, block_rows, span).t...  7.21 us
    all_to_all x1, waiting for transfers between devices, shards(): lax.all_to_all(pooled.reshape(count, chunks // count, block_rows, span).t...  6.95 us
    all_to_all x1, starting transfers between devices, gather_columns(): pieces = lax.all_to_all(copies, axis, 0, 0, tiled=True)  6.71 us
    ppermute x4, waiting for transfers between devices, from_behind(): lax.ppermute(value, axis, [(source, source + steps) for source in range(f...  4.91 us
    add x4, other arithmetic, march(): field_e + inverse * (field_hy - hy_down - (field_hx - hx_left) - current)  3.39 us
    add x3, other arithmetic, march(): field_hy = field_hy + hy_step * (e_up - field_e)  1.36 us
    broadcast_in_dim x1, local copies, waits for them, and re-layouts, gather_columns(): copies = jnp.broadcast_to(value[None], (count,) + value.shape)  1.34 us
  transfers between devices with their start and end apart: 6, of which 2 were waited for; matrix products, arithmetic and copies ran while one was open for 10% of the time, Pallas kernels for 0%

profile of v4, /device:TPU:32, one launch (start us, length us, event | category | flops | bytes accessed | tf_op | source)
XLA Modules:
  0.0 54.8 jit_solution(9315886033134191630)
XLA Ops:
  0.6 1.3 %broadcast_in_dim.96 = f32[8,2,128]{2,1,0:T(2,128)} broadcast(f32[2,128]{1,0:T(2,128)} %param.6), dimensions={1,2} | broadcast | bytes 9216 | tf_op jit(solution)/shard_map/broadcast_in_dim | solution.py:31
  2.0 6.7 %all-to-all-start = ((f32[8,2,128]{2,1,0:T(2,128)}), f32[8,2,128]{2,1,0:T(2,128)S(1)}, u32[]{:S(2)}, u32[]{:S(2)}) async-start(f32[8,2,128]{2,1,0:T(2,128)} %broadcast_in_dim.96), calls=%async_computation | async-start | bytes 16384 | tf_op jit(solution)/shard_map/all_to_all | solution.py:32
  8.7 1.3 %fusion.14 = (f32[2,2,4,4096]{3,2,1,0:T(4,128)S(1)}, f32[2,2,4,4096]{3,2,1,0:T(4,128)S(1)}) fusion(f32[1,2,8,4096]{3,2,1,0:T(8,128)} %bitcast.73, f32[1,2,8,4096]{3,2,1,0:T(8,128)} %bitcast.79), kind=kLoop, calls=%fused_computation.49 | loop fusion | flops 131072 | bytes 1048576 | tf_op jit(solution)/shard_map/stack | solution.py:87
  10.0 2.1 %collective-permute-start.2 = (f32[2,2,4,4096]{3,2,1,0:T(4,128)S(1)}, f32[2,2,4,4096]{3,2,1,0:T(4,128)S(1)}, u32[]{:S(2)}, u32[]{:S(2)}) collective-permute-start(f32[2,2,4,4096]{3,2,1,0:T(4,128)S(1)} %get-tuple-element.16), channel_id=1, source_target_pairs={{0,1},{1,2},{2,3},{3,4},{4,5},{5,6},{6,7},{7,8},{8,9},{9,10},{10,1... | collective-permute-start | bytes 786440 | tf_op jit(solution)/shard_map/ppermute | solution.py:20
  12.1 5.8 %collective-permute-start.3 = (f32[2,2,4,4096]{3,2,1,0:T(4,128)S(1)}, f32[2,2,4,4096]{3,2,1,0:T(4,128)S(1)}, u32[]{:S(2)}, u32[]{:S(2)}) collective-permute-start(f32[2,2,4,4096]{3,2,1,0:T(4,128)S(1)} %get-tuple-element.17), channel_id=1, source_target_pairs={{1,0},{2,1},{3,2},{4,3},{5,4},{6,5},{7,6},{8,7},{9,8},{10,9},{11,1... | collective-permute-start | bytes 786440 | tf_op jit(solution)/shard_map/ppermute | solution.py:20
  18.0 0.7 %multiply_sine_fusion = (f32[2]{0:T(128)S(1)}, f32[2]{0:T(128)S(1)}, f32[2]{0:T(128)S(1)}, f32[2]{0:T(128)S(1)}) fusion(f32[2]{0:T(128)} %param.11), kind=kLoop, calls=%fused_computation.116 | loop fusion | flops 6 | bytes 40 | tf_op jit(solution)/shard_map/sin | solution.py:123
  18.8 0.5 fusion.2
  19.7 0.2 fusion.16
  20.0 0.6 %multiply_reduce_fusion.1 = (f32[8,4096]{1,0:T(8,128)S(1)}, f32[10,8,4096]{2,1,0:T(8,128)S(1)}) fusion(f32[10,4096]{1,0:T(8,128)S(1)} %mul.234, f32[8,4096]{1,0:T(8,128)S(1)} %get-tuple-element.23, s32[8,4096]{1,0:T(8,128)S(1)} %get-tuple-element.19, f32[8,4096]{1,0:T(8,128)S(1)} %get-tuple-element.24, s32[8,4096]{1,0:T(8,128)S(1)} %get-tuple-element.20, ...), kind=kLoop, calls=%fused_computation.1 | loop fusion | flops 4227072 | bytes 2654208 | tf_op jit(solution)/shard_map/reduce_sum | solution.py:115
  20.6 0.4 fusion.12
  21.0 1.9 %collective-permute-start.1 = (f32[2,4096]{1,0:T(2,128)S(1)}, f32[2,4096]{1,0:T(2,128)S(1)}, u32[]{:S(2)}, u32[]{:S(2)}) collective-permute-start(f32[2,4096]{1,0:T(2,128)S(1)} %get-tuple-element.6), channel_id=1, source_target_pairs={{1,0},{2,1},{3,2},{4,3},{5,4},{6,5},{7,6},{8,7},{9,8},{10,9},{11,1... | collective-permute-start | bytes 98312 | tf_op jit(solution)/shard_map/ppermute | solution.py:20
  23.0 2.4 %collective-permute-start = (f32[2,4096]{1,0:T(2,128)S(1)}, f32[2,4096]{1,0:T(2,128)S(1)}, u32[]{:S(2)}, u32[]{:S(2)}) collective-permute-start(f32[2,4096]{1,0:T(2,128)S(1)} %get-tuple-element.7), channel_id=1, source_target_pairs={{0,1},{1,2},{2,3},{3,4},{4,5},{5,6},{6,7},{7,8},{8,9},{9,10},{10,1... | collective-permute-start | bytes 98312 | tf_op jit(solution)/shard_map/ppermute | solution.py:20
  25.4 4.9 %collective-permute-done = f32[2,4096]{1,0:T(2,128)S(1)} collective-permute-done((f32[2,4096]{1,0:T(2,128)S(1)}, f32[2,4096]{1,0:T(2,128)S(1)}, u32[]{:S(2)}, u32[]{:S(2)}) %collective-permute-start) | collective-permute-done | bytes 32800 | tf_op jit(solution)/shard_map/ppermute | solution.py:20
  30.3 0.3 concatenate.14
  30.8 0.3 multiply_add_fusion.8
  31.1 0.3 slice.263
  31.5 0.5 multiply_add_fusion.7
  32.1 0.8 %multiply_add_fusion.5 = f32[2,2,16,4096]{3,2,1,0:T(8,128)S(1)} fusion(f32[2,2,16,4096]{3,2,1,0:T(8,128)S(1)} %get-tuple-element.9, f32[2,2,16,4095]{3,2,1,0:T(8,128)S(1)} %bitcast.72, f32[2,2,16,4096]{3,2,1,0:T(8,128)S(1)} %get-tuple-element.8, f32[2,2,15,4096]{3,2,1,0:T(8,128)S(1)} %bitcast.71, f32[2]{0:T(128)S(1)} %get-tuple-element.47, ...), kind=kLoop, calls=%fused_computation.16 | loop fusion | flops 4718592 | bytes 7028560 | tf_op jit(solution)/shard_map/add | solution.py:78
  32.9 0.3 slice.267
  33.3 0.4 multiply_add_fusion.4
  33.7 0.9 %multiply_add_fusion.2 = f32[2,2,16,4096]{3,2,1,0:T(8,128)S(1)} fusion(f32[2,2,16,4096]{3,2,1,0:T(8,128)S(1)} %multiply_add_fusion.5, f32[2,2,16,4096]{3,2,1,0:T(8,128)S(1)} %get-tuple-element.13, f32[2,2,16,4095]{3,2,1,0:T(8,128)S(1)} %bitcast.70, f32[2,2,16,4096]{3,2,1,0:T(8,128)S(1)} %get-tuple-element.12, f32[2,2,15,4096]{3,2,1,0:T(8,128)S(1)} %bitcast.69, ...), kind=kLoop, calls=%fused_computation.12 | loop fusion | flops 5505024 | bytes 8077136 | tf_op jit(solution)/shard_map/add | solution.py:78
  34.8 0.3 slice.271
  35.2 0.4 multiply_add_fusion.1
  35.6 1.4 %multiply_add_fusion = f32[2,2,16,4096]{3,2,1,0:T(8,128)S(1)} fusion(f32[2,2,16,4096]{3,2,1,0:T(8,128)S(1)} %multiply_add_fusion.2, f32[2,2,16,4095]{3,2,1,0:T(8,128)S(1)} %bitcast.86, f32[2,2,15,4096]{3,2,1,0:T(8,128)S(1)} %bitcast.85, f32[2,2,16,4096]{3,2,1,0:T(8,128)S(1)} %multiply_add_fusion.5, f32[2]{0:T(128)S(1)} %get-tuple-element.46, ...), kind=kLoop, calls=%fused_computation.9 | loop fusion | flops 7864320 | bytes 11157136 | tf_op jit(solution)/shard_map/add | solution.py:78
  37.2 0.8 %multiply_reduce_fusion = f32[10,4096]{1,0:T(8,128)S(1)} fusion(f32[8,4096]{1,0:T(8,128)S(1)} %fusion.18, f32[8,4096]{1,0:T(8,128)S(1)} %get-tuple-element.23, s32[8,4096]{1,0:T(8,128)S(1)} %get-tuple-element.19, f32[8,4096]{1,0:T(8,128)S(1)} %get-tuple-element.24, s32[8,4096]{1,0:T(8,128)S(1)} %get-tuple-element.20, f32[8,4096]{1,0:T(8,128)S(1)} %get-tuple-element.25, ...), kind=kLoop, calls=%fused_computation | loop fusion | flops 4218880 | bytes 1343488 | tf_op jit(solution)/shard_map/reduce_sum | solution.py:130
  38.3 0.2 fusion.28
  38.5 0.2 convolution_bitcast_fusion
  38.7 0.7 %copy.21 = f32[8,2,128]{2,1,0:T(2,128)} copy(f32[8,2,128]{2,0,1:T(8,128)S(1)} %convolution_bitcast_fusion) | data formatting | bytes 16384 | tf_op jit(solution)/shard_map/rky,cy->krc/transpose | solution.py:136
  39.3 7.2 %all-to-all-start.1 = ((f32[8,2,128]{2,1,0:T(2,128)}), f32[8,2,128]{2,1,0:T(2,128)S(1)}, u32[]{:S(2)}, u32[]{:S(2)}) async-start(f32[8,2,128]{2,1,0:T(2,128)} %copy.21), calls=%async_computation.1 | async-start | bytes 16384 | tf_op jit(solution)/shard_map/all_to_all | solution.py:142
  46.5 0.7 %slice_bitcast_fusion = f32[2,8,4096]{2,1,0:T(8,128)} fusion(f32[2,2,16,4096]{3,2,1,0:T(8,128)S(1)} %multiply_add_fusion), kind=kLoop, calls=%fused_computation.50 | loop fusion | bytes 524288 | tf_op jit(solution)/shard_map/squeeze | solution.py:146
  47.3 7.0 %all-to-all-done.1 = f32[8,2,128]{2,1,0:T(2,128)S(1)} async-done(((f32[8,2,128]{2,1,0:T(2,128)}), f32[8,2,128]{2,1,0:T(2,128)S(1)}, u32[]{:S(2)}, u32[]{:S(2)}) %all-to-all-start.1) | async-done | bytes 8224 | tf_op jit(solution)/shard_map/all_to_all | solution.py:142
  54.2 0.6 %reduce_sum.89 = f32[2,128]{1,0:T(2,128)} reduce(f32[8,2,128]{2,1,0:T(2,128)S(1)} %all-to-all-done.1, f32[]{:T(128)} %constant.82.clone.1), dimensions={0}, to_apply=%region_8.9 | reduce | flops 1792 | bytes 9220 | tf_op jit(solution)/shard_map/reduce_sum | solution.py:145
  (45 shorter events, 1.6 us)
Async XLA Ops:
  0.6 18.2 %copy-start.2 = (s32[4,8,4096]{2,1,0:T(8,128)S(1)}, s32[4,8,4096]{2,1,0:T(8,128)}, u32[]{:S(2)}) copy-start(s32[4,8,4096]{2,1,0:T(8,128)} %param.7) | copy-start | bytes 1572868
  2.0 17.5 %all-to-all-start = ((f32[8,2,128]{2,1,0:T(2,128)}), f32[8,2,128]{2,1,0:T(2,128)S(1)}, u32[]{:S(2)}, u32[]{:S(2)}) async-start(f32[8,2,128]{2,1,0:T(2,128)} %broadcast_in_dim.96), calls=%async_computation | async-start | bytes 16384 | tf_op jit(solution)/shard_map/all_to_all | solution.py:32
  10.0 9.4 %copy-start.3 = (bf16[4,8,4096]{2,1,0:T(8,128)(2,1)S(1)}, bf16[4,8,4096]{2,1,0:T(8,128)(2,1)}, u32[]{:S(2)}) copy-start(bf16[4,8,4096]{2,1,0:T(8,128)(2,1)} %param.8) | copy-start | bytes 786436
  10.0 20.7 %collective-permute-start.2 = (f32[2,2,4,4096]{3,2,1,0:T(4,128)S(1)}, f32[2,2,4,4096]{3,2,1,0:T(4,128)S(1)}, u32[]{:S(2)}, u32[]{:S(2)}) collective-permute-start(f32[2,2,4,4096]{3,2,1,0:T(4,128)S(1)} %get-tuple-element.16), channel_id=1, source_target_pairs={{0,1},{1,2},{2,3},{3,4},{4,5},{5,6},{6,7},{7,8},{8,9},{9,10},{10,1... | collective-permute-start | bytes 786440 | tf_op jit(solution)/shard_map/ppermute | solution.py:20
  12.1 18.7 %collective-permute-start.3 = (f32[2,2,4,4096]{3,2,1,0:T(4,128)S(1)}, f32[2,2,4,4096]{3,2,1,0:T(4,128)S(1)}, u32[]{:S(2)}, u32[]{:S(2)}) collective-permute-start(f32[2,2,4,4096]{3,2,1,0:T(4,128)S(1)} %get-tuple-element.17), channel_id=1, source_target_pairs={{1,0},{2,1},{3,2},{4,3},{5,4},{6,5},{7,6},{8,7},{9,8},{10,9},{11,1... | collective-permute-start | bytes 786440 | tf_op jit(solution)/shard_map/ppermute | solution.py:20
  20.6 10.2 %copy-start = (f32[2,8,4096]{2,1,0:T(8,128)S(1)}, f32[2,8,4096]{2,1,0:T(8,128)}, u32[]{:S(2)}) copy-start(f32[2,8,4096]{2,1,0:T(8,128)} %param.9) | copy-start | bytes 786436
  20.6 10.2 %copy-start.1 = (f32[2,8,4096]{2,1,0:T(8,128)S(1)}, f32[2,8,4096]{2,1,0:T(8,128)}, u32[]{:S(2)}) copy-start(f32[2,8,4096]{2,1,0:T(8,128)} %param.10) | copy-start | bytes 786436
  21.0 4.4 %collective-permute-start.1 = (f32[2,4096]{1,0:T(2,128)S(1)}, f32[2,4096]{1,0:T(2,128)S(1)}, u32[]{:S(2)}, u32[]{:S(2)}) collective-permute-start(f32[2,4096]{1,0:T(2,128)S(1)} %get-tuple-element.6), channel_id=1, source_target_pairs={{1,0},{2,1},{3,2},{4,3},{5,4},{6,5},{7,6},{8,7},{9,8},{10,9},{11,1... | collective-permute-start | bytes 98312 | tf_op jit(solution)/shard_map/ppermute | solution.py:20
  23.0 7.3 %collective-permute-start = (f32[2,4096]{1,0:T(2,128)S(1)}, f32[2,4096]{1,0:T(2,128)S(1)}, u32[]{:S(2)}, u32[]{:S(2)}) collective-permute-start(f32[2,4096]{1,0:T(2,128)S(1)} %get-tuple-element.7), channel_id=1, source_target_pairs={{0,1},{1,2},{2,3},{3,4},{4,5},{5,6},{6,7},{7,8},{8,9},{9,10},{10,1... | collective-permute-start | bytes 98312 | tf_op jit(solution)/shard_map/ppermute | solution.py:20
  39.3 14.9 %all-to-all-start.1 = ((f32[8,2,128]{2,1,0:T(2,128)}), f32[8,2,128]{2,1,0:T(2,128)S(1)}, u32[]{:S(2)}, u32[]{:S(2)}) async-start(f32[8,2,128]{2,1,0:T(2,128)} %copy.21), calls=%async_computation.1 | async-start | bytes 16384 | tf_op jit(solution)/shard_map/all_to_all | solution.py:142

commit v5 on v4

--- a/solution.py
+++ b/solution.py
@@ -1,6 +1,8 @@
 import jax
 import jax.numpy as jnp
 from jax import lax
+from jax.experimental import pallas as pl
+from jax.experimental.pallas import tpu as pltpu
 from jax.sharding import PartitionSpec as P
 
 ITERS = 4
@@ -60,27 +62,51 @@
     return lax.pad(kept, jnp.zeros((), value.dtype), config)
 
 
+def march_kernel(drive_ref, source_ref, density_ref, inverse_ref, step_ref, final_ref, sense_ref, history_ref):
+    runs, waves, rows, cols = source_ref.shape
+    row_id = lax.broadcasted_iota(jnp.int32, (rows, cols), 0)
+    col_id = lax.broadcasted_iota(jnp.int32, (rows, cols), 1)
+    sense_ref[...] = jnp.zeros((rows, cols), jnp.float32)
+    for wave in range(waves):
+        for run in range(runs):
+            field_e = jnp.zeros((rows, cols), jnp.float32)
+            field_hx = jnp.zeros((rows, cols), jnp.float32)
+            field_hy = jnp.zeros((rows, cols), jnp.float32)
+            current = jnp.zeros((rows, cols), jnp.float32)
+            for turn in range(ITERS):
+                e_up = jnp.where(row_id < rows - 1, pltpu.roll(field_e, rows - 1, 0), 0.0)
+                e_right = jnp.where(col_id < cols - 1, pltpu.roll(field_e, cols - 1, 1), 0.0)
+                field_hx = field_hx - time_step * (e_right - field_e)
+                field_hy = field_hy + step_ref[...] * (e_up - field_e)
+                current = drude_decay * current + drude_gain * density_ref[...] * field_e
+                hy_down = jnp.where(row_id > 0, pltpu.roll(field_hy, 1, 0), 0.0)
+                hx_left = jnp.where(col_id > 0, pltpu.roll(field_hx, 1, 1), 0.0)
+                field_e = (
+                    field_e
+                    + inverse_ref[...] * (field_hy - hy_down - (field_hx - hx_left) - current)
+                    + drive_ref[turn, wave] * source_ref[run, wave]
+                )
+                if run == 0:
+                    history_ref[turn] = field_e
+                else:
+                    sense_ref[...] += field_e * history_ref[ITERS - 1 - turn]
+            if run == 0:
+                final_ref[wave] = field_e
+
+
 def march(source, drive, density_cell, inverse, hy_step):
-    field_e = jnp.zeros_like(source)
-    field_hx = jnp.zeros_like(source)
-    field_hy = jnp.zeros_like(source)
-    current = jnp.zeros_like(source)
-    history = []
-    for turn in range(ITERS):
-        e_up = shifted_in(field_e, 2, -1)
-        e_right = shifted_in(field_e, 3, -1)
-        field_hx = field_hx - time_step * (e_right - field_e)
-        field_hy = field_hy + hy_step * (e_up - field_e)
-        current = drude_decay * current + drude_gain * density_cell * field_e
-        hy_down = shifted_in(field_hy, 2, 1)
-        hx_left = shifted_in(field_hx, 3, 1)
-        field_e = (
-            field_e
-            + inverse * (field_hy - hy_down - (field_hx - hx_left) - current)
-            + drive[turn] * source
-        )
-        history.append(field_e)
-    return history
+    runs, waves, rows, cols = source.shape
+    vmem = pltpu.MemorySpace.VMEM
+    return pl.pallas_call(
+        march_kernel,
+        out_shape=(
+            jax.ShapeDtypeStruct((waves, rows, cols), jnp.float32),
+            jax.ShapeDtypeStruct((rows, cols), jnp.float32),
+        ),
+        in_specs=[pl.BlockSpec(memory_space=pltpu.MemorySpace.SMEM)] + [pl.BlockSpec(memory_space=vmem)] * 4,
+        out_specs=(pl.BlockSpec(memory_space=vmem), pl.BlockSpec(memory_space=vmem)),
+        scratch_shapes=[pltpu.VMEM((ITERS, rows, cols), jnp.float32)],
+    )(drive, source, density_cell, inverse, hy_step)
 
 
 def shards(density, foot_index, foot_weight, source_fwd, source_adj, omega):
@@ -119,12 +145,9 @@
     global_row = lax.axis_index("tile") * cells_x - HALO + lax.broadcasted_iota(jnp.int32, (rows_ext, 1), 0)
     valid = (global_row >= 0) & (global_row < cells_x * lax.axis_size("tile"))
     inverse_ext = jnp.where(valid, time_step / (1.0 + high_contrast * density_ext), 0.0)
-    hy_step = jnp.where(valid, time_step, 0.0)
-    drive = [jnp.sin(omega * (turn + 1.0))[None, :, None, None] for turn in range(ITERS)]
-    history = march(sources_ext, drive, density_ext, inverse_ext, hy_step)
-    sense = jnp.zeros((rows_ext, cells_y), jnp.float32)
-    for turn in range(ITERS):
-        sense = sense + jnp.sum(history[turn][1] * history[ITERS - 1 - turn][0], axis=0)
+    hy_step = jnp.broadcast_to(jnp.where(valid, time_step, 0.0), (rows_ext, cells_y))
+    drive = jnp.stack([jnp.sin(omega * (turn + 1.0)) for turn in range(ITERS)])
+    final, sense = march(sources_ext, drive, density_ext, inverse_ext, hy_step)
     total_waves = source_fwd.shape[0] * lax.axis_size("wl")
     scaled = high_contrast / total_waves * sense[HALO : HALO + cells_x]
     per_col = jnp.sum(matched * scaled[None], axis=1)
@@ -143,7 +166,7 @@
         pooled.reshape(count, chunks // count, block_rows, span).transpose(0, 2, 1, 3).reshape(count, block_rows, -1),
         "wl", 0, 0, tiled=True,
     ).sum(axis=0)
-    return (history[ITERS - 1][0, :, HALO : HALO + cells_x], density_grad)
+    return (final[:, HALO : HALO + cells_x], density_grad)
 
 
 def solution(mesh):

time: 55.1 us -> 59.1 us (1.073)
  the two profiles are of different devices: /device:TPU:32 before, /device:TPU:25 now
where the time goes in v5:
time: 59.1 us; the launch traced here: 58.7 us
  starting transfers between devices  27.7 us (47%)
  waiting for transfers between devices  11 us (19%)
  other arithmetic  8.06 us (14%)
  Pallas kernels  5.5 us (9%)
  local copies, waits for them, and re-layouts  5.05 us (9%)
  between operations  0.94 us (2%)
    ppermute x4, starting transfers between devices, from_behind(): lax.ppermute(value, axis, [(source, source + steps) for source in range(f...  12.9 us
    all_to_all x1, starting transfers between devices, shards(): lax.all_to_all(pooled.reshape(count, chunks // count, block_rows, span).t...  7.53 us
    all_to_all x1, starting transfers between devices, gather_columns(): pieces = lax.all_to_all(copies, axis, 0, 0, tiled=True)  7.33 us
    all_to_all x1, waiting for transfers between devices, shards(): lax.all_to_all(pooled.reshape(count, chunks // count, block_rows, span).t...  5.64 us
    pallas_call x1, Pallas kernels, march(): pl.pallas_call(march_kernel, out_shape=(jax.ShapeDtypeStruct((waves, rows...  5.5 us
    ppermute x4, waiting for transfers between devices, from_behind(): lax.ppermute(value, axis, [(source, source + steps) for source in range(f...  5.4 us
    another operation x1, other arithmetic, shards(): sources = jnp.stack([source_fwd, source_adj])  1.35 us
    broadcast_in_dim x1, local copies, waits for them, and re-layouts, gather_columns(): copies = jnp.broadcast_to(value[None], (count,) + value.shape)  1.34 us
  transfers between devices with their start and end apart: 6, of which 2 were waited for; matrix products, arithmetic and copies ran while one was open for 10% of the time, Pallas kernels for 0%

profile of v5, /device:TPU:25, one launch (start us, length us, event | category | flops | bytes accessed | tf_op | source)
XLA Modules:
  0.0 58.7 jit_solution(9946223571819921663)
XLA Ops:
  0.6 1.3 %broadcast_in_dim.84 = f32[8,2,128]{2,1,0:T(2,128)} broadcast(f32[2,128]{1,0:T(2,128)} %param.6), dimensions={1,2} | broadcast | bytes 9216 | tf_op jit(solution)/shard_map/broadcast_in_dim | solution.py:33
  2.0 7.3 %all-to-all-start = ((f32[8,2,128]{2,1,0:T(2,128)}), f32[8,2,128]{2,1,0:T(2,128)S(1)}, u32[]{:S(2)}, u32[]{:S(2)}) async-start(f32[8,2,128]{2,1,0:T(2,128)} %broadcast_in_dim.84), calls=%async_computation | async-start | bytes 16384 | tf_op jit(solution)/shard_map/all_to_all | solution.py:34
  9.3 1.3 %fusion.10 = (f32[2,2,4,4096]{3,2,1,0:T(4,128)S(1)}, f32[2,2,4,4096]{3,2,1,0:T(4,128)S(1)}) fusion(f32[1,2,8,4096]{3,2,1,0:T(8,128)} %bitcast.67, f32[1,2,8,4096]{3,2,1,0:T(8,128)} %bitcast.69), kind=kLoop, calls=%fused_computation.29 | loop fusion | flops 131072 | bytes 1048576 | tf_op jit(solution)/shard_map/stack | solution.py:113
  10.7 3.3 %collective-permute-start = (f32[2,2,4,4096]{3,2,1,0:T(4,128)S(1)}, f32[2,2,4,4096]{3,2,1,0:T(4,128)S(1)}, u32[]{:S(2)}, u32[]{:S(2)}) collective-permute-start(f32[2,2,4,4096]{3,2,1,0:T(4,128)S(1)} %get-tuple-element.18), channel_id=1, source_target_pairs={{0,1},{1,2},{2,3},{3,4},{4,5},{5,6},{6,7},{7,8},{8,9},{9,10},{10,1... | collective-permute-start | bytes 786440 | tf_op jit(solution)/shard_map/ppermute | solution.py:22
  14.0 1.9 %collective-permute-start.1 = (f32[2,2,4,4096]{3,2,1,0:T(4,128)S(1)}, f32[2,2,4,4096]{3,2,1,0:T(4,128)S(1)}, u32[]{:S(2)}, u32[]{:S(2)}) collective-permute-start(f32[2,2,4,4096]{3,2,1,0:T(4,128)S(1)} %get-tuple-element.19), channel_id=1, source_target_pairs={{1,0},{2,1},{3,2},{4,3},{5,4},{6,5},{7,6},{8,7},{9,8},{10,9},{11,1... | collective-permute-start | bytes 786440 | tf_op jit(solution)/shard_map/ppermute | solution.py:22
  15.9 0.5 fusion.2
  16.6 0.5 copy-done.6
  17.2 0.6 %pad_maximum_fusion.2.drive_ref = f32[4,2]{1,0:T(4,128)} fusion(f32[1,2]{1,0:T(1,128)S(1)} %get-tuple-element.39, f32[1,2]{1,0:T(1,128)S(1)} %get-tuple-element.40, f32[1,2]{1,0:T(1,128)S(1)} %get-tuple-element.38, f32[1,2]{1,0:T(1,128)S(1)} %get-tuple-element.37), kind=kLoop, calls=%fused_computation.85 | loop fusion | flops 24 | bytes 64 | tf_op jit(solution)/shard_map/stack | solution.py:149
  17.8 0.1 pad_slice_fusion.12
  17.9 0.1 pad_slice_fusion.8
  18.0 0.1 stack.69
  18.1 0.2 fusion.12
  18.4 0.6 multiply_reduce_fusion.1
  18.9 0.4 fusion.8
  19.4 5.7 %collective-permute-start.2 = (f32[2,4096]{1,0:T(2,128)S(1)}, f32[2,4096]{1,0:T(2,128)S(1)}, u32[]{:S(2)}, u32[]{:S(2)}) collective-permute-start(f32[2,4096]{1,0:T(2,128)S(1)} %get-tuple-element.7), channel_id=1, source_target_pairs={{0,1},{1,2},{2,3},{3,4},{4,5},{5,6},{6,7},{7,8},{8,9},{9,10},{10,1... | collective-permute-start | bytes 98312 | tf_op jit(solution)/shard_map/ppermute | solution.py:22
  25.1 1.9 %collective-permute-start.3 = (f32[2,4096]{1,0:T(2,128)S(1)}, f32[2,4096]{1,0:T(2,128)S(1)}, u32[]{:S(2)}, u32[]{:S(2)}) collective-permute-start(f32[2,4096]{1,0:T(2,128)S(1)} %get-tuple-element.6), channel_id=1, source_target_pairs={{1,0},{2,1},{3,2},{4,3},{5,4},{6,5},{7,6},{8,7},{9,8},{10,9},{11,1... | collective-permute-start | bytes 98312 | tf_op jit(solution)/shard_map/ppermute | solution.py:22
  27.1 5.4 %collective-permute-done.3 = f32[2,4096]{1,0:T(2,128)S(1)} collective-permute-done((f32[2,4096]{1,0:T(2,128)S(1)}, f32[2,4096]{1,0:T(2,128)S(1)}, u32[]{:S(2)}, u32[]{:S(2)}) %collective-permute-start.3) | collective-permute-done | bytes 32800 | tf_op jit(solution)/shard_map/ppermute | solution.py:22
  32.5 0.3 concatenate.7.density_ref
  32.8 0.8 %divide_select_fusion.inverse_ref = f32[16,4096]{1,0:T(8,128)} fusion(f32[16,4096]{1,0:T(8,128)S(1)} %concatenate.7.density_ref, pred[16]{0:T(512)(128)(4,1)S(1)} %compare_and_fusion), kind=kLoop, calls=%fused_computation.31 | loop fusion | flops 262144 | bytes 524304 | tf_op jit(solution)/shard_map/jit(_where)/select_n | solution.py:147
  33.6 1.2 %pad_maximum_fusion.source_ref = f32[2,2,16,4096]{3,2,1,0:T(8,128)} fusion(f32[2,2,4,4096]{3,2,1,0:T(4,128)S(1)} %collective-permute-done.1, f32[1,2,8,4096]{3,2,1,0:T(8,128)S(1)} %bitcast.70, f32[1,2,8,4096]{3,2,1,0:T(8,128)S(1)} %bitcast.68, f32[2,2,4,4096]{3,2,1,0:T(4,128)S(1)} %collective-permute-done), kind=kLoop, calls=%fused_computation.8 | loop fusion | flops 786432 | bytes 2097152 | tf_op jit(solution)/shard_map/concatenate | solution.py:28
  34.8 0.8 %broadcast_in_dim.89.step_ref = f32[16,4096]{1,0:T(8,128)} broadcast(f32[16]{0:T(128)S(1)} %broadcast_select_fusion), dimensions={0} | broadcast | bytes 262208 | tf_op jit(solution)/shard_map/broadcast_in_dim | solution.py:148
  35.6 5.5 %shard_map.77 = (f32[2,16,4096]{2,1,0:T(8,128)}, f32[16,4096]{1,0:T(8,128)}) custom-call(f32[4,2]{1,0:T(4,128)} %pad_maximum_fusion.2.drive_ref, f32[2,2,16,4096]{3,2,1,0:T(8,128)} %pad_maximum_fusion.source_ref, f32[16,4096]{1,0:T(8,128)} %copy-done, f32[16,4096]{1,0:T(8,128)} %divide_select_fusion.inverse_ref, f32[16,4096]{1,0:T(8,128)} %broadcast_in_dim.89.step_ref), custom_call_target="tpu_custom_call" | custom-call | tf_op jit(solution)/shard_map/pallas_call | solution.py:100
  41.1 1.0 %slice_multiply_fusion.2 = f32[8,4096]{1,0:T(8,128)S(1)} fusion(f32[16,4096]{1,0:T(8,128)} %get-tuple-element.5), kind=kLoop, calls=%fused_computation.43 | loop fusion | flops 32768 | bytes 262144 | tf_op jit(solution)/shard_map/mul | solution.py:152
  42.1 0.8 %multiply_reduce_fusion = f32[10,4096]{1,0:T(8,128)S(1)} fusion(f32[8,4096]{1,0:T(8,128)S(1)} %slice_multiply_fusion.2, f32[8,4096]{1,0:T(8,128)S(1)} %get-tuple-element.15, s32[8,4096]{1,0:T(8,128)S(1)} %get-tuple-element.11, f32[8,4096]{1,0:T(8,128)S(1)} %get-tuple-element.16, s32[8,4096]{1,0:T(8,128)S(1)} %get-tuple-element.12, ...), kind=kLoop, calls=%fused_computation | loop fusion | flops 4218880 | bytes 1343488 | tf_op jit(solution)/shard_map/reduce_sum | solution.py:153
  42.9 0.1 fusion.32
  43.2 0.2 fusion.23
  43.4 0.2 convolution_bitcast_fusion
  43.6 0.7 %copy.21 = f32[8,2,128]{2,1,0:T(2,128)} copy(f32[8,2,128]{2,0,1:T(8,128)S(1)} %convolution_bitcast_fusion) | data formatting | bytes 16384 | tf_op jit(solution)/shard_map/rky,cy->krc/transpose | solution.py:159
  44.2 7.5 %all-to-all-start.1 = ((f32[8,2,128]{2,1,0:T(2,128)}), f32[8,2,128]{2,1,0:T(2,128)S(1)}, u32[]{:S(2)}, u32[]{:S(2)}) async-start(f32[8,2,128]{2,1,0:T(2,128)} %copy.21), calls=%async_computation.1 | async-start | bytes 16384 | tf_op jit(solution)/shard_map/all_to_all | solution.py:165
  51.8 0.7 %slice.137 = f32[2,8,4096]{2,1,0:T(8,128)} slice(f32[2,16,4096]{2,1,0:T(8,128)S(1)} %copy-done.5), slice={[0:2], [4:12], [0:4096]} | slice | bytes 524288 | tf_op jit(solution)/shard_map/slice | solution.py:169
  52.5 5.6 %all-to-all-done.1 = f32[8,2,128]{2,1,0:T(2,128)S(1)} async-done(((f32[8,2,128]{2,1,0:T(2,128)}), f32[8,2,128]{2,1,0:T(2,128)S(1)}, u32[]{:S(2)}, u32[]{:S(2)}) %all-to-all-start.1) | async-done | bytes 8224 | tf_op jit(solution)/shard_map/all_to_all | solution.py:165
  58.2 0.6 reduce_sum.49
  (35 shorter events, 0.5 us)
Async XLA Ops:
  0.6 15.3 %copy-start.3 = (s32[4,8,4096]{2,1,0:T(8,128)S(1)}, s32[4,8,4096]{2,1,0:T(8,128)}, u32[]{:S(2)}) copy-start(s32[4,8,4096]{2,1,0:T(8,128)} %param.7) | copy-start | bytes 1572868
  2.0 15.8 %all-to-all-start = ((f32[8,2,128]{2,1,0:T(2,128)}), f32[8,2,128]{2,1,0:T(2,128)S(1)}, u32[]{:S(2)}, u32[]{:S(2)}) async-start(f32[8,2,128]{2,1,0:T(2,128)} %broadcast_in_dim.84), calls=%async_computation | async-start | bytes 16384 | tf_op jit(solution)/shard_map/all_to_all | solution.py:34
  10.7 5.9 %copy-start.4 = (bf16[4,8,4096]{2,1,0:T(8,128)(2,1)S(1)}, bf16[4,8,4096]{2,1,0:T(8,128)(2,1)}, u32[]{:S(2)}) copy-start(bf16[4,8,4096]{2,1,0:T(8,128)(2,1)} %param.8) | copy-start | bytes 786436
  10.7 22.9 %collective-permute-start = (f32[2,2,4,4096]{3,2,1,0:T(4,128)S(1)}, f32[2,2,4,4096]{3,2,1,0:T(4,128)S(1)}, u32[]{:S(2)}, u32[]{:S(2)}) collective-permute-start(f32[2,2,4,4096]{3,2,1,0:T(4,128)S(1)} %get-tuple-element.18), channel_id=1, source_target_pairs={{0,1},{1,2},{2,3},{3,4},{4,5},{5,6},{6,7},{7,8},{8,9},{9,10},{10,1... | collective-permute-start | bytes 786440 | tf_op jit(solution)/shard_map/ppermute | solution.py:22
  14.0 19.7 %collective-permute-start.1 = (f32[2,2,4,4096]{3,2,1,0:T(4,128)S(1)}, f32[2,2,4,4096]{3,2,1,0:T(4,128)S(1)}, u32[]{:S(2)}, u32[]{:S(2)}) collective-permute-start(f32[2,2,4,4096]{3,2,1,0:T(4,128)S(1)} %get-tuple-element.19), channel_id=1, source_target_pairs={{1,0},{2,1},{3,2},{4,3},{5,4},{6,5},{7,6},{8,7},{9,8},{10,9},{11,1... | collective-permute-start | bytes 786440 | tf_op jit(solution)/shard_map/ppermute | solution.py:22
  16.5 0.7 %copy-start.6 = (f32[2]{0:T(128)S(1)}, f32[2]{0:T(128)}, u32[]{:S(2)}) copy-start(f32[2]{0:T(128)} %param.11) | copy-start | bytes 28
  18.9 14.7 %copy-start.1 = (f32[2,8,4096]{2,1,0:T(8,128)S(1)}, f32[2,8,4096]{2,1,0:T(8,128)}, u32[]{:S(2)}) copy-start(f32[2,8,4096]{2,1,0:T(8,128)} %param.9) | copy-start | bytes 786436
  18.9 14.7 %copy-start.2 = (f32[2,8,4096]{2,1,0:T(8,128)S(1)}, f32[2,8,4096]{2,1,0:T(8,128)}, u32[]{:S(2)}) copy-start(f32[2,8,4096]{2,1,0:T(8,128)} %param.10) | copy-start | bytes 786436
  19.4 7.7 %collective-permute-start.2 = (f32[2,4096]{1,0:T(2,128)S(1)}, f32[2,4096]{1,0:T(2,128)S(1)}, u32[]{:S(2)}, u32[]{:S(2)}) collective-permute-start(f32[2,4096]{1,0:T(2,128)S(1)} %get-tuple-element.7), channel_id=1, source_target_pairs={{0,1},{1,2},{2,3},{3,4},{4,5},{5,6},{6,7},{7,8},{8,9},{9,10},{10,1... | collective-permute-start | bytes 98312 | tf_op jit(solution)/shard_map/ppermute | solution.py:22
  25.1 7.3 %collective-permute-start.3 = (f32[2,4096]{1,0:T(2,128)S(1)}, f32[2,4096]{1,0:T(2,128)S(1)}, u32[]{:S(2)}, u32[]{:S(2)}) collective-permute-start(f32[2,4096]{1,0:T(2,128)S(1)} %get-tuple-element.6), channel_id=1, source_target_pairs={{1,0},{2,1},{3,2},{4,3},{5,4},{6,5},{7,6},{8,7},{9,8},{10,9},{11,1... | collective-permute-start | bytes 98312 | tf_op jit(solution)/shard_map/ppermute | solution.py:22
  32.8 2.0 %copy-start = (f32[16,4096]{1,0:T(8,128)}, f32[16,4096]{1,0:T(8,128)S(1)}, u32[]{:S(2)}) copy-start(f32[16,4096]{1,0:T(8,128)S(1)} %concatenate.7.density_ref) | copy-start | bytes 786436
  42.1 9.7 %copy-start.5 = (f32[2,16,4096]{2,1,0:T(8,128)S(1)}, f32[2,16,4096]{2,1,0:T(8,128)}, u32[]{:S(2)}) copy-start(f32[2,16,4096]{2,1,0:T(8,128)} %get-tuple-element.4) | copy-start | bytes 1572868
  44.2 13.9 %all-to-all-start.1 = ((f32[8,2,128]{2,1,0:T(2,128)}), f32[8,2,128]{2,1,0:T(2,128)S(1)}, u32[]{:S(2)}, u32[]{:S(2)}) async-start(f32[8,2,128]{2,1,0:T(2,128)} %copy.21), calls=%async_computation.1 | async-start | bytes 16384 | tf_op jit(solution)/shard_map/all_to_all | solution.py:165

commit v6 on v5

--- a/solution.py
+++ b/solution.py
@@ -62,10 +62,30 @@
     return lax.pad(kept, jnp.zeros((), value.dtype), config)
 
 
-def march_kernel(drive_ref, source_ref, density_ref, inverse_ref, step_ref, final_ref, sense_ref, history_ref):
+def march_kernel(
+    bounds_ref, drive_ref, fwd_ref, adj_ref, src_above_ref, src_below_ref,
+    dens_ref, dens_above_ref, dens_below_ref, matched_ref,
+    final_ref, per_col_ref,
+    source_ref, density_ref, history_ref, sense_ref,
+):
     runs, waves, rows, cols = source_ref.shape
+    own = fwd_ref.shape[1]
+    reach = dens_above_ref.shape[0]
+    for wave in range(waves):
+        for run, own_ref in enumerate((fwd_ref, adj_ref)):
+            source_ref[run, wave, 0:HALO] = src_above_ref[run, wave]
+            source_ref[run, wave, HALO : HALO + own] = own_ref[wave]
+            source_ref[run, wave, HALO + own : rows] = src_below_ref[run, wave]
+    density_ref[...] = jnp.zeros((rows, cols), jnp.float32)
+    density_ref[HALO - reach : HALO] = dens_above_ref[...]
+    density_ref[HALO : HALO + own] = dens_ref[...]
+    density_ref[HALO + own : HALO + own + reach] = dens_below_ref[...]
     row_id = lax.broadcasted_iota(jnp.int32, (rows, cols), 0)
     col_id = lax.broadcasted_iota(jnp.int32, (rows, cols), 1)
+    valid = (row_id >= bounds_ref[0]) & (row_id < bounds_ref[1])
+    density = density_ref[...]
+    inverse = jnp.where(valid, time_step / (1.0 + high_contrast * density), 0.0)
+    hy_step = jnp.where(valid, time_step, 0.0)
     sense_ref[...] = jnp.zeros((rows, cols), jnp.float32)
     for wave in range(waves):
         for run in range(runs):
@@ -77,13 +97,13 @@
                 e_up = jnp.where(row_id < rows - 1, pltpu.roll(field_e, rows - 1, 0), 0.0)
                 e_right = jnp.where(col_id < cols - 1, pltpu.roll(field_e, cols - 1, 1), 0.0)
                 field_hx = field_hx - time_step * (e_right - field_e)
-                field_hy = field_hy + step_ref[...] * (e_up - field_e)
-                current = drude_decay * current + drude_gain * density_ref[...] * field_e
+                field_hy = field_hy + hy_step * (e_up - field_e)
+                current = drude_decay * current + drude_gain * density * field_e
                 hy_down = jnp.where(row_id > 0, pltpu.roll(field_hy, 1, 0), 0.0)
                 hx_left = jnp.where(col_id > 0, pltpu.roll(field_hx, 1, 1), 0.0)
                 field_e = (
                     field_e
-                    + inverse_ref[...] * (field_hy - hy_down - (field_hx - hx_left) - current)
+                    + inverse * (field_hy - hy_down - (field_hx - hx_left) - current)
                     + drive_ref[turn, wave] * source_ref[run, wave]
                 )
                 if run == 0:
@@ -92,26 +112,37 @@
                     sense_ref[...] += field_e * history_ref[ITERS - 1 - turn]
             if run == 0:
                 final_ref[wave] = field_e
-
-
-def march(source, drive, density_cell, inverse, hy_step):
-    runs, waves, rows, cols = source.shape
+    scaled = drive_ref[ITERS, 0] * sense_ref[HALO : HALO + own]
+    for code in range(matched_ref.shape[0]):
+        per_col_ref[code : code + 1] = jnp.sum(matched_ref[code] * scaled, axis=0, keepdims=True)
+
+
+def march(bounds, drive, fwd, adj, src_above, src_below, dens, dens_above, dens_below, matched):
+    runs, waves, _, cols = src_above.shape
+    rows = fwd.shape[1] + 2 * HALO
     vmem = pltpu.MemorySpace.VMEM
+    smem = pltpu.MemorySpace.SMEM
     return pl.pallas_call(
         march_kernel,
         out_shape=(
             jax.ShapeDtypeStruct((waves, rows, cols), jnp.float32),
-            jax.ShapeDtypeStruct((rows, cols), jnp.float32),
+            jax.ShapeDtypeStruct((matched.shape[0], cols), jnp.float32),
         ),
-        in_specs=[pl.BlockSpec(memory_space=pltpu.MemorySpace.SMEM)] + [pl.BlockSpec(memory_space=vmem)] * 4,
+        in_specs=[pl.BlockSpec(memory_space=smem)] * 2 + [pl.BlockSpec(memory_space=vmem)] * 8,
         out_specs=(pl.BlockSpec(memory_space=vmem), pl.BlockSpec(memory_space=vmem)),
-        scratch_shapes=[pltpu.VMEM((ITERS, rows, cols), jnp.float32)],
-    )(drive, source, density_cell, inverse, hy_step)
+        scratch_shapes=[
+            pltpu.VMEM((runs, waves, rows, cols), jnp.float32),
+            pltpu.VMEM((rows, cols), jnp.float32),
+            pltpu.VMEM((ITERS, rows, cols), jnp.float32),
+            pltpu.VMEM((rows, cols), jnp.float32),
+        ],
+    )(bounds, drive, fwd, adj, src_above, src_below, dens, dens_above, dens_below, matched)
 
 
 def shards(density, foot_index, foot_weight, source_fwd, source_adj, omega):
     sources = jnp.stack([source_fwd, source_adj])
-    sources_ext = with_halo(sources, "tile")
+    src_above = from_behind(sources[:, :, -HALO:], "tile", 1)
+    src_below = from_behind(sources[:, :, :HALO], "tile", -1)
     strip = gather_columns(density, "wl")
     block_rows, block_cols = strip.shape
     cells_x, cells_y = foot_index.shape[1:]
@@ -139,18 +170,17 @@
     above = from_behind(last_rows, "tile", 1)
     below = from_behind(first_rows, "tile", -1)
     density_cell = jnp.sum(matched * candidates[:, None, :], axis=0)
-    pad = jnp.zeros((HALO - reach, cells_y), jnp.float32)
-    density_ext = jnp.concatenate([pad, above, density_cell, below, pad], axis=0)
     rows_ext = cells_x + 2 * HALO
-    global_row = lax.axis_index("tile") * cells_x - HALO + lax.broadcasted_iota(jnp.int32, (rows_ext, 1), 0)
-    valid = (global_row >= 0) & (global_row < cells_x * lax.axis_size("tile"))
-    inverse_ext = jnp.where(valid, time_step / (1.0 + high_contrast * density_ext), 0.0)
-    hy_step = jnp.broadcast_to(jnp.where(valid, time_step, 0.0), (rows_ext, cells_y))
-    drive = jnp.stack([jnp.sin(omega * (turn + 1.0)) for turn in range(ITERS)])
-    final, sense = march(sources_ext, drive, density_ext, inverse_ext, hy_step)
+    first = HALO - lax.axis_index("tile") * cells_x
+    bounds = jnp.stack([first, first + cells_x * lax.axis_size("tile")]).astype(jnp.int32)
     total_waves = source_fwd.shape[0] * lax.axis_size("wl")
-    scaled = high_contrast / total_waves * sense[HALO : HALO + cells_x]
-    per_col = jnp.sum(matched * scaled[None], axis=1)
+    drive = jnp.concatenate(
+        [jnp.stack([jnp.sin(omega * (turn + 1.0)) for turn in range(ITERS)]),
+         jnp.full((1, omega.shape[0]), high_contrast / total_waves, jnp.float32)]
+    )
+    final, per_col = march(
+        bounds, drive, source_fwd, source_adj, src_above, src_below, density_cell, above, below, matched
+    )
     per_col = per_col.reshape(block_rows, len(SHIFTS), cells_y)
     gathered = jnp.zeros((block_rows, cells_y), jnp.float32)
     for slot, shift in enumerate(SHIFTS):

time: 59.1 us -> 57.6 us (0.975)
  the two profiles are of different devices: /device:TPU:25 before, /device:TPU:32 now
where the time goes in v6:
time: 57.6 us; the launch traced here: 57.2 us
  starting transfers between devices  27.3 us (47%)
  waiting for transfers between devices  11.2 us (19%)
  Pallas kernels  6.18 us (11%)
  local copies, waits for them, and re-layouts  5.68 us (10%)
  other arithmetic  5.58 us (10%)
  between operations  0.87 us (2%)
    ppermute x4, starting transfers between devices, from_behind(): lax.ppermute(value, axis, [(source, source + steps) for source in range(f...  14.3 us
    all_to_all x1, waiting for transfers between devices, shards(): lax.all_to_all(pooled.reshape(count, chunks // count, block_rows, span).t...  6.94 us
    all_to_all x1, starting transfers between devices, gather_columns(): pieces = lax.all_to_all(copies, axis, 0, 0, tiled=True)  6.71 us
    all_to_all x1, starting transfers between devices, shards(): lax.all_to_all(pooled.reshape(count, chunks // count, block_rows, span).t...  6.32 us
    pallas_call x1, Pallas kernels, march(): pl.pallas_call(march_kernel, out_shape=(jax.ShapeDtypeStruct((waves, rows...  6.18 us
    ppermute x4, waiting for transfers between devices, from_behind(): lax.ppermute(value, axis, [(source, source + steps) for source in range(f...  4.23 us
    another operation x1, other arithmetic, shards(): sources = jnp.stack([source_fwd, source_adj])  1.35 us
    broadcast_in_dim x1, local copies, waits for them, and re-layouts, gather_columns(): copies = jnp.broadcast_to(value[None], (count,) + value.shape)  1.34 us
  transfers between devices with their start and end apart: 6, of which 2 were waited for; matrix products, arithmetic and copies ran while one was open for 12% of the time, Pallas kernels for 0%

profile of v6, /device:TPU:32, one launch (start us, length us, event | category | flops | bytes accessed | tf_op | source)
XLA Modules:
  0.0 57.2 jit_solution(5625492462181619133)
XLA Ops:
  0.6 1.3 %broadcast_in_dim.54 = f32[8,2,128]{2,1,0:T(2,128)} broadcast(f32[2,128]{1,0:T(2,128)} %param.6), dimensions={1,2} | broadcast | bytes 9216 | tf_op jit(solution)/shard_map/broadcast_in_dim | solution.py:33
  2.0 6.7 %all-to-all-start = ((f32[8,2,128]{2,1,0:T(2,128)}), f32[8,2,128]{2,1,0:T(2,128)S(1)}, u32[]{:S(2)}, u32[]{:S(2)}) async-start(f32[8,2,128]{2,1,0:T(2,128)} %broadcast_in_dim.54), calls=%async_computation | async-start | bytes 16384 | tf_op jit(solution)/shard_map/all_to_all | solution.py:34
  8.7 1.3 %pad_maximum_fusion = (f32[2,2,4,4096]{3,2,1,0:T(4,128)S(1)}, f32[2,2,4,4096]{3,2,1,0:T(4,128)S(1)}) fusion(f32[1,2,8,4096]{3,2,1,0:T(8,128)} %bitcast.70, f32[1,2,8,4096]{3,2,1,0:T(8,128)} %bitcast.69), kind=kLoop, calls=%fused_computation.28 | loop fusion | flops 131072 | bytes 1048576 | tf_op jit(solution)/shard_map/stack | solution.py:143
  10.0 0.0 copy-start.2
  10.1 4.7 %collective-permute-start.1 = (f32[2,2,4,4096]{3,2,1,0:T(4,128)S(1)}, f32[2,2,4,4096]{3,2,1,0:T(4,128)S(1)}, u32[]{:S(2)}, u32[]{:S(2)}) collective-permute-start(f32[2,2,4,4096]{3,2,1,0:T(4,128)S(1)} %get-tuple-element.18), channel_id=1, source_target_pairs={{1,0},{2,1},{3,2},{4,3},{5,4},{6,5},{7,6},{8,7},{9,8},{10,9},{11,1... | collective-permute-start | bytes 786440 | tf_op jit(solution)/shard_map/ppermute | solution.py:22
  14.7 1.9 %collective-permute-start = (f32[2,2,4,4096]{3,2,1,0:T(4,128)S(1)}, f32[2,2,4,4096]{3,2,1,0:T(4,128)}, u32[]{:S(2)}, u32[]{:S(2)}) collective-permute-start(f32[2,2,4,4096]{3,2,1,0:T(4,128)S(1)} %get-tuple-element.19), channel_id=1, source_target_pairs={{0,1},{1,2},{2,3},{3,4},{4,5},{5,6},{6,7},{7,8},{8,9},{9,10},{10,1... | collective-permute-start | bytes 786440 | tf_op jit(solution)/shard_map/ppermute | solution.py:22
  16.7 0.7 %sine_bitcast_fusion = (f32[1,2]{1,0:T(1,128)S(1)}, f32[1,2]{1,0:T(1,128)S(1)}, f32[1,2]{1,0:T(1,128)S(1)}, f32[1,2]{1,0:T(1,128)S(1)}) fusion(f32[2]{0:T(128)} %param.11), kind=kLoop, calls=%fused_computation.84 | loop fusion | flops 6 | bytes 40 | tf_op jit(solution)/shard_map/stack | solution.py:178
  17.4 0.5 fusion.2
  18.1 0.1 pad_slice_fusion.8
  18.2 0.1 pad_slice_fusion.12
  18.3 0.1 stack.77
  18.4 0.2 fusion.12
  18.7 1.2 %select_add_fusion = (f32[10,8,4096]{2,1,0:T(8,128)S(1)}, f32[8,4096]{1,0:T(8,128)}) fusion(f32[8,4096]{1,0:T(8,128)S(1)} %get-tuple-element.15, s32[8,4096]{1,0:T(8,128)S(1)} %get-tuple-element.11, f32[8,4096]{1,0:T(8,128)S(1)} %get-tuple-element.16, s32[8,4096]{1,0:T(8,128)S(1)} %get-tuple-element.12, f32[8,4096]{1,0:T(8,128)S(1)} %get-tuple-element.17, ...), kind=kLoop, calls=%fused_computation.1 | loop fusion | flops 4227072 | bytes 2654208 | tf_op jit(solution)/shard_map/add | solution.py:156
  19.9 0.4 fusion.8
  20.3 5.8 %collective-permute-start.3 = (f32[2,4096]{1,0:T(2,128)S(1)}, f32[2,4096]{1,0:T(2,128)S(1)}, u32[]{:S(2)}, u32[]{:S(2)}) collective-permute-start(f32[2,4096]{1,0:T(2,128)S(1)} %get-tuple-element.6), channel_id=1, source_target_pairs={{1,0},{2,1},{3,2},{4,3},{5,4},{6,5},{7,6},{8,7},{9,8},{10,9},{11,1... | collective-permute-start | bytes 98312 | tf_op jit(solution)/shard_map/ppermute | solution.py:22
  26.0 1.9 %collective-permute-start.2 = (f32[2,4096]{1,0:T(2,128)S(1)}, f32[2,4096]{1,0:T(2,128)S(1)}, u32[]{:S(2)}, u32[]{:S(2)}) collective-permute-start(f32[2,4096]{1,0:T(2,128)S(1)} %get-tuple-element.7), channel_id=1, source_target_pairs={{0,1},{1,2},{2,3},{3,4},{4,5},{5,6},{6,7},{7,8},{8,9},{9,10},{10,1... | collective-permute-start | bytes 98312 | tf_op jit(solution)/shard_map/ppermute | solution.py:22
  28.0 0.6 %pad_add_fusion.bounds_ref = s32[2]{0:T(128)} fusion(s32[1]{0:T(128)} %bitcast.1, s32[1]{0:T(128)} %bitcast), kind=kLoop, calls=%fused_computation.83 | loop fusion | flops 2 | bytes 16 | tf_op jit(solution)/shard_map/stack | solution.py:175
  28.5 0.6 %concatenate.3.drive_ref = f32[5,2]{1,0:T(8,128)} concatenate(f32[1,2]{1,0:T(1,128)S(1)} %get-tuple-element.39, f32[1,2]{1,0:T(1,128)S(1)} %get-tuple-element.38, f32[1,2]{1,0:T(1,128)S(1)} %get-tuple-element.40, f32[1,2]{1,0:T(1,128)S(1)} %get-tuple-element.37, f32[1,2]{1,0:T(1,128)S(1)} %broadcast.108), dimensions={0} | concatenate | bytes 80 | tf_op jit(solution)/shard_map/concatenate | solution.py:177
  29.1 4.2 %collective-permute-done.2.dens_above_ref = f32[2,4096]{1,0:T(2,128)S(1)} collective-permute-done((f32[2,4096]{1,0:T(2,128)S(1)}, f32[2,4096]{1,0:T(2,128)S(1)}, u32[]{:S(2)}, u32[]{:S(2)}) %collective-permute-start.2) | collective-permute-done | bytes 32800 | tf_op jit(solution)/shard_map/ppermute | solution.py:22
  33.4 0.0 collective-permute-done.1.src_below_ref
  33.4 0.6 copy-done.6
  34.0 0.1 copy-done.3
  34.1 6.2 %shard_map.77 = (f32[2,16,4096]{2,1,0:T(8,128)}, f32[10,4096]{1,0:T(8,128)}) custom-call(s32[2]{0:T(128)} %pad_add_fusion.bounds_ref, f32[5,2]{1,0:T(8,128)} %concatenate.3.drive_ref, f32[2,8,4096]{2,1,0:T(8,128)} %fwd_ref.1, f32[2,8,4096]{2,1,0:T(8,128)} %adj_ref.1, f32[2,2,4,4096]{3,2,1,0:T(4,128)} %collective-permute-done.src_above_ref, ...), custom_call_target="tpu_custom_call" | custom-call | tf_op jit(solution)/shard_map/pallas_call | solution.py:125
  40.3 1.0 %reshape.59 = f32[2,5,4096]{2,1,0:T(8,128)S(1)} reshape(f32[10,4096]{1,0:T(8,128)} %get-tuple-element.5) | data formatting | bytes 327680 | tf_op jit(solution)/shard_map/reshape | solution.py:184
  41.3 0.1 fusion.32
  41.6 0.2 fusion.23
  41.8 0.2 convolution_bitcast_fusion
  41.9 0.7 %copy.30 = f32[8,2,128]{2,1,0:T(2,128)} copy(f32[8,2,128]{2,0,1:T(8,128)S(1)} %convolution_bitcast_fusion) | data formatting | bytes 16384 | tf_op jit(solution)/shard_map/rky,cy->krc/transpose | solution.py:189
  42.6 6.3 %all-to-all-start.1 = ((f32[8,2,128]{2,1,0:T(2,128)}), f32[8,2,128]{2,1,0:T(2,128)S(1)}, u32[]{:S(2)}, u32[]{:S(2)}) async-start(f32[8,2,128]{2,1,0:T(2,128)} %copy.30), calls=%async_computation.1 | async-start | bytes 16384 | tf_op jit(solution)/shard_map/all_to_all | solution.py:195
  48.9 0.7 %slice.134 = f32[2,8,4096]{2,1,0:T(8,128)} slice(f32[2,16,4096]{2,1,0:T(8,128)S(1)} %copy-done.4), slice={[0:2], [4:12], [0:4096]} | slice | bytes 524288 | tf_op jit(solution)/shard_map/slice | solution.py:199
  49.7 6.9 %all-to-all-done.1 = f32[8,2,128]{2,1,0:T(2,128)S(1)} async-done(((f32[8,2,128]{2,1,0:T(2,128)}), f32[8,2,128]{2,1,0:T(2,128)S(1)}, u32[]{:S(2)}, u32[]{:S(2)}) %all-to-all-start.1) | async-done | bytes 8224 | tf_op jit(solution)/shard_map/all_to_all | solution.py:195
  56.6 0.6 %reduce_sum.39 = f32[2,128]{1,0:T(2,128)} reduce(f32[8,2,128]{2,1,0:T(2,128)S(1)} %all-to-all-done.1, f32[]{:T(128)} %constant.80.clone.1), dimensions={0}, to_apply=%region_3.4 | reduce | flops 1792 | bytes 9220 | tf_op jit(solution)/shard_map/reduce_sum | solution.py:198
  (28 shorter events, 0.3 us)
Async XLA Ops:
  0.6 16.8 %copy-start.1 = (s32[4,8,4096]{2,1,0:T(8,128)S(1)}, s32[4,8,4096]{2,1,0:T(8,128)}, u32[]{:S(2)}) copy-start(s32[4,8,4096]{2,1,0:T(8,128)} %param.7) | copy-start | bytes 1572868
  2.0 16.1 %all-to-all-start = ((f32[8,2,128]{2,1,0:T(2,128)}), f32[8,2,128]{2,1,0:T(2,128)S(1)}, u32[]{:S(2)}, u32[]{:S(2)}) async-start(f32[8,2,128]{2,1,0:T(2,128)} %broadcast_in_dim.54), calls=%async_computation | async-start | bytes 16384 | tf_op jit(solution)/shard_map/all_to_all | solution.py:34
  10.0 7.9 %copy-start.2 = (bf16[4,8,4096]{2,1,0:T(8,128)(2,1)S(1)}, bf16[4,8,4096]{2,1,0:T(8,128)(2,1)}, u32[]{:S(2)}) copy-start(bf16[4,8,4096]{2,1,0:T(8,128)(2,1)} %param.8) | copy-start | bytes 786436
  10.1 23.3 %collective-permute-start.1 = (f32[2,2,4,4096]{3,2,1,0:T(4,128)S(1)}, f32[2,2,4,4096]{3,2,1,0:T(4,128)S(1)}, u32[]{:S(2)}, u32[]{:S(2)}) collective-permute-start(f32[2,2,4,4096]{3,2,1,0:T(4,128)S(1)} %get-tuple-element.18), channel_id=1, source_target_pairs={{1,0},{2,1},{3,2},{4,3},{5,4},{6,5},{7,6},{8,7},{9,8},{10,9},{11,1... | collective-permute-start | bytes 786440 | tf_op jit(solution)/shard_map/ppermute | solution.py:22
  14.7 18.7 %collective-permute-start = (f32[2,2,4,4096]{3,2,1,0:T(4,128)S(1)}, f32[2,2,4,4096]{3,2,1,0:T(4,128)}, u32[]{:S(2)}, u32[]{:S(2)}) collective-permute-start(f32[2,2,4,4096]{3,2,1,0:T(4,128)S(1)} %get-tuple-element.19), channel_id=1, source_target_pairs={{0,1},{1,2},{2,3},{3,4},{4,5},{5,6},{6,7},{7,8},{8,9},{9,10},{10,1... | collective-permute-start | bytes 786440 | tf_op jit(solution)/shard_map/ppermute | solution.py:22
  19.9 13.5 %copy-start = (f32[10,8,4096]{2,1,0:T(8,128)}, f32[10,8,4096]{2,1,0:T(8,128)S(1)}, u32[]{:S(2)}) copy-start(f32[10,8,4096]{2,1,0:T(8,128)S(1)} %get-tuple-element.8.matched_ref) | copy-start | bytes 3932164
  20.3 8.9 %collective-permute-start.3 = (f32[2,4096]{1,0:T(2,128)S(1)}, f32[2,4096]{1,0:T(2,128)S(1)}, u32[]{:S(2)}, u32[]{:S(2)}) collective-permute-start(f32[2,4096]{1,0:T(2,128)S(1)} %get-tuple-element.6), channel_id=1, source_target_pairs={{1,0},{2,1},{3,2},{4,3},{5,4},{6,5},{7,6},{8,7},{9,8},{10,9},{11,1... | collective-permute-start | bytes 98312 | tf_op jit(solution)/shard_map/ppermute | solution.py:22
  26.0 7.3 %collective-permute-start.2 = (f32[2,4096]{1,0:T(2,128)S(1)}, f32[2,4096]{1,0:T(2,128)S(1)}, u32[]{:S(2)}, u32[]{:S(2)}) collective-permute-start(f32[2,4096]{1,0:T(2,128)S(1)} %get-tuple-element.7), channel_id=1, source_target_pairs={{0,1},{1,2},{2,3},{3,4},{4,5},{5,6},{6,7},{7,8},{8,9},{9,10},{10,1... | collective-permute-start | bytes 98312 | tf_op jit(solution)/shard_map/ppermute | solution.py:22
  29.1 4.2 %copy-start.5 = (f32[2,4096]{1,0:T(2,128)}, f32[2,4096]{1,0:T(2,128)S(1)}, u32[]{:S(2)}) copy-start(f32[2,4096]{1,0:T(2,128)S(1)} %collective-permute-done.3.dens_below_ref) | copy-start | bytes 98308
  33.4 0.6 %copy-start.6 = (f32[2,4096]{1,0:T(2,128)}, f32[2,4096]{1,0:T(2,128)S(1)}, u32[]{:S(2)}) copy-start(f32[2,4096]{1,0:T(2,128)S(1)} %collective-permute-done.2.dens_above_ref) | copy-start | bytes 98308
  33.4 0.7 %copy-start.3 = (f32[2,2,4,4096]{3,2,1,0:T(4,128)}, f32[2,2,4,4096]{3,2,1,0:T(4,128)S(1)}, u32[]{:S(2)}) copy-start(f32[2,2,4,4096]{3,2,1,0:T(4,128)S(1)} %collective-permute-done.1.src_below_ref) | copy-start | bytes 786436
  40.3 8.7 %copy-start.4 = (f32[2,16,4096]{2,1,0:T(8,128)S(1)}, f32[2,16,4096]{2,1,0:T(8,128)}, u32[]{:S(2)}) copy-start(f32[2,16,4096]{2,1,0:T(8,128)} %get-tuple-element.4) | copy-start | bytes 1572868
  42.6 14.0 %all-to-all-start.1 = ((f32[8,2,128]{2,1,0:T(2,128)}), f32[8,2,128]{2,1,0:T(2,128)S(1)}, u32[]{:S(2)}, u32[]{:S(2)}) async-start(f32[8,2,128]{2,1,0:T(2,128)} %copy.30), calls=%async_computation.1 | async-start | bytes 16384 | tf_op jit(solution)/shard_map/all_to_all | solution.py:195

commit v7 on v6

--- a/solution.py
+++ b/solution.py
@@ -7,6 +7,8 @@
 
 ITERS = 4
 HALO = 4
+FACTOR = 4
+GRAD_SCALE = 4.0 / 16
 SHIFTS = (-2, -1, 0, 1, 2)
 
 
@@ -63,29 +65,32 @@
 
 
 def march_kernel(
-    bounds_ref, drive_ref, fwd_ref, adj_ref, src_above_ref, src_below_ref,
+    drive_ref, fwd_ref, adj_ref, src_above_ref, src_below_ref,
     dens_ref, dens_above_ref, dens_below_ref, matched_ref,
-    final_ref, per_col_ref,
-    source_ref, density_ref, history_ref, sense_ref,
+    final_ref, gathered_ref,
+    source_ref, density_ref, step_ref, history_ref, sense_ref,
 ):
     runs, waves, rows, cols = source_ref.shape
     own = fwd_ref.shape[1]
-    reach = dens_above_ref.shape[0]
+    reach = dens_above_ref.shape[0] - 1
+    block_rows = gathered_ref.shape[0]
     for wave in range(waves):
         for run, own_ref in enumerate((fwd_ref, adj_ref)):
             source_ref[run, wave, 0:HALO] = src_above_ref[run, wave]
             source_ref[run, wave, HALO : HALO + own] = own_ref[wave]
             source_ref[run, wave, HALO + own : rows] = src_below_ref[run, wave]
     density_ref[...] = jnp.zeros((rows, cols), jnp.float32)
-    density_ref[HALO - reach : HALO] = dens_above_ref[...]
+    density_ref[HALO - reach : HALO] = dens_above_ref[0:reach]
     density_ref[HALO : HALO + own] = dens_ref[...]
-    density_ref[HALO + own : HALO + own + reach] = dens_below_ref[...]
+    density_ref[HALO + own : HALO + own + reach] = dens_below_ref[1 : reach + 1]
+    step_ref[0:HALO] = jnp.broadcast_to(time_step * dens_above_ref[reach : reach + 1], (HALO, cols))
+    step_ref[HALO : HALO + own] = jnp.full((own, cols), time_step, jnp.float32)
+    step_ref[HALO + own : rows] = jnp.broadcast_to(time_step * dens_below_ref[0:1], (HALO, cols))
     row_id = lax.broadcasted_iota(jnp.int32, (rows, cols), 0)
     col_id = lax.broadcasted_iota(jnp.int32, (rows, cols), 1)
-    valid = (row_id >= bounds_ref[0]) & (row_id < bounds_ref[1])
     density = density_ref[...]
-    inverse = jnp.where(valid, time_step / (1.0 + high_contrast * density), 0.0)
-    hy_step = jnp.where(valid, time_step, 0.0)
+    hy_step = step_ref[...]
+    inverse = jnp.where(hy_step > 0.0, time_step / (1.0 + high_contrast * density), 0.0)
     sense_ref[...] = jnp.zeros((rows, cols), jnp.float32)
     for wave in range(waves):
         for run in range(runs):
@@ -112,12 +117,20 @@
                     sense_ref[...] += field_e * history_ref[ITERS - 1 - turn]
             if run == 0:
                 final_ref[wave] = field_e
-    scaled = drive_ref[ITERS, 0] * sense_ref[HALO : HALO + own]
-    for code in range(matched_ref.shape[0]):
-        per_col_ref[code : code + 1] = jnp.sum(matched_ref[code] * scaled, axis=0, keepdims=True)
-
-
-def march(bounds, drive, fwd, adj, src_above, src_below, dens, dens_above, dens_below, matched):
+    scaled = GRAD_SCALE * sense_ref[HALO : HALO + own]
+    lane = lax.broadcasted_iota(jnp.int32, (1, cols), 1)
+    for row in range(block_rows):
+        acc = jnp.zeros((1, cols), jnp.float32)
+        for slot, shift in enumerate(SHIFTS):
+            code = row * len(SHIFTS) + slot
+            per_col = jnp.sum(matched_ref[code] * scaled, axis=0, keepdims=True)
+            moved = FACTOR * shift
+            inside = (lane >= moved) & (lane < cols + moved)
+            acc = acc + jnp.where(inside, pltpu.roll(per_col, moved % cols, 1), 0.0)
+        gathered_ref[row : row + 1] = acc
+
+
+def march(drive, fwd, adj, src_above, src_below, dens, dens_above, dens_below, matched, block_rows):
     runs, waves, _, cols = src_above.shape
     rows = fwd.shape[1] + 2 * HALO
     vmem = pltpu.MemorySpace.VMEM
@@ -126,17 +139,18 @@
         march_kernel,
         out_shape=(
             jax.ShapeDtypeStruct((waves, rows, cols), jnp.float32),
-            jax.ShapeDtypeStruct((matched.shape[0], cols), jnp.float32),
+            jax.ShapeDtypeStruct((block_rows, cols), jnp.float32),
         ),
-        in_specs=[pl.BlockSpec(memory_space=smem)] * 2 + [pl.BlockSpec(memory_space=vmem)] * 8,
+        in_specs=[pl.BlockSpec(memory_space=smem)] + [pl.BlockSpec(memory_space=vmem)] * 8,
         out_specs=(pl.BlockSpec(memory_space=vmem), pl.BlockSpec(memory_space=vmem)),
         scratch_shapes=[
             pltpu.VMEM((runs, waves, rows, cols), jnp.float32),
             pltpu.VMEM((rows, cols), jnp.float32),
+            pltpu.VMEM((rows, cols), jnp.float32),
             pltpu.VMEM((ITERS, rows, cols), jnp.float32),
             pltpu.VMEM((rows, cols), jnp.float32),
         ],
-    )(bounds, drive, fwd, adj, src_above, src_below, dens, dens_above, dens_below, matched)
+    )(drive, fwd, adj, src_above, src_below, dens, dens_above, dens_below, matched)
 
 
 def shards(density, foot_index, foot_weight, source_fwd, source_adj, omega):
@@ -147,6 +161,7 @@
     block_rows, block_cols = strip.shape
     cells_x, cells_y = foot_index.shape[1:]
     factor = cells_y // block_cols
+    assert factor == FACTOR and high_contrast / (source_fwd.shape[0] * lax.axis_size("wl")) == GRAD_SCALE
     weights = foot_weight.astype(jnp.float32)
     col_block = lax.broadcasted_iota(jnp.int32, (1, cells_y), 1) // factor
     key = (foot_index // block_cols) * len(SHIFTS) + (foot_index % block_cols - col_block[None]) + 2
@@ -167,24 +182,14 @@
     reach = 2
     last_rows = jnp.sum(matched[:, -reach:] * candidates[:, None, :], axis=0)
     first_rows = jnp.sum(matched[:, :reach] * candidates[:, None, :], axis=0)
-    above = from_behind(last_rows, "tile", 1)
-    below = from_behind(first_rows, "tile", -1)
+    present = jnp.ones((1, cells_y), jnp.float32)
+    above = from_behind(jnp.concatenate([last_rows, present]), "tile", 1)
+    below = from_behind(jnp.concatenate([present, first_rows]), "tile", -1)
     density_cell = jnp.sum(matched * candidates[:, None, :], axis=0)
-    rows_ext = cells_x + 2 * HALO
-    first = HALO - lax.axis_index("tile") * cells_x
-    bounds = jnp.stack([first, first + cells_x * lax.axis_size("tile")]).astype(jnp.int32)
-    total_waves = source_fwd.shape[0] * lax.axis_size("wl")
-    drive = jnp.concatenate(
-        [jnp.stack([jnp.sin(omega * (turn + 1.0)) for turn in range(ITERS)]),
-         jnp.full((1, omega.shape[0]), high_contrast / total_waves, jnp.float32)]
+    drive = jnp.stack([jnp.sin(omega * (turn + 1.0)) for turn in range(ITERS)])
+    final, gathered = march(
+        drive, source_fwd, source_adj, src_above, src_below, density_cell, above, below, matched, block_rows
     )
-    final, per_col = march(
-        bounds, drive, source_fwd, source_adj, src_above, src_below, density_cell, above, below, matched
-    )
-    per_col = per_col.reshape(block_rows, len(SHIFTS), cells_y)
-    gathered = jnp.zeros((block_rows, cells_y), jnp.float32)
-    for slot, shift in enumerate(SHIFTS):
-        gathered = gathered + lane_shift(per_col[:, slot], factor * shift)
     count = lax.axis_size("wl")
     pooled = jnp.einsum(
         "rky,cy->krc",

time: 57.6 us -> 57.2 us (level)
  the two profiles are of different devices: /device:TPU:32 before, /device:TPU:25 now
where the time goes in v7:
time: 57.2 us; the launch traced here: 56.7 us
  starting transfers between devices  27.7 us (48%)
  waiting for transfers between devices  9.93 us (17%)
  Pallas kernels  6.12 us (11%)
  local copies, waits for them, and re-layouts  5.48 us (10%)
  other arithmetic  5.45 us (10%)
  matrix products  1.18 us (2%)
  between operations  0.84 us (1%)
    ppermute x4, starting transfers between devices, from_behind(): lax.ppermute(value, axis, [(source, source + steps) for source in range(f...  12.9 us
    all_to_all x1, starting transfers between devices, shards(): lax.all_to_all(pooled.reshape(count, chunks // count, block_rows, span).t...  7.53 us
    all_to_all x1, starting transfers between devices, gather_columns(): pieces = lax.all_to_all(copies, axis, 0, 0, tiled=True)  7.33 us
    pallas_call x1, Pallas kernels, march(): pl.pallas_call(march_kernel, out_shape=(jax.ShapeDtypeStruct((waves, rows...  6.12 us
    ppermute x4, waiting for transfers between devices, from_behind(): lax.ppermute(value, axis, [(source, source + steps) for source in range(f...  5.17 us
    all_to_all x1, waiting for transfers between devices, shards(): lax.all_to_all(pooled.reshape(count, chunks // count, block_rows, span).t...  4.76 us
    another operation x1, other arithmetic, shards(): sources = jnp.stack([source_fwd, source_adj])  2.05 us
    slice x1, local copies, waits for them, and re-layouts, shards(): return (final[:, HALO:HALO + cells_x], density_grad)  1.77 us
  transfers between devices with their start and end apart: 6, of which 2 were waited for; matrix products, arithmetic and copies ran while one was open for 13% of the time, Pallas kernels for 0%

profile of v7, /device:TPU:25, one launch (start us, length us, event | category | flops | bytes accessed | tf_op | source)
XLA Modules:
  0.0 56.7 jit_solution(3317166981781369443)
XLA Ops:
  0.6 1.3 %broadcast_in_dim.55 = f32[8,2,128]{2,1,0:T(2,128)} broadcast(f32[2,128]{1,0:T(2,128)} %param.6), dimensions={1,2} | broadcast | bytes 9216 | tf_op jit(solution)/shard_map/broadcast_in_dim | solution.py:35
  2.0 7.3 %all-to-all-start = ((f32[8,2,128]{2,1,0:T(2,128)}), f32[8,2,128]{2,1,0:T(2,128)S(1)}, u32[]{:S(2)}, u32[]{:S(2)}) async-start(f32[8,2,128]{2,1,0:T(2,128)} %broadcast_in_dim.55), calls=%async_computation | async-start | bytes 16384 | tf_op jit(solution)/shard_map/all_to_all | solution.py:36
  9.3 2.0 %pad_maximum_fusion = (f32[2,2,4,4096]{3,2,1,0:T(4,128)S(1)}, f32[2,2,4,4096]{3,2,1,0:T(4,128)}) fusion(f32[1,2,8,4096]{3,2,1,0:T(8,128)} %bitcast.52, f32[1,2,8,4096]{3,2,1,0:T(8,128)} %bitcast.51), kind=kLoop, calls=%fused_computation.28 | loop fusion | flops 131072 | bytes 1048576 | tf_op jit(solution)/shard_map/stack | solution.py:157
  11.4 3.3 %collective-permute-start = (f32[2,2,4,4096]{3,2,1,0:T(4,128)}, f32[2,2,4,4096]{3,2,1,0:T(4,128)S(1)}, u32[]{:S(2)}, u32[]{:S(2)}) collective-permute-start(f32[2,2,4,4096]{3,2,1,0:T(4,128)} %get-tuple-element.19), channel_id=1, source_target_pairs={{0,1},{1,2},{2,3},{3,4},{4,5},{5,6},{6,7},{7,8},{8,9},{9,10},{10,1... | collective-permute-start | bytes 786440 | tf_op jit(solution)/shard_map/ppermute | solution.py:24
  14.6 1.9 %collective-permute-start.1 = (f32[2,2,4,4096]{3,2,1,0:T(4,128)S(1)}, f32[2,2,4,4096]{3,2,1,0:T(4,128)S(1)}, u32[]{:S(2)}, u32[]{:S(2)}) collective-permute-start(f32[2,2,4,4096]{3,2,1,0:T(4,128)S(1)} %get-tuple-element.18), channel_id=1, source_target_pairs={{1,0},{2,1},{3,2},{4,3},{5,4},{6,5},{7,6},{8,7},{9,8},{10,9},{11,1... | collective-permute-start | bytes 786440 | tf_op jit(solution)/shard_map/ppermute | solution.py:24
  16.6 0.5 fusion.2
  17.1 0.0 copy-start.7
  17.3 0.5 copy-done.7
  17.8 0.1 sine_bitcast_fusion.3
  17.9 0.0 all-to-all-done
  17.9 0.1 pad_slice_fusion.8
  18.0 0.1 pad_slice_fusion.4
  18.0 0.1 stack.69
  18.1 0.2 fusion.12
  18.4 1.2 %select_add_fusion = (f32[10,8,4096]{2,1,0:T(8,128)S(1)}, f32[8,4096]{1,0:T(8,128)}) fusion(f32[8,4096]{1,0:T(8,128)S(1)} %get-tuple-element.15, s32[8,4096]{1,0:T(8,128)S(1)} %get-tuple-element.11, f32[8,4096]{1,0:T(8,128)S(1)} %get-tuple-element.16, s32[8,4096]{1,0:T(8,128)S(1)} %get-tuple-element.12, f32[8,4096]{1,0:T(8,128)S(1)} %get-tuple-element.17, ...), kind=kLoop, calls=%fused_computation.1 | loop fusion | flops 4227072 | bytes 2654208 | tf_op jit(solution)/shard_map/add | solution.py:171
  19.6 0.4 fusion.8
  20.0 5.7 %collective-permute-start.2 = (f32[3,4096]{1,0:T(4,128)S(1)}, f32[3,4096]{1,0:T(4,128)S(1)}, u32[]{:S(2)}, u32[]{:S(2)}) collective-permute-start(f32[3,4096]{1,0:T(4,128)S(1)} %concatenate.6), channel_id=1, source_target_pairs={{0,1},{1,2},{2,3},{3,4},{4,5},{5,6},{6,7},{7,8},{8,9},{9,10},{10,1... | collective-permute-start | bytes 147464 | tf_op jit(solution)/shard_map/ppermute | solution.py:24
  25.8 1.9 %collective-permute-start.3 = (f32[3,4096]{1,0:T(4,128)S(1)}, f32[3,4096]{1,0:T(4,128)S(1)}, u32[]{:S(2)}, u32[]{:S(2)}) collective-permute-start(f32[3,4096]{1,0:T(4,128)S(1)} %concatenate.7), channel_id=1, source_target_pairs={{1,0},{2,1},{3,2},{4,3},{5,4},{6,5},{7,6},{8,7},{9,8},{10,9},{11,1... | collective-permute-start | bytes 147464 | tf_op jit(solution)/shard_map/ppermute | solution.py:24
  27.8 0.6 %pad_maximum_fusion.1.drive_ref = f32[4,2]{1,0:T(4,128)} fusion(f32[1,2]{1,0:T(1,128)S(1)} %get-tuple-element.34, f32[1,2]{1,0:T(1,128)S(1)} %get-tuple-element.35, f32[1,2]{1,0:T(1,128)S(1)} %get-tuple-element.33, f32[1,2]{1,0:T(1,128)S(1)} %get-tuple-element.32), kind=kLoop, calls=%fused_computation.68 | loop fusion | flops 24 | bytes 64 | tf_op jit(solution)/shard_map/stack | solution.py:189
  28.4 0.0 collective-permute-done.2.dens_above_ref
  28.4 5.2 %collective-permute-done.3.dens_below_ref = f32[3,4096]{1,0:T(4,128)S(1)} collective-permute-done((f32[3,4096]{1,0:T(4,128)S(1)}, f32[3,4096]{1,0:T(4,128)S(1)}, u32[]{:S(2)}, u32[]{:S(2)}) %collective-permute-start.3) | collective-permute-done | bytes 49184 | tf_op jit(solution)/shard_map/ppermute | solution.py:24
  33.5 0.0 collective-permute-done.src_above_ref
  33.6 0.6 %copy-done.6 = f32[3,4096]{1,0:T(4,128)} copy-done((f32[3,4096]{1,0:T(4,128)}, f32[3,4096]{1,0:T(4,128)S(1)}, u32[]{:S(2)}) %copy-start.6) | copy-done | bytes 49176
  34.1 0.1 copy-done.3
  34.2 0.1 copy-done.4
  34.4 6.1 %shard_map.77 = (f32[2,16,4096]{2,1,0:T(8,128)}, f32[2,4096]{1,0:T(2,128)}) custom-call(f32[4,2]{1,0:T(4,128)} %pad_maximum_fusion.1.drive_ref, f32[2,8,4096]{2,1,0:T(8,128)} %fwd_ref.1, f32[2,8,4096]{2,1,0:T(8,128)} %adj_ref.1, f32[2,2,4,4096]{3,2,1,0:T(4,128)} %copy-done.3, f32[2,2,4,4096]{3,2,1,0:T(4,128)} %copy-done.4, ...), custom_call_target="tpu_custom_call" | custom-call | tf_op jit(solution)/shard_map/pallas_call | solution.py:138
  40.5 0.9 %convolution_bitcast_fusion = f32[8,2,128]{2,0,1:T(8,128)S(1)} fusion(s32[512]{0:T(512)S(1)} %get-tuple-element.36, s32[512]{0:T(512)S(1)} %get-tuple-element.37, pred[512]{0:T(512)(128)(4,1)S(1)} %fusion.27, f32[1,2,8,512]{3,1,2,0:T(2,128)} %bitcast.64), kind=kOutput, calls=%fused_computation.6 | convolution fusion | flops 12713984 | bytes 45568 | tf_op jit(solution)/shard_map/rky,cy->krc/dot_general | solution.py:194
  41.4 0.7 %copy.8 = f32[8,2,128]{2,1,0:T(2,128)} copy(f32[8,2,128]{2,0,1:T(8,128)S(1)} %convolution_bitcast_fusion) | data formatting | bytes 16384 | tf_op jit(solution)/shard_map/rky,cy->krc/transpose | solution.py:194
  42.1 7.5 %all-to-all-start.1 = ((f32[8,2,128]{2,1,0:T(2,128)}), f32[8,2,128]{2,1,0:T(2,128)S(1)}, u32[]{:S(2)}, u32[]{:S(2)}) async-start(f32[8,2,128]{2,1,0:T(2,128)} %copy.8), calls=%async_computation.1 | async-start | bytes 16384 | tf_op jit(solution)/shard_map/all_to_all | solution.py:200
  49.6 1.8 %slice.107 = f32[2,8,4096]{2,1,0:T(8,128)} slice(f32[2,16,4096]{2,1,0:T(8,128)} %get-tuple-element.4), slice={[0:2], [4:12], [0:4096]} | slice | bytes 524288 | tf_op jit(solution)/shard_map/slice | solution.py:204
  51.4 4.8 %all-to-all-done.1 = f32[8,2,128]{2,1,0:T(2,128)S(1)} async-done(((f32[8,2,128]{2,1,0:T(2,128)}), f32[8,2,128]{2,1,0:T(2,128)S(1)}, u32[]{:S(2)}, u32[]{:S(2)}) %all-to-all-start.1) | async-done | bytes 8224 | tf_op jit(solution)/shard_map/all_to_all | solution.py:200
  56.1 0.6 %reduce_sum.39 = f32[2,128]{1,0:T(2,128)} reduce(f32[8,2,128]{2,1,0:T(2,128)S(1)} %all-to-all-done.1, f32[]{:T(128)} %constant.69.clone.1), dimensions={0}, to_apply=%region_3.4 | reduce | flops 1792 | bytes 9220 | tf_op jit(solution)/shard_map/reduce_sum | solution.py:203
  (23 shorter events, 0.2 us)
Async XLA Ops:
  0.6 15.9 %copy-start.1 = (s32[4,8,4096]{2,1,0:T(8,128)S(1)}, s32[4,8,4096]{2,1,0:T(8,128)}, u32[]{:S(2)}) copy-start(s32[4,8,4096]{2,1,0:T(8,128)} %param.7) | copy-start | bytes 1572868
  2.0 15.9 %all-to-all-start = ((f32[8,2,128]{2,1,0:T(2,128)}), f32[8,2,128]{2,1,0:T(2,128)S(1)}, u32[]{:S(2)}, u32[]{:S(2)}) async-start(f32[8,2,128]{2,1,0:T(2,128)} %broadcast_in_dim.55), calls=%async_computation | async-start | bytes 16384 | tf_op jit(solution)/shard_map/all_to_all | solution.py:36
  11.4 5.8 %copy-start.2 = (bf16[4,8,4096]{2,1,0:T(8,128)(2,1)S(1)}, bf16[4,8,4096]{2,1,0:T(8,128)(2,1)}, u32[]{:S(2)}) copy-start(bf16[4,8,4096]{2,1,0:T(8,128)(2,1)} %param.8) | copy-start | bytes 786436
  11.4 22.2 %collective-permute-start = (f32[2,2,4,4096]{3,2,1,0:T(4,128)}, f32[2,2,4,4096]{3,2,1,0:T(4,128)S(1)}, u32[]{:S(2)}, u32[]{:S(2)}) collective-permute-start(f32[2,2,4,4096]{3,2,1,0:T(4,128)} %get-tuple-element.19), channel_id=1, source_target_pairs={{0,1},{1,2},{2,3},{3,4},{4,5},{5,6},{6,7},{7,8},{8,9},{9,10},{10,1... | collective-permute-start | bytes 786440 | tf_op jit(solution)/shard_map/ppermute | solution.py:24
  14.6 18.9 %collective-permute-start.1 = (f32[2,2,4,4096]{3,2,1,0:T(4,128)S(1)}, f32[2,2,4,4096]{3,2,1,0:T(4,128)S(1)}, u32[]{:S(2)}, u32[]{:S(2)}) collective-permute-start(f32[2,2,4,4096]{3,2,1,0:T(4,128)S(1)} %get-tuple-element.18), channel_id=1, source_target_pairs={{1,0},{2,1},{3,2},{4,3},{5,4},{6,5},{7,6},{8,7},{9,8},{10,9},{11,1... | collective-permute-start | bytes 786440 | tf_op jit(solution)/shard_map/ppermute | solution.py:24
  17.1 0.7 %copy-start.7 = (f32[2]{0:T(128)S(1)}, f32[2]{0:T(128)}, u32[]{:S(2)}) copy-start(f32[2]{0:T(128)} %param.11) | copy-start | bytes 28
  19.6 13.9 %copy-start = (f32[10,8,4096]{2,1,0:T(8,128)}, f32[10,8,4096]{2,1,0:T(8,128)S(1)}, u32[]{:S(2)}) copy-start(f32[10,8,4096]{2,1,0:T(8,128)S(1)} %get-tuple-element.8.matched_ref) | copy-start | bytes 3932164
  20.0 8.3 %collective-permute-start.2 = (f32[3,4096]{1,0:T(4,128)S(1)}, f32[3,4096]{1,0:T(4,128)S(1)}, u32[]{:S(2)}, u32[]{:S(2)}) collective-permute-start(f32[3,4096]{1,0:T(4,128)S(1)} %concatenate.6), channel_id=1, source_target_pairs={{0,1},{1,2},{2,3},{3,4},{4,5},{5,6},{6,7},{7,8},{8,9},{9,10},{10,1... | collective-permute-start | bytes 147464 | tf_op jit(solution)/shard_map/ppermute | solution.py:24
  25.8 7.7 %collective-permute-start.3 = (f32[3,4096]{1,0:T(4,128)S(1)}, f32[3,4096]{1,0:T(4,128)S(1)}, u32[]{:S(2)}, u32[]{:S(2)}) collective-permute-start(f32[3,4096]{1,0:T(4,128)S(1)} %concatenate.7), channel_id=1, source_target_pairs={{1,0},{2,1},{3,2},{4,3},{5,4},{6,5},{7,6},{8,7},{9,8},{10,9},{11,1... | collective-permute-start | bytes 147464 | tf_op jit(solution)/shard_map/ppermute | solution.py:24
  28.4 5.2 %copy-start.5 = (f32[3,4096]{1,0:T(4,128)}, f32[3,4096]{1,0:T(4,128)S(1)}, u32[]{:S(2)}) copy-start(f32[3,4096]{1,0:T(4,128)S(1)} %collective-permute-done.2.dens_above_ref) | copy-start | bytes 147460
  33.5 0.6 %copy-start.6 = (f32[3,4096]{1,0:T(4,128)}, f32[3,4096]{1,0:T(4,128)S(1)}, u32[]{:S(2)}) copy-start(f32[3,4096]{1,0:T(4,128)S(1)} %collective-permute-done.3.dens_below_ref) | copy-start | bytes 147460
  33.5 0.7 %copy-start.3 = (f32[2,2,4,4096]{3,2,1,0:T(4,128)}, f32[2,2,4,4096]{3,2,1,0:T(4,128)S(1)}, u32[]{:S(2)}) copy-start(f32[2,2,4,4096]{3,2,1,0:T(4,128)S(1)} %collective-permute-done.src_above_ref) | copy-start | bytes 786436
  33.5 0.8 %copy-start.4 = (f32[2,2,4,4096]{3,2,1,0:T(4,128)}, f32[2,2,4,4096]{3,2,1,0:T(4,128)S(1)}, u32[]{:S(2)}) copy-start(f32[2,2,4,4096]{3,2,1,0:T(4,128)S(1)} %collective-permute-done.1.src_below_ref) | copy-start | bytes 786436
  42.1 14.1 %all-to-all-start.1 = ((f32[8,2,128]{2,1,0:T(2,128)}), f32[8,2,128]{2,1,0:T(2,128)S(1)}, u32[]{:S(2)}, u32[]{:S(2)}) async-start(f32[8,2,128]{2,1,0:T(2,128)} %copy.8), calls=%async_computation.1 | async-start | bytes 16384 | tf_op jit(solution)/shard_map/all_to_all | solution.py:200

commit v8 on v7

--- a/solution.py
+++ b/solution.py
@@ -67,13 +67,13 @@
 def march_kernel(
     drive_ref, fwd_ref, adj_ref, src_above_ref, src_below_ref,
     dens_ref, dens_above_ref, dens_below_ref, matched_ref,
-    final_ref, gathered_ref,
-    source_ref, density_ref, step_ref, history_ref, sense_ref,
+    final_ref, pieces_ref,
+    source_ref, density_ref, step_ref, history_ref, sense_ref, gathered_ref,
 ):
     runs, waves, rows, cols = source_ref.shape
     own = fwd_ref.shape[1]
     reach = dens_above_ref.shape[0] - 1
-    block_rows = gathered_ref.shape[0]
+    block_rows = pieces_ref.shape[1]
     for wave in range(waves):
         for run, own_ref in enumerate((fwd_ref, adj_ref)):
             source_ref[run, wave, 0:HALO] = src_above_ref[run, wave]
@@ -128,9 +128,21 @@
             inside = (lane >= moved) & (lane < cols + moved)
             acc = acc + jnp.where(inside, pltpu.roll(per_col, moved % cols, 1), 0.0)
         gathered_ref[row : row + 1] = acc
-
-
-def march(drive, fwd, adj, src_above, src_below, dens, dens_above, dens_below, matched, block_rows):
+    gathered_ref[block_rows:] = jnp.zeros((gathered_ref.shape[0] - block_rows, cols), jnp.float32)
+    span = pieces_ref.shape[2]
+    width = span * FACTOR
+    spread = (
+        lax.broadcasted_iota(jnp.int32, (width, span), 0) // FACTOR
+        == lax.broadcasted_iota(jnp.int32, (width, span), 1)
+    ).astype(jnp.float32)
+    for chunk in range(pieces_ref.shape[0]):
+        pieces_ref[chunk] = jnp.dot(
+            gathered_ref[:, chunk * width : (chunk + 1) * width], spread,
+            precision=lax.Precision.HIGHEST, preferred_element_type=jnp.float32,
+        )[:block_rows]
+
+
+def march(drive, fwd, adj, src_above, src_below, dens, dens_above, dens_below, matched, block_rows, chunks):
     runs, waves, _, cols = src_above.shape
     rows = fwd.shape[1] + 2 * HALO
     vmem = pltpu.MemorySpace.VMEM
@@ -139,7 +151,7 @@
         march_kernel,
         out_shape=(
             jax.ShapeDtypeStruct((waves, rows, cols), jnp.float32),
-            jax.ShapeDtypeStruct((block_rows, cols), jnp.float32),
+            jax.ShapeDtypeStruct((chunks, block_rows, 128), jnp.float32),
         ),
         in_specs=[pl.BlockSpec(memory_space=smem)] + [pl.BlockSpec(memory_space=vmem)] * 8,
         out_specs=(pl.BlockSpec(memory_space=vmem), pl.BlockSpec(memory_space=vmem)),
@@ -149,6 +161,7 @@
             pltpu.VMEM((rows, cols), jnp.float32),
             pltpu.VMEM((ITERS, rows, cols), jnp.float32),
             pltpu.VMEM((rows, cols), jnp.float32),
+            pltpu.VMEM((8, cols), jnp.float32),
         ],
     )(drive, fwd, adj, src_above, src_below, dens, dens_above, dens_below, matched)
 
@@ -169,6 +182,8 @@
     matched = jnp.zeros((block_rows * len(SHIFTS), cells_x, cells_y), jnp.float32)
     for entry in range(foot_index.shape[0]):
         matched = matched + jnp.where(key[entry][None] == codes, weights[entry][None], 0.0)
+    drive = jnp.stack([jnp.sin(omega * (turn + 1.0)) for turn in range(ITERS)])
+    matched, drive = lax.optimization_barrier((matched, drive))
     span = 128
     chunks = block_cols // span
     spread = (
@@ -186,19 +201,12 @@
     above = from_behind(jnp.concatenate([last_rows, present]), "tile", 1)
     below = from_behind(jnp.concatenate([present, first_rows]), "tile", -1)
     density_cell = jnp.sum(matched * candidates[:, None, :], axis=0)
-    drive = jnp.stack([jnp.sin(omega * (turn + 1.0)) for turn in range(ITERS)])
-    final, gathered = march(
-        drive, source_fwd, source_adj, src_above, src_below, density_cell, above, below, matched, block_rows
+    final, pieces = march(
+        drive, source_fwd, source_adj, src_above, src_below, density_cell, above, below, matched, block_rows, chunks
     )
     count = lax.axis_size("wl")
-    pooled = jnp.einsum(
-        "rky,cy->krc",
-        gathered.reshape(block_rows, chunks, span * factor),
-        spread,
-        precision=lax.Precision.HIGHEST,
-    )
     density_grad = lax.all_to_all(
-        pooled.reshape(count, chunks // count, block_rows, span).transpose(0, 2, 1, 3).reshape(count, block_rows, -1),
+        pieces.reshape(count, chunks // count, block_rows, span).transpose(0, 2, 1, 3).reshape(count, block_rows, -1),
         "wl", 0, 0, tiled=True,
     ).sum(axis=0)
     return (final[:, HALO : HALO + cells_x], density_grad)

time: 57.2 us -> 54 us (0.944)
  starting transfers between devices: 27.7 us -> 26.1 us
  matrix products: 1.18 us -> 0.25 us
  waiting for transfers between devices: 9.93 us -> 9.28 us
    dot_general x1 -> x0, matrix products: 0.93 us -> none  [shards(): jnp.einsum('rky,cy->krc', gathered.reshape(block_rows, chunks, span * fac...]
    all_to_all x1, starting transfers between devices: 7.53 us -> 6.65 us  [shards(): lax.all_to_all(pieces.reshape(count, chunks // count, block_rows, span).t...]
    reduce_sum x1 -> x2, other arithmetic: 0.58 us -> 1.34 us  [the longest x1 0.77 us: shards(): density_cell = jnp.sum(matched * candidates[:, None, :], axis=0)]
    add x1, other arithmetic: 1.19 us -> 0.47 us  [shards(): matched + jnp.where(key[entry][None] == codes, weights[entry][None], 0.0)]
    ppermute x4, starting transfers between devices: 12.9 us -> 12.1 us  [from_behind(): lax.ppermute(value, axis, [(source, source + steps) for source in range(f...]
    another operation x1, other arithmetic: 2.05 us -> 1.35 us  [shards(): sources = jnp.stack([source_fwd, source_adj])]
    another operation x2, other arithmetic: 0.67 us -> 1.33 us  [shards(): drive = jnp.stack([jnp.sin(omega * (turn + 1.0)) for turn in range(ITERS)])]
    transpose x1 -> x0, local copies, waits for them, and re-layouts: 0.66 us -> none  [shards(): jnp.einsum('rky,cy->krc', gathered.reshape(block_rows, chunks, span * fac...]
  transfers between devices with their start and end apart: 6 -> 6, of which waited for: 2 -> 2; matrix products, arithmetic and copies ran while one was open for 13% -> 14% of each run, Pallas kernels for 0% -> 0%
where the time goes in v8:
time: 54 us; the launch traced here: 53.5 us
  starting transfers between devices  26.1 us (48%)
  waiting for transfers between devices  9.28 us (17%)
  Pallas kernels  6.65 us (12%)
  other arithmetic  5.46 us (10%)
  local copies, waits for them, and re-layouts  4.96 us (9%)
  between operations  0.83 us (2%)
    ppermute x4, starting transfers between devices, from_behind(): lax.ppermute(value, axis, [(source, source + steps) for source in range(f...  12.1 us
    all_to_all x1, starting transfers between devices, gather_columns(): pieces = lax.all_to_all(copies, axis, 0, 0, tiled=True)  7.33 us
    pallas_call x1, Pallas kernels, march(): pl.pallas_call(march_kernel, out_shape=(jax.ShapeDtypeStruct((waves, rows...  6.65 us
    all_to_all x1, starting transfers between devices, shards(): lax.all_to_all(pieces.reshape(count, chunks // count, block_rows, span).t...  6.65 us
    all_to_all x1, waiting for transfers between devices, shards(): lax.all_to_all(pieces.reshape(count, chunks // count, block_rows, span).t...  4.76 us
    ppermute x4, waiting for transfers between devices, from_behind(): lax.ppermute(value, axis, [(source, source + steps) for source in range(f...  4.51 us
    slice x1, local copies, waits for them, and re-layouts, shards(): return (final[:, HALO:HALO + cells_x], density_grad)  1.77 us
    unnamed x14, local copies, waits for them, and re-layouts  1.44 us
  transfers between devices with their start and end apart: 6, of which 2 were waited for; matrix products, arithmetic and copies ran while one was open for 14% of the time, Pallas kernels for 0%

profile of v8, /device:TPU:25, one launch (start us, length us, event | category | flops | bytes accessed | tf_op | source)
XLA Modules:
  0.0 53.5 jit_solution(15809743296900753770)
XLA Ops:
  0.6 0.0 copy-start.1
  0.6 1.3 %broadcast_in_dim.55 = f32[8,2,128]{2,1,0:T(2,128)} broadcast(f32[2,128]{1,0:T(2,128)} %param.6), dimensions={1,2} | broadcast | bytes 9216 | tf_op jit(solution)/shard_map/broadcast_in_dim | solution.py:35
  2.0 7.3 %all-to-all-start = ((f32[8,2,128]{2,1,0:T(2,128)}), f32[8,2,128]{2,1,0:T(2,128)S(1)}, u32[]{:S(2)}, u32[]{:S(2)}) async-start(f32[8,2,128]{2,1,0:T(2,128)} %broadcast_in_dim.55), calls=%async_computation | async-start | bytes 16384 | tf_op jit(solution)/shard_map/all_to_all | solution.py:36
  9.3 1.3 %pad_maximum_fusion = (f32[2,2,4,4096]{3,2,1,0:T(4,128)S(1)}, f32[2,2,4,4096]{3,2,1,0:T(4,128)S(1)}) fusion(f32[1,2,8,4096]{3,2,1,0:T(8,128)} %bitcast.43, f32[1,2,8,4096]{3,2,1,0:T(8,128)} %bitcast.42), kind=kLoop, calls=%fused_computation.25 | loop fusion | flops 131072 | bytes 1048576 | tf_op jit(solution)/shard_map/stack | solution.py:170
  10.7 0.0 copy-start.2
  10.7 3.0 %collective-permute-start.1 = (f32[2,2,4,4096]{3,2,1,0:T(4,128)S(1)}, f32[2,2,4,4096]{3,2,1,0:T(4,128)S(1)}, u32[]{:S(2)}, u32[]{:S(2)}) collective-permute-start(f32[2,2,4,4096]{3,2,1,0:T(4,128)S(1)} %get-tuple-element.12), channel_id=1, source_target_pairs={{1,0},{2,1},{3,2},{4,3},{5,4},{6,5},{7,6},{8,7},{9,8},{10,9},{11,1... | collective-permute-start | bytes 786440 | tf_op jit(solution)/shard_map/ppermute | solution.py:24
  13.7 4.8 %collective-permute-start = (f32[2,2,4,4096]{3,2,1,0:T(4,128)S(1)}, f32[2,2,4,4096]{3,2,1,0:T(4,128)S(1)}, u32[]{:S(2)}, u32[]{:S(2)}) collective-permute-start(f32[2,2,4,4096]{3,2,1,0:T(4,128)S(1)} %get-tuple-element.13), channel_id=1, source_target_pairs={{0,1},{1,2},{2,3},{3,4},{4,5},{5,6},{6,7},{7,8},{8,9},{9,10},{10,1... | collective-permute-start | bytes 786440 | tf_op jit(solution)/shard_map/ppermute | solution.py:24
  18.5 0.7 %sine_bitcast_fusion.3 = (f32[1,2]{1,0:T(1,128)S(1)}, f32[1,2]{1,0:T(1,128)S(1)}, f32[1,2]{1,0:T(1,128)S(1)}, f32[1,2]{1,0:T(1,128)S(1)}) fusion(f32[2]{0:T(128)} %param.11), kind=kLoop, calls=%fused_computation.65 | loop fusion | flops 6 | bytes 40 | tf_op jit(solution)/shard_map/stack | solution.py:185
  19.3 0.5 fusion.2
  19.9 0.6 %pad_maximum_fusion.1.drive_ref = f32[4,2]{1,0:T(4,128)} fusion(f32[1,2]{1,0:T(1,128)S(1)} %get-tuple-element.36, f32[1,2]{1,0:T(1,128)S(1)} %get-tuple-element.37, f32[1,2]{1,0:T(1,128)S(1)} %get-tuple-element.35, f32[1,2]{1,0:T(1,128)S(1)} %get-tuple-element.34), kind=kLoop, calls=%fused_computation.59 | loop fusion | flops 24 | bytes 64 | tf_op jit(solution)/shard_map/stack | solution.py:185
  20.5 0.5 select_add_fusion.matched_ref
  21.0 0.0 all-to-all-done
  21.0 0.1 pad_slice_fusion.4
  21.1 0.1 pad_slice_fusion.8
  21.2 0.1 stack.69
  21.3 0.2 fusion.9
  21.6 0.4 multiply_reduce_fusion.1
  22.1 1.9 %collective-permute-start.2 = (f32[3,4096]{1,0:T(4,128)S(1)}, f32[3,4096]{1,0:T(4,128)S(1)}, u32[]{:S(2)}, u32[]{:S(2)}) collective-permute-start(f32[3,4096]{1,0:T(4,128)S(1)} %concatenate.6), channel_id=1, source_target_pairs={{0,1},{1,2},{2,3},{3,4},{4,5},{5,6},{6,7},{7,8},{8,9},{9,10},{10,1... | collective-permute-start | bytes 147464 | tf_op jit(solution)/shard_map/ppermute | solution.py:24
  24.0 2.4 %collective-permute-start.3 = (f32[3,4096]{1,0:T(4,128)S(1)}, f32[3,4096]{1,0:T(4,128)S(1)}, u32[]{:S(2)}, u32[]{:S(2)}) collective-permute-start(f32[3,4096]{1,0:T(4,128)S(1)} %concatenate.7), channel_id=1, source_target_pairs={{1,0},{2,1},{3,2},{4,3},{5,4},{6,5},{7,6},{8,7},{9,8},{10,9},{11,1... | collective-permute-start | bytes 147464 | tf_op jit(solution)/shard_map/ppermute | solution.py:24
  26.4 0.8 %multiply_reduce_fusion.dens_ref = f32[8,4096]{1,0:T(8,128)} fusion(f32[10,8,4096]{2,1,0:T(8,128)S(1)} %select_add_fusion.matched_ref, f32[10,4096]{1,0:T(8,128)S(1)} %mul.44), kind=kLoop, calls=%fused_computation | loop fusion | flops 622592 | bytes 1605632 | tf_op jit(solution)/shard_map/reduce_sum | solution.py:203
  27.2 0.0 collective-permute-done.2.dens_above_ref
  27.2 4.5 %collective-permute-done.3.dens_below_ref = f32[3,4096]{1,0:T(4,128)S(1)} collective-permute-done((f32[3,4096]{1,0:T(4,128)S(1)}, f32[3,4096]{1,0:T(4,128)S(1)}, u32[]{:S(2)}, u32[]{:S(2)}) %collective-permute-start.3) | collective-permute-done | bytes 49184 | tf_op jit(solution)/shard_map/ppermute | solution.py:24
  31.7 0.0 collective-permute-done.1.src_below_ref
  31.7 0.0 collective-permute-done.src_above_ref
  31.7 0.6 %copy-done.6 = f32[3,4096]{1,0:T(4,128)} copy-done((f32[3,4096]{1,0:T(4,128)}, f32[3,4096]{1,0:T(4,128)S(1)}, u32[]{:S(2)}) %copy-start.6) | copy-done | bytes 49176
  32.3 0.1 copy-done.3
  32.4 0.7 %copy-done.4 = f32[2,2,4,4096]{3,2,1,0:T(4,128)} copy-done((f32[2,2,4,4096]{3,2,1,0:T(4,128)}, f32[2,2,4,4096]{3,2,1,0:T(4,128)S(1)}, u32[]{:S(2)}) %copy-start.4) | copy-done | bytes 262168
  33.1 6.7 %shard_map.77 = (f32[2,16,4096]{2,1,0:T(8,128)}, f32[8,2,128]{2,1,0:T(2,128)}) custom-call(f32[4,2]{1,0:T(4,128)} %pad_maximum_fusion.1.drive_ref, f32[2,8,4096]{2,1,0:T(8,128)} %fwd_ref.1, f32[2,8,4096]{2,1,0:T(8,128)} %adj_ref.1, f32[2,2,4,4096]{3,2,1,0:T(4,128)} %copy-done.4, f32[2,2,4,4096]{3,2,1,0:T(4,128)} %copy-done.3, ...), custom_call_target="tpu_custom_call" | custom-call | tf_op jit(solution)/shard_map/pallas_call | solution.py:150
  39.8 6.6 %all-to-all-start.1 = ((f32[8,2,128]{2,1,0:T(2,128)}), f32[8,2,128]{2,1,0:T(2,128)S(1)}, u32[]{:S(2)}, u32[]{:S(2)}) async-start(f32[8,2,128]{2,1,0:T(2,128)} %get-tuple-element.9), calls=%async_computation.1 | async-start | bytes 16384 | tf_op jit(solution)/shard_map/all_to_all | solution.py:208
  46.4 1.8 %slice.107 = f32[2,8,4096]{2,1,0:T(8,128)} slice(f32[2,16,4096]{2,1,0:T(8,128)} %get-tuple-element.8), slice={[0:2], [4:12], [0:4096]} | slice | bytes 524288 | tf_op jit(solution)/shard_map/slice | solution.py:212
  48.2 4.8 %all-to-all-done.1 = f32[8,2,128]{2,1,0:T(2,128)S(1)} async-done(((f32[8,2,128]{2,1,0:T(2,128)}), f32[8,2,128]{2,1,0:T(2,128)S(1)}, u32[]{:S(2)}, u32[]{:S(2)}) %all-to-all-start.1) | async-done | bytes 8224 | tf_op jit(solution)/shard_map/all_to_all | solution.py:208
  53.0 0.6 %reduce_sum.39 = f32[2,128]{1,0:T(2,128)} reduce(f32[8,2,128]{2,1,0:T(2,128)S(1)} %all-to-all-done.1, f32[]{:T(128)} %constant.66.clone.1), dimensions={0}, to_apply=%region_3.4 | reduce | flops 1792 | bytes 9220 | tf_op jit(solution)/shard_map/reduce_sum | solution.py:211
  (20 shorter events, 0.2 us)
Async XLA Ops:
  0.6 18.6 %copy-start.1 = (s32[4,8,4096]{2,1,0:T(8,128)S(1)}, s32[4,8,4096]{2,1,0:T(8,128)}, u32[]{:S(2)}) copy-start(s32[4,8,4096]{2,1,0:T(8,128)} %param.7) | copy-start | bytes 1572868
  2.0 19.0 %all-to-all-start = ((f32[8,2,128]{2,1,0:T(2,128)}), f32[8,2,128]{2,1,0:T(2,128)S(1)}, u32[]{:S(2)}, u32[]{:S(2)}) async-start(f32[8,2,128]{2,1,0:T(2,128)} %broadcast_in_dim.55), calls=%async_computation | async-start | bytes 16384 | tf_op jit(solution)/shard_map/all_to_all | solution.py:36
  10.7 9.2 %copy-start.2 = (bf16[4,8,4096]{2,1,0:T(8,128)(2,1)S(1)}, bf16[4,8,4096]{2,1,0:T(8,128)(2,1)}, u32[]{:S(2)}) copy-start(bf16[4,8,4096]{2,1,0:T(8,128)(2,1)} %param.8) | copy-start | bytes 786436
  10.7 21.0 %collective-permute-start.1 = (f32[2,2,4,4096]{3,2,1,0:T(4,128)S(1)}, f32[2,2,4,4096]{3,2,1,0:T(4,128)S(1)}, u32[]{:S(2)}, u32[]{:S(2)}) collective-permute-start(f32[2,2,4,4096]{3,2,1,0:T(4,128)S(1)} %get-tuple-element.12), channel_id=1, source_target_pairs={{1,0},{2,1},{3,2},{4,3},{5,4},{6,5},{7,6},{8,7},{9,8},{10,9},{11,1... | collective-permute-start | bytes 786440 | tf_op jit(solution)/shard_map/ppermute | solution.py:24
  13.7 18.0 %collective-permute-start = (f32[2,2,4,4096]{3,2,1,0:T(4,128)S(1)}, f32[2,2,4,4096]{3,2,1,0:T(4,128)S(1)}, u32[]{:S(2)}, u32[]{:S(2)}) collective-permute-start(f32[2,2,4,4096]{3,2,1,0:T(4,128)S(1)} %get-tuple-element.13), channel_id=1, source_target_pairs={{0,1},{1,2},{2,3},{3,4},{4,5},{5,6},{6,7},{7,8},{8,9},{9,10},{10,1... | collective-permute-start | bytes 786440 | tf_op jit(solution)/shard_map/ppermute | solution.py:24
  21.0 6.2 %copy-start = (f32[10,8,4096]{2,1,0:T(8,128)}, f32[10,8,4096]{2,1,0:T(8,128)S(1)}, u32[]{:S(2)}) copy-start(f32[10,8,4096]{2,1,0:T(8,128)S(1)} %select_add_fusion.matched_ref) | copy-start | bytes 3932164
  22.1 5.1 %collective-permute-start.2 = (f32[3,4096]{1,0:T(4,128)S(1)}, f32[3,4096]{1,0:T(4,128)S(1)}, u32[]{:S(2)}, u32[]{:S(2)}) collective-permute-start(f32[3,4096]{1,0:T(4,128)S(1)} %concatenate.6), channel_id=1, source_target_pairs={{0,1},{1,2},{2,3},{3,4},{4,5},{5,6},{6,7},{7,8},{8,9},{9,10},{10,1... | collective-permute-start | bytes 147464 | tf_op jit(solution)/shard_map/ppermute | solution.py:24
  24.0 7.7 %collective-permute-start.3 = (f32[3,4096]{1,0:T(4,128)S(1)}, f32[3,4096]{1,0:T(4,128)S(1)}, u32[]{:S(2)}, u32[]{:S(2)}) collective-permute-start(f32[3,4096]{1,0:T(4,128)S(1)} %concatenate.7), channel_id=1, source_target_pairs={{1,0},{2,1},{3,2},{4,3},{5,4},{6,5},{7,6},{8,7},{9,8},{10,9},{11,1... | collective-permute-start | bytes 147464 | tf_op jit(solution)/shard_map/ppermute | solution.py:24
  27.2 4.5 %copy-start.5 = (f32[3,4096]{1,0:T(4,128)}, f32[3,4096]{1,0:T(4,128)S(1)}, u32[]{:S(2)}) copy-start(f32[3,4096]{1,0:T(4,128)S(1)} %collective-permute-done.2.dens_above_ref) | copy-start | bytes 147460
  31.7 0.6 %copy-start.6 = (f32[3,4096]{1,0:T(4,128)}, f32[3,4096]{1,0:T(4,128)S(1)}, u32[]{:S(2)}) copy-start(f32[3,4096]{1,0:T(4,128)S(1)} %collective-permute-done.3.dens_below_ref) | copy-start | bytes 147460
  31.7 0.7 %copy-start.3 = (f32[2,2,4,4096]{3,2,1,0:T(4,128)}, f32[2,2,4,4096]{3,2,1,0:T(4,128)S(1)}, u32[]{:S(2)}) copy-start(f32[2,2,4,4096]{3,2,1,0:T(4,128)S(1)} %collective-permute-done.1.src_below_ref) | copy-start | bytes 786436
  32.4 0.7 %copy-start.4 = (f32[2,2,4,4096]{3,2,1,0:T(4,128)}, f32[2,2,4,4096]{3,2,1,0:T(4,128)S(1)}, u32[]{:S(2)}) copy-start(f32[2,2,4,4096]{3,2,1,0:T(4,128)S(1)} %collective-permute-done.src_above_ref) | copy-start | bytes 786436
  39.8 13.2 %all-to-all-start.1 = ((f32[8,2,128]{2,1,0:T(2,128)}), f32[8,2,128]{2,1,0:T(2,128)S(1)}, u32[]{:S(2)}, u32[]{:S(2)}) async-start(f32[8,2,128]{2,1,0:T(2,128)} %get-tuple-element.9), calls=%async_computation.1 | async-start | bytes 16384 | tf_op jit(solution)/shard_map/all_to_all | solution.py:208

commit v9 on v8

--- a/solution.py
+++ b/solution.py
@@ -65,21 +65,34 @@
 
 
 def march_kernel(
-    drive_ref, fwd_ref, adj_ref, src_above_ref, src_below_ref,
-    dens_ref, dens_above_ref, dens_below_ref, matched_ref,
+    drive_ref, fwd_ref, adj_ref, src_above_hbm, src_below_hbm,
+    dens_ref, dens_above_hbm, dens_below_hbm, matched_ref,
     final_ref, pieces_ref,
     source_ref, density_ref, step_ref, history_ref, sense_ref, gathered_ref,
+    src_above_ref, src_below_ref, dens_above_ref, dens_below_ref, copy_sems,
 ):
+    copies = [
+        pltpu.make_async_copy(src_above_hbm, src_above_ref, copy_sems.at[0]),
+        pltpu.make_async_copy(src_below_hbm, src_below_ref, copy_sems.at[1]),
+        pltpu.make_async_copy(dens_above_hbm, dens_above_ref, copy_sems.at[2]),
+        pltpu.make_async_copy(dens_below_hbm, dens_below_ref, copy_sems.at[3]),
+    ]
+    for copy in copies:
+        copy.start()
     runs, waves, rows, cols = source_ref.shape
     own = fwd_ref.shape[1]
     reach = dens_above_ref.shape[0] - 1
     block_rows = pieces_ref.shape[1]
+    copies[0].wait()
+    copies[1].wait()
     for wave in range(waves):
         for run, own_ref in enumerate((fwd_ref, adj_ref)):
             source_ref[run, wave, 0:HALO] = src_above_ref[run, wave]
             source_ref[run, wave, HALO : HALO + own] = own_ref[wave]
             source_ref[run, wave, HALO + own : rows] = src_below_ref[run, wave]
     density_ref[...] = jnp.zeros((rows, cols), jnp.float32)
+    copies[2].wait()
+    copies[3].wait()
     density_ref[HALO - reach : HALO] = dens_above_ref[0:reach]
     density_ref[HALO : HALO + own] = dens_ref[...]
     density_ref[HALO + own : HALO + own + reach] = dens_below_ref[1 : reach + 1]
@@ -89,6 +102,7 @@
     row_id = lax.broadcasted_iota(jnp.int32, (rows, cols), 0)
     col_id = lax.broadcasted_iota(jnp.int32, (rows, cols), 1)
     density = density_ref[...]
+    half_density = drude_gain * density
     hy_step = step_ref[...]
     inverse = jnp.where(hy_step > 0.0, time_step / (1.0 + high_contrast * density), 0.0)
     sense_ref[...] = jnp.zeros((rows, cols), jnp.float32)
@@ -99,12 +113,12 @@
             field_hy = jnp.zeros((rows, cols), jnp.float32)
             current = jnp.zeros((rows, cols), jnp.float32)
             for turn in range(ITERS):
-                e_up = jnp.where(row_id < rows - 1, pltpu.roll(field_e, rows - 1, 0), 0.0)
+                e_up = pltpu.roll(field_e, rows - 1, 0)
                 e_right = jnp.where(col_id < cols - 1, pltpu.roll(field_e, cols - 1, 1), 0.0)
                 field_hx = field_hx - time_step * (e_right - field_e)
                 field_hy = field_hy + hy_step * (e_up - field_e)
-                current = drude_decay * current + drude_gain * density * field_e
-                hy_down = jnp.where(row_id > 0, pltpu.roll(field_hy, 1, 0), 0.0)
+                current = drude_decay * current + half_density * field_e
+                hy_down = pltpu.roll(field_hy, 1, 0)
                 hx_left = jnp.where(col_id > 0, pltpu.roll(field_hx, 1, 1), 0.0)
                 field_e = (
                     field_e
@@ -153,7 +167,12 @@
             jax.ShapeDtypeStruct((waves, rows, cols), jnp.float32),
             jax.ShapeDtypeStruct((chunks, block_rows, 128), jnp.float32),
         ),
-        in_specs=[pl.BlockSpec(memory_space=smem)] + [pl.BlockSpec(memory_space=vmem)] * 8,
+        in_specs=[pl.BlockSpec(memory_space=smem)]
+        + [pl.BlockSpec(memory_space=vmem)] * 2
+        + [pl.BlockSpec(memory_space=pl.ANY)] * 2
+        + [pl.BlockSpec(memory_space=vmem)]
+        + [pl.BlockSpec(memory_space=pl.ANY)] * 2
+        + [pl.BlockSpec(memory_space=vmem)],
         out_specs=(pl.BlockSpec(memory_space=vmem), pl.BlockSpec(memory_space=vmem)),
         scratch_shapes=[
             pltpu.VMEM((runs, waves, rows, cols), jnp.float32),
@@ -162,6 +181,11 @@
             pltpu.VMEM((ITERS, rows, cols), jnp.float32),
             pltpu.VMEM((rows, cols), jnp.float32),
             pltpu.VMEM((8, cols), jnp.float32),
+            pltpu.VMEM(src_above.shape, jnp.float32),
+            pltpu.VMEM(src_below.shape, jnp.float32),
+            pltpu.VMEM(dens_above.shape, jnp.float32),
+            pltpu.VMEM(dens_below.shape, jnp.float32),
+            pltpu.SemaphoreType.DMA((4,)),
         ],
     )(drive, fwd, adj, src_above, src_below, dens, dens_above, dens_below, matched)
 

time: 54 us -> 54.8 us (1.015)
  Pallas kernels: 6.65 us -> 7.48 us
    pallas_call x1, Pallas kernels: 6.65 us -> 7.48 us  [march(): pl.pallas_call(march_kernel, out_shape=(jax.ShapeDtypeStruct((waves, rows...]
  transfers between devices with their start and end apart: 6 -> 6, of which waited for: 2 -> 2; matrix products, arithmetic and copies ran while one was open for 14% -> 13% of each run, Pallas kernels for 0% -> 0%
where the time goes in v9:
time: 54.8 us; the launch traced here: 54.4 us
  starting transfers between devices  26.1 us (48%)
  waiting for transfers between devices  9.28 us (17%)
  Pallas kernels  7.48 us (14%)
  other arithmetic  5.46 us (10%)
  local copies, waits for them, and re-layouts  4.96 us (9%)
  between operations  0.84 us (2%)
    ppermute x4, starting transfers between devices, from_behind(): lax.ppermute(value, axis, [(source, source + steps) for source in range(f...  12.1 us
    pallas_call x1, Pallas kernels, march(): pl.pallas_call(march_kernel, out_shape=(jax.ShapeDtypeStruct((waves, rows...  7.48 us
    all_to_all x1, starting transfers between devices, gather_columns(): pieces = lax.all_to_all(copies, axis, 0, 0, tiled=True)  7.33 us
    all_to_all x1, starting transfers between devices, shards(): lax.all_to_all(pieces.reshape(count, chunks // count, block_rows, span).t...  6.66 us
    all_to_all x1, waiting for transfers between devices, shards(): lax.all_to_all(pieces.reshape(count, chunks // count, block_rows, span).t...  4.76 us
    ppermute x4, waiting for transfers between devices, from_behind(): lax.ppermute(value, axis, [(source, source + steps) for source in range(f...  4.51 us
    slice x1, local copies, waits for them, and re-layouts, shards(): return (final[:, HALO:HALO + cells_x], density_grad)  1.77 us
    unnamed x14, local copies, waits for them, and re-layouts  1.44 us
  transfers between devices with their start and end apart: 6, of which 2 were waited for; matrix products, arithmetic and copies ran while one was open for 13% of the time, Pallas kernels for 0%

profile of v9, /device:TPU:25, one launch (start us, length us, event | category | flops | bytes accessed | tf_op | source)
XLA Modules:
  0.0 54.4 jit_solution(13291677752597574374)
XLA Ops:
  0.6 0.0 copy-start.1
  0.6 1.3 %broadcast_in_dim.55 = f32[8,2,128]{2,1,0:T(2,128)} broadcast(f32[2,128]{1,0:T(2,128)} %param.6), dimensions={1,2} | broadcast | bytes 9216 | tf_op jit(solution)/shard_map/broadcast_in_dim | solution.py:35
  2.0 7.3 %all-to-all-start = ((f32[8,2,128]{2,1,0:T(2,128)}), f32[8,2,128]{2,1,0:T(2,128)S(1)}, u32[]{:S(2)}, u32[]{:S(2)}) async-start(f32[8,2,128]{2,1,0:T(2,128)} %broadcast_in_dim.55), calls=%async_computation | async-start | bytes 16384 | tf_op jit(solution)/shard_map/all_to_all | solution.py:36
  9.3 1.3 %pad_maximum_fusion = (f32[2,2,4,4096]{3,2,1,0:T(4,128)S(1)}, f32[2,2,4,4096]{3,2,1,0:T(4,128)S(1)}) fusion(f32[1,2,8,4096]{3,2,1,0:T(8,128)} %bitcast.43, f32[1,2,8,4096]{3,2,1,0:T(8,128)} %bitcast.42), kind=kLoop, calls=%fused_computation.25 | loop fusion | flops 131072 | bytes 1048576 | tf_op jit(solution)/shard_map/stack | solution.py:194
  10.7 0.0 copy-start.2
  10.7 3.0 %collective-permute-start.1 = (f32[2,2,4,4096]{3,2,1,0:T(4,128)S(1)}, f32[2,2,4,4096]{3,2,1,0:T(4,128)S(1)}, u32[]{:S(2)}, u32[]{:S(2)}) collective-permute-start(f32[2,2,4,4096]{3,2,1,0:T(4,128)S(1)} %get-tuple-element.12), channel_id=1, source_target_pairs={{1,0},{2,1},{3,2},{4,3},{5,4},{6,5},{7,6},{8,7},{9,8},{10,9},{11,1... | collective-permute-start | bytes 786440 | tf_op jit(solution)/shard_map/ppermute | solution.py:24
  13.7 4.8 %collective-permute-start = (f32[2,2,4,4096]{3,2,1,0:T(4,128)S(1)}, f32[2,2,4,4096]{3,2,1,0:T(4,128)S(1)}, u32[]{:S(2)}, u32[]{:S(2)}) collective-permute-start(f32[2,2,4,4096]{3,2,1,0:T(4,128)S(1)} %get-tuple-element.13), channel_id=1, source_target_pairs={{0,1},{1,2},{2,3},{3,4},{4,5},{5,6},{6,7},{7,8},{8,9},{9,10},{10,1... | collective-permute-start | bytes 786440 | tf_op jit(solution)/shard_map/ppermute | solution.py:24
  18.5 0.7 %sine_bitcast_fusion.3 = (f32[1,2]{1,0:T(1,128)S(1)}, f32[1,2]{1,0:T(1,128)S(1)}, f32[1,2]{1,0:T(1,128)S(1)}, f32[1,2]{1,0:T(1,128)S(1)}) fusion(f32[2]{0:T(128)} %param.11), kind=kLoop, calls=%fused_computation.65 | loop fusion | flops 6 | bytes 40 | tf_op jit(solution)/shard_map/stack | solution.py:209
  19.3 0.5 fusion.2
  19.9 0.6 %pad_maximum_fusion.1.drive_ref = f32[4,2]{1,0:T(4,128)} fusion(f32[1,2]{1,0:T(1,128)S(1)} %get-tuple-element.36, f32[1,2]{1,0:T(1,128)S(1)} %get-tuple-element.37, f32[1,2]{1,0:T(1,128)S(1)} %get-tuple-element.35, f32[1,2]{1,0:T(1,128)S(1)} %get-tuple-element.34), kind=kLoop, calls=%fused_computation.59 | loop fusion | flops 24 | bytes 64 | tf_op jit(solution)/shard_map/stack | solution.py:209
  20.5 0.5 select_add_fusion.matched_ref
  21.0 0.0 all-to-all-done
  21.0 0.1 pad_slice_fusion.4
  21.1 0.1 pad_slice_fusion.8
  21.2 0.1 stack.69
  21.3 0.2 fusion.9
  21.6 0.4 multiply_reduce_fusion.1
  22.1 1.9 %collective-permute-start.2 = (f32[3,4096]{1,0:T(4,128)S(1)}, f32[3,4096]{1,0:T(4,128)S(1)}, u32[]{:S(2)}, u32[]{:S(2)}) collective-permute-start(f32[3,4096]{1,0:T(4,128)S(1)} %concatenate.6), channel_id=1, source_target_pairs={{0,1},{1,2},{2,3},{3,4},{4,5},{5,6},{6,7},{7,8},{8,9},{9,10},{10,1... | collective-permute-start | bytes 147464 | tf_op jit(solution)/shard_map/ppermute | solution.py:24
  24.0 2.4 %collective-permute-start.3 = (f32[3,4096]{1,0:T(4,128)S(1)}, f32[3,4096]{1,0:T(4,128)S(1)}, u32[]{:S(2)}, u32[]{:S(2)}) collective-permute-start(f32[3,4096]{1,0:T(4,128)S(1)} %concatenate.7), channel_id=1, source_target_pairs={{1,0},{2,1},{3,2},{4,3},{5,4},{6,5},{7,6},{8,7},{9,8},{10,9},{11,1... | collective-permute-start | bytes 147464 | tf_op jit(solution)/shard_map/ppermute | solution.py:24
  26.4 0.8 %multiply_reduce_fusion.dens_ref = f32[8,4096]{1,0:T(8,128)} fusion(f32[10,8,4096]{2,1,0:T(8,128)S(1)} %select_add_fusion.matched_ref, f32[10,4096]{1,0:T(8,128)S(1)} %mul.44), kind=kLoop, calls=%fused_computation | loop fusion | flops 622592 | bytes 1605632 | tf_op jit(solution)/shard_map/reduce_sum | solution.py:227
  27.2 0.0 collective-permute-done.2.dens_above_hbm
  27.2 4.5 %collective-permute-done.3.dens_below_hbm = f32[3,4096]{1,0:T(4,128)S(1)} collective-permute-done((f32[3,4096]{1,0:T(4,128)S(1)}, f32[3,4096]{1,0:T(4,128)S(1)}, u32[]{:S(2)}, u32[]{:S(2)}) %collective-permute-start.3) | collective-permute-done | bytes 49184 | tf_op jit(solution)/shard_map/ppermute | solution.py:24
  31.7 0.0 collective-permute-done.1.src_below_hbm
  31.7 0.0 collective-permute-done.src_above_hbm
  31.7 0.6 %copy-done.6 = f32[3,4096]{1,0:T(4,128)} copy-done((f32[3,4096]{1,0:T(4,128)}, f32[3,4096]{1,0:T(4,128)S(1)}, u32[]{:S(2)}) %copy-start.6) | copy-done | bytes 49176
  32.3 0.1 copy-done.3
  32.4 0.7 %copy-done.4 = f32[2,2,4,4096]{3,2,1,0:T(4,128)} copy-done((f32[2,2,4,4096]{3,2,1,0:T(4,128)}, f32[2,2,4,4096]{3,2,1,0:T(4,128)S(1)}, u32[]{:S(2)}) %copy-start.4) | copy-done | bytes 262168
  33.1 7.5 %shard_map.77 = (f32[2,16,4096]{2,1,0:T(8,128)}, f32[8,2,128]{2,1,0:T(2,128)}) custom-call(f32[4,2]{1,0:T(4,128)} %pad_maximum_fusion.1.drive_ref, f32[2,8,4096]{2,1,0:T(8,128)} %fwd_ref.1, f32[2,8,4096]{2,1,0:T(8,128)} %adj_ref.1, f32[2,2,4,4096]{3,2,1,0:T(4,128)} %copy-done.4, f32[2,2,4,4096]{3,2,1,0:T(4,128)} %copy-done.3, ...), custom_call_target="tpu_custom_call" | custom-call | tf_op jit(solution)/shard_map/pallas_call | solution.py:164
  40.6 6.7 %all-to-all-start.1 = ((f32[8,2,128]{2,1,0:T(2,128)}), f32[8,2,128]{2,1,0:T(2,128)S(1)}, u32[]{:S(2)}, u32[]{:S(2)}) async-start(f32[8,2,128]{2,1,0:T(2,128)} %get-tuple-element.9), calls=%async_computation.1 | async-start | bytes 16384 | tf_op jit(solution)/shard_map/all_to_all | solution.py:232
  47.3 1.8 %slice.107 = f32[2,8,4096]{2,1,0:T(8,128)} slice(f32[2,16,4096]{2,1,0:T(8,128)} %get-tuple-element.8), slice={[0:2], [4:12], [0:4096]} | slice | bytes 524288 | tf_op jit(solution)/shard_map/slice | solution.py:236
  49.0 4.8 %all-to-all-done.1 = f32[8,2,128]{2,1,0:T(2,128)S(1)} async-done(((f32[8,2,128]{2,1,0:T(2,128)}), f32[8,2,128]{2,1,0:T(2,128)S(1)}, u32[]{:S(2)}, u32[]{:S(2)}) %all-to-all-start.1) | async-done | bytes 8224 | tf_op jit(solution)/shard_map/all_to_all | solution.py:232
  53.8 0.6 %reduce_sum.39 = f32[2,128]{1,0:T(2,128)} reduce(f32[8,2,128]{2,1,0:T(2,128)S(1)} %all-to-all-done.1, f32[]{:T(128)} %constant.66.clone.1), dimensions={0}, to_apply=%region_3.4 | reduce | flops 1792 | bytes 9220 | tf_op jit(solution)/shard_map/reduce_sum | solution.py:235
  (20 shorter events, 0.2 us)
Async XLA Ops:
  0.6 18.6 %copy-start.1 = (s32[4,8,4096]{2,1,0:T(8,128)S(1)}, s32[4,8,4096]{2,1,0:T(8,128)}, u32[]{:S(2)}) copy-start(s32[4,8,4096]{2,1,0:T(8,128)} %param.7) | copy-start | bytes 1572868
  2.0 19.0 %all-to-all-start = ((f32[8,2,128]{2,1,0:T(2,128)}), f32[8,2,128]{2,1,0:T(2,128)S(1)}, u32[]{:S(2)}, u32[]{:S(2)}) async-start(f32[8,2,128]{2,1,0:T(2,128)} %broadcast_in_dim.55), calls=%async_computation | async-start | bytes 16384 | tf_op jit(solution)/shard_map/all_to_all | solution.py:36
  10.7 9.2 %copy-start.2 = (bf16[4,8,4096]{2,1,0:T(8,128)(2,1)S(1)}, bf16[4,8,4096]{2,1,0:T(8,128)(2,1)}, u32[]{:S(2)}) copy-start(bf16[4,8,4096]{2,1,0:T(8,128)(2,1)} %param.8) | copy-start | bytes 786436
  10.7 21.0 %collective-permute-start.1 = (f32[2,2,4,4096]{3,2,1,0:T(4,128)S(1)}, f32[2,2,4,4096]{3,2,1,0:T(4,128)S(1)}, u32[]{:S(2)}, u32[]{:S(2)}) collective-permute-start(f32[2,2,4,4096]{3,2,1,0:T(4,128)S(1)} %get-tuple-element.12), channel_id=1, source_target_pairs={{1,0},{2,1},{3,2},{4,3},{5,4},{6,5},{7,6},{8,7},{9,8},{10,9},{11,1... | collective-permute-start | bytes 786440 | tf_op jit(solution)/shard_map/ppermute | solution.py:24
  13.7 18.0 %collective-permute-start = (f32[2,2,4,4096]{3,2,1,0:T(4,128)S(1)}, f32[2,2,4,4096]{3,2,1,0:T(4,128)S(1)}, u32[]{:S(2)}, u32[]{:S(2)}) collective-permute-start(f32[2,2,4,4096]{3,2,1,0:T(4,128)S(1)} %get-tuple-element.13), channel_id=1, source_target_pairs={{0,1},{1,2},{2,3},{3,4},{4,5},{5,6},{6,7},{7,8},{8,9},{9,10},{10,1... | collective-permute-start | bytes 786440 | tf_op jit(solution)/shard_map/ppermute | solution.py:24
  21.0 6.2 %copy-start = (f32[10,8,4096]{2,1,0:T(8,128)}, f32[10,8,4096]{2,1,0:T(8,128)S(1)}, u32[]{:S(2)}) copy-start(f32[10,8,4096]{2,1,0:T(8,128)S(1)} %select_add_fusion.matched_ref) | copy-start | bytes 3932164
  22.1 5.1 %collective-permute-start.2 = (f32[3,4096]{1,0:T(4,128)S(1)}, f32[3,4096]{1,0:T(4,128)S(1)}, u32[]{:S(2)}, u32[]{:S(2)}) collective-permute-start(f32[3,4096]{1,0:T(4,128)S(1)} %concatenate.6), channel_id=1, source_target_pairs={{0,1},{1,2},{2,3},{3,4},{4,5},{5,6},{6,7},{7,8},{8,9},{9,10},{10,1... | collective-permute-start | bytes 147464 | tf_op jit(solution)/shard_map/ppermute | solution.py:24
  24.0 7.7 %collective-permute-start.3 = (f32[3,4096]{1,0:T(4,128)S(1)}, f32[3,4096]{1,0:T(4,128)S(1)}, u32[]{:S(2)}, u32[]{:S(2)}) collective-permute-start(f32[3,4096]{1,0:T(4,128)S(1)} %concatenate.7), channel_id=1, source_target_pairs={{1,0},{2,1},{3,2},{4,3},{5,4},{6,5},{7,6},{8,7},{9,8},{10,9},{11,1... | collective-permute-start | bytes 147464 | tf_op jit(solution)/shard_map/ppermute | solution.py:24
  27.2 4.5 %copy-start.5 = (f32[3,4096]{1,0:T(4,128)}, f32[3,4096]{1,0:T(4,128)S(1)}, u32[]{:S(2)}) copy-start(f32[3,4096]{1,0:T(4,128)S(1)} %collective-permute-done.2.dens_above_hbm) | copy-start | bytes 147460
  31.7 0.6 %copy-start.6 = (f32[3,4096]{1,0:T(4,128)}, f32[3,4096]{1,0:T(4,128)S(1)}, u32[]{:S(2)}) copy-start(f32[3,4096]{1,0:T(4,128)S(1)} %collective-permute-done.3.dens_below_hbm) | copy-start | bytes 147460
  31.7 0.7 %copy-start.3 = (f32[2,2,4,4096]{3,2,1,0:T(4,128)}, f32[2,2,4,4096]{3,2,1,0:T(4,128)S(1)}, u32[]{:S(2)}) copy-start(f32[2,2,4,4096]{3,2,1,0:T(4,128)S(1)} %collective-permute-done.1.src_below_hbm) | copy-start | bytes 786436
  32.4 0.7 %copy-start.4 = (f32[2,2,4,4096]{3,2,1,0:T(4,128)}, f32[2,2,4,4096]{3,2,1,0:T(4,128)S(1)}, u32[]{:S(2)}) copy-start(f32[2,2,4,4096]{3,2,1,0:T(4,128)S(1)} %collective-permute-done.src_above_hbm) | copy-start | bytes 786436
  40.6 13.2 %all-to-all-start.1 = ((f32[8,2,128]{2,1,0:T(2,128)}), f32[8,2,128]{2,1,0:T(2,128)S(1)}, u32[]{:S(2)}, u32[]{:S(2)}) async-start(f32[8,2,128]{2,1,0:T(2,128)} %get-tuple-element.9), calls=%async_computation.1 | async-start | bytes 16384 | tf_op jit(solution)/shard_map/all_to_all | solution.py:232

commit v10 on v8

--- a/solution.py
+++ b/solution.py
@@ -89,6 +89,7 @@
     row_id = lax.broadcasted_iota(jnp.int32, (rows, cols), 0)
     col_id = lax.broadcasted_iota(jnp.int32, (rows, cols), 1)
     density = density_ref[...]
+    half_density = drude_gain * density
     hy_step = step_ref[...]
     inverse = jnp.where(hy_step > 0.0, time_step / (1.0 + high_contrast * density), 0.0)
     sense_ref[...] = jnp.zeros((rows, cols), jnp.float32)
@@ -103,7 +104,7 @@
                 e_right = jnp.where(col_id < cols - 1, pltpu.roll(field_e, cols - 1, 1), 0.0)
                 field_hx = field_hx - time_step * (e_right - field_e)
                 field_hy = field_hy + hy_step * (e_up - field_e)
-                current = drude_decay * current + drude_gain * density * field_e
+                current = drude_decay * current + half_density * field_e
                 hy_down = jnp.where(row_id > 0, pltpu.roll(field_hy, 1, 0), 0.0)
                 hx_left = jnp.where(col_id > 0, pltpu.roll(field_hx, 1, 1), 0.0)
                 field_e = (

time: 54 us -> 53.9 us (level)
  no operation moved by 1% of the time
where the time goes in v10:
time: 53.9 us; the launch traced here: 53.5 us
  starting transfers between devices  26.1 us (48%)
  waiting for transfers between devices  9.28 us (17%)
  Pallas kernels  6.64 us (12%)
  other arithmetic  5.46 us (10%)
  local copies, waits for them, and re-layouts  4.96 us (9%)
  between operations  0.83 us (2%)
    ppermute x4, starting transfers between devices, from_behind(): lax.ppermute(value, axis, [(source, source + steps) for source in range(f...  12.1 us
    all_to_all x1, starting transfers between devices, gather_columns(): pieces = lax.all_to_all(copies, axis, 0, 0, tiled=True)  7.33 us
    all_to_all x1, starting transfers between devices, shards(): lax.all_to_all(pieces.reshape(count, chunks // count, block_rows, span).t...  6.65 us
    pallas_call x1, Pallas kernels, march(): pl.pallas_call(march_kernel, out_shape=(jax.ShapeDtypeStruct((waves, rows...  6.64 us
    all_to_all x1, waiting for transfers between devices, shards(): lax.all_to_all(pieces.reshape(count, chunks // count, block_rows, span).t...  4.76 us
    ppermute x4, waiting for transfers between devices, from_behind(): lax.ppermute(value, axis, [(source, source + steps) for source in range(f...  4.51 us
    slice x1, local copies, waits for them, and re-layouts, shards(): return (final[:, HALO:HALO + cells_x], density_grad)  1.77 us
    unnamed x14, local copies, waits for them, and re-layouts  1.44 us
  transfers between devices with their start and end apart: 6, of which 2 were waited for; matrix products, arithmetic and copies ran while one was open for 14% of the time, Pallas kernels for 0%

profile of v10, /device:TPU:25, one launch (start us, length us, event | category | flops | bytes accessed | tf_op | source)
XLA Modules:
  0.0 53.5 jit_solution(10470924522134276601)
XLA Ops:
  0.6 0.0 copy-start.1
  0.6 1.3 %broadcast_in_dim.55 = f32[8,2,128]{2,1,0:T(2,128)} broadcast(f32[2,128]{1,0:T(2,128)} %param.6), dimensions={1,2} | broadcast | bytes 9216 | tf_op jit(solution)/shard_map/broadcast_in_dim | solution.py:35
  2.0 7.3 %all-to-all-start = ((f32[8,2,128]{2,1,0:T(2,128)}), f32[8,2,128]{2,1,0:T(2,128)S(1)}, u32[]{:S(2)}, u32[]{:S(2)}) async-start(f32[8,2,128]{2,1,0:T(2,128)} %broadcast_in_dim.55), calls=%async_computation | async-start | bytes 16384 | tf_op jit(solution)/shard_map/all_to_all | solution.py:36
  9.3 1.3 %pad_maximum_fusion = (f32[2,2,4,4096]{3,2,1,0:T(4,128)S(1)}, f32[2,2,4,4096]{3,2,1,0:T(4,128)S(1)}) fusion(f32[1,2,8,4096]{3,2,1,0:T(8,128)} %bitcast.43, f32[1,2,8,4096]{3,2,1,0:T(8,128)} %bitcast.42), kind=kLoop, calls=%fused_computation.25 | loop fusion | flops 131072 | bytes 1048576 | tf_op jit(solution)/shard_map/stack | solution.py:171
  10.7 0.0 copy-start.2
  10.7 3.0 %collective-permute-start.1 = (f32[2,2,4,4096]{3,2,1,0:T(4,128)S(1)}, f32[2,2,4,4096]{3,2,1,0:T(4,128)S(1)}, u32[]{:S(2)}, u32[]{:S(2)}) collective-permute-start(f32[2,2,4,4096]{3,2,1,0:T(4,128)S(1)} %get-tuple-element.12), channel_id=1, source_target_pairs={{1,0},{2,1},{3,2},{4,3},{5,4},{6,5},{7,6},{8,7},{9,8},{10,9},{11,1... | collective-permute-start | bytes 786440 | tf_op jit(solution)/shard_map/ppermute | solution.py:24
  13.7 4.8 %collective-permute-start = (f32[2,2,4,4096]{3,2,1,0:T(4,128)S(1)}, f32[2,2,4,4096]{3,2,1,0:T(4,128)S(1)}, u32[]{:S(2)}, u32[]{:S(2)}) collective-permute-start(f32[2,2,4,4096]{3,2,1,0:T(4,128)S(1)} %get-tuple-element.13), channel_id=1, source_target_pairs={{0,1},{1,2},{2,3},{3,4},{4,5},{5,6},{6,7},{7,8},{8,9},{9,10},{10,1... | collective-permute-start | bytes 786440 | tf_op jit(solution)/shard_map/ppermute | solution.py:24
  18.5 0.7 %sine_bitcast_fusion.3 = (f32[1,2]{1,0:T(1,128)S(1)}, f32[1,2]{1,0:T(1,128)S(1)}, f32[1,2]{1,0:T(1,128)S(1)}, f32[1,2]{1,0:T(1,128)S(1)}) fusion(f32[2]{0:T(128)} %param.11), kind=kLoop, calls=%fused_computation.65 | loop fusion | flops 6 | bytes 40 | tf_op jit(solution)/shard_map/stack | solution.py:186
  19.3 0.5 fusion.2
  19.9 0.6 %pad_maximum_fusion.1.drive_ref = f32[4,2]{1,0:T(4,128)} fusion(f32[1,2]{1,0:T(1,128)S(1)} %get-tuple-element.36, f32[1,2]{1,0:T(1,128)S(1)} %get-tuple-element.37, f32[1,2]{1,0:T(1,128)S(1)} %get-tuple-element.35, f32[1,2]{1,0:T(1,128)S(1)} %get-tuple-element.34), kind=kLoop, calls=%fused_computation.59 | loop fusion | flops 24 | bytes 64 | tf_op jit(solution)/shard_map/stack | solution.py:186
  20.5 0.5 select_add_fusion.matched_ref
  21.0 0.0 all-to-all-done
  21.0 0.1 pad_slice_fusion.4
  21.1 0.1 pad_slice_fusion.8
  21.2 0.1 stack.69
  21.3 0.2 fusion.9
  21.6 0.4 multiply_reduce_fusion.1
  22.1 1.9 %collective-permute-start.2 = (f32[3,4096]{1,0:T(4,128)S(1)}, f32[3,4096]{1,0:T(4,128)S(1)}, u32[]{:S(2)}, u32[]{:S(2)}) collective-permute-start(f32[3,4096]{1,0:T(4,128)S(1)} %concatenate.6), channel_id=1, source_target_pairs={{0,1},{1,2},{2,3},{3,4},{4,5},{5,6},{6,7},{7,8},{8,9},{9,10},{10,1... | collective-permute-start | bytes 147464 | tf_op jit(solution)/shard_map/ppermute | solution.py:24
  24.0 2.4 %collective-permute-start.3 = (f32[3,4096]{1,0:T(4,128)S(1)}, f32[3,4096]{1,0:T(4,128)S(1)}, u32[]{:S(2)}, u32[]{:S(2)}) collective-permute-start(f32[3,4096]{1,0:T(4,128)S(1)} %concatenate.7), channel_id=1, source_target_pairs={{1,0},{2,1},{3,2},{4,3},{5,4},{6,5},{7,6},{8,7},{9,8},{10,9},{11,1... | collective-permute-start | bytes 147464 | tf_op jit(solution)/shard_map/ppermute | solution.py:24
  26.4 0.8 %multiply_reduce_fusion.dens_ref = f32[8,4096]{1,0:T(8,128)} fusion(f32[10,8,4096]{2,1,0:T(8,128)S(1)} %select_add_fusion.matched_ref, f32[10,4096]{1,0:T(8,128)S(1)} %mul.44), kind=kLoop, calls=%fused_computation | loop fusion | flops 622592 | bytes 1605632 | tf_op jit(solution)/shard_map/reduce_sum | solution.py:204
  27.2 0.0 collective-permute-done.2.dens_above_ref
  27.2 4.5 %collective-permute-done.3.dens_below_ref = f32[3,4096]{1,0:T(4,128)S(1)} collective-permute-done((f32[3,4096]{1,0:T(4,128)S(1)}, f32[3,4096]{1,0:T(4,128)S(1)}, u32[]{:S(2)}, u32[]{:S(2)}) %collective-permute-start.3) | collective-permute-done | bytes 49184 | tf_op jit(solution)/shard_map/ppermute | solution.py:24
  31.7 0.0 collective-permute-done.1.src_below_ref
  31.7 0.0 collective-permute-done.src_above_ref
  31.7 0.6 %copy-done.6 = f32[3,4096]{1,0:T(4,128)} copy-done((f32[3,4096]{1,0:T(4,128)}, f32[3,4096]{1,0:T(4,128)S(1)}, u32[]{:S(2)}) %copy-start.6) | copy-done | bytes 49176
  32.3 0.1 copy-done.3
  32.4 0.7 %copy-done.4 = f32[2,2,4,4096]{3,2,1,0:T(4,128)} copy-done((f32[2,2,4,4096]{3,2,1,0:T(4,128)}, f32[2,2,4,4096]{3,2,1,0:T(4,128)S(1)}, u32[]{:S(2)}) %copy-start.4) | copy-done | bytes 262168
  33.1 6.6 %shard_map.77 = (f32[2,16,4096]{2,1,0:T(8,128)}, f32[8,2,128]{2,1,0:T(2,128)}) custom-call(f32[4,2]{1,0:T(4,128)} %pad_maximum_fusion.1.drive_ref, f32[2,8,4096]{2,1,0:T(8,128)} %fwd_ref.1, f32[2,8,4096]{2,1,0:T(8,128)} %adj_ref.1, f32[2,2,4,4096]{3,2,1,0:T(4,128)} %copy-done.4, f32[2,2,4,4096]{3,2,1,0:T(4,128)} %copy-done.3, ...), custom_call_target="tpu_custom_call" | custom-call | tf_op jit(solution)/shard_map/pallas_call | solution.py:151
  39.8 6.6 %all-to-all-start.1 = ((f32[8,2,128]{2,1,0:T(2,128)}), f32[8,2,128]{2,1,0:T(2,128)S(1)}, u32[]{:S(2)}, u32[]{:S(2)}) async-start(f32[8,2,128]{2,1,0:T(2,128)} %get-tuple-element.9), calls=%async_computation.1 | async-start | bytes 16384 | tf_op jit(solution)/shard_map/all_to_all | solution.py:209
  46.4 1.8 %slice.107 = f32[2,8,4096]{2,1,0:T(8,128)} slice(f32[2,16,4096]{2,1,0:T(8,128)} %get-tuple-element.8), slice={[0:2], [4:12], [0:4096]} | slice | bytes 524288 | tf_op jit(solution)/shard_map/slice | solution.py:213
  48.2 4.8 %all-to-all-done.1 = f32[8,2,128]{2,1,0:T(2,128)S(1)} async-done(((f32[8,2,128]{2,1,0:T(2,128)}), f32[8,2,128]{2,1,0:T(2,128)S(1)}, u32[]{:S(2)}, u32[]{:S(2)}) %all-to-all-start.1) | async-done | bytes 8224 | tf_op jit(solution)/shard_map/all_to_all | solution.py:209
  52.9 0.6 %reduce_sum.39 = f32[2,128]{1,0:T(2,128)} reduce(f32[8,2,128]{2,1,0:T(2,128)S(1)} %all-to-all-done.1, f32[]{:T(128)} %constant.66.clone.1), dimensions={0}, to_apply=%region_3.4 | reduce | flops 1792 | bytes 9220 | tf_op jit(solution)/shard_map/reduce_sum | solution.py:212
  (20 shorter events, 0.2 us)
Async XLA Ops:
  0.6 18.6 %copy-start.1 = (s32[4,8,4096]{2,1,0:T(8,128)S(1)}, s32[4,8,4096]{2,1,0:T(8,128)}, u32[]{:S(2)}) copy-start(s32[4,8,4096]{2,1,0:T(8,128)} %param.7) | copy-start | bytes 1572868
  2.0 19.0 %all-to-all-start = ((f32[8,2,128]{2,1,0:T(2,128)}), f32[8,2,128]{2,1,0:T(2,128)S(1)}, u32[]{:S(2)}, u32[]{:S(2)}) async-start(f32[8,2,128]{2,1,0:T(2,128)} %broadcast_in_dim.55), calls=%async_computation | async-start | bytes 16384 | tf_op jit(solution)/shard_map/all_to_all | solution.py:36
  10.7 9.2 %copy-start.2 = (bf16[4,8,4096]{2,1,0:T(8,128)(2,1)S(1)}, bf16[4,8,4096]{2,1,0:T(8,128)(2,1)}, u32[]{:S(2)}) copy-start(bf16[4,8,4096]{2,1,0:T(8,128)(2,1)} %param.8) | copy-start | bytes 786436
  10.7 21.0 %collective-permute-start.1 = (f32[2,2,4,4096]{3,2,1,0:T(4,128)S(1)}, f32[2,2,4,4096]{3,2,1,0:T(4,128)S(1)}, u32[]{:S(2)}, u32[]{:S(2)}) collective-permute-start(f32[2,2,4,4096]{3,2,1,0:T(4,128)S(1)} %get-tuple-element.12), channel_id=1, source_target_pairs={{1,0},{2,1},{3,2},{4,3},{5,4},{6,5},{7,6},{8,7},{9,8},{10,9},{11,1... | collective-permute-start | bytes 786440 | tf_op jit(solution)/shard_map/ppermute | solution.py:24
  13.7 18.0 %collective-permute-start = (f32[2,2,4,4096]{3,2,1,0:T(4,128)S(1)}, f32[2,2,4,4096]{3,2,1,0:T(4,128)S(1)}, u32[]{:S(2)}, u32[]{:S(2)}) collective-permute-start(f32[2,2,4,4096]{3,2,1,0:T(4,128)S(1)} %get-tuple-element.13), channel_id=1, source_target_pairs={{0,1},{1,2},{2,3},{3,4},{4,5},{5,6},{6,7},{7,8},{8,9},{9,10},{10,1... | collective-permute-start | bytes 786440 | tf_op jit(solution)/shard_map/ppermute | solution.py:24
  21.0 6.2 %copy-start = (f32[10,8,4096]{2,1,0:T(8,128)}, f32[10,8,4096]{2,1,0:T(8,128)S(1)}, u32[]{:S(2)}) copy-start(f32[10,8,4096]{2,1,0:T(8,128)S(1)} %select_add_fusion.matched_ref) | copy-start | bytes 3932164
  22.1 5.1 %collective-permute-start.2 = (f32[3,4096]{1,0:T(4,128)S(1)}, f32[3,4096]{1,0:T(4,128)S(1)}, u32[]{:S(2)}, u32[]{:S(2)}) collective-permute-start(f32[3,4096]{1,0:T(4,128)S(1)} %concatenate.6), channel_id=1, source_target_pairs={{0,1},{1,2},{2,3},{3,4},{4,5},{5,6},{6,7},{7,8},{8,9},{9,10},{10,1... | collective-permute-start | bytes 147464 | tf_op jit(solution)/shard_map/ppermute | solution.py:24
  24.0 7.7 %collective-permute-start.3 = (f32[3,4096]{1,0:T(4,128)S(1)}, f32[3,4096]{1,0:T(4,128)S(1)}, u32[]{:S(2)}, u32[]{:S(2)}) collective-permute-start(f32[3,4096]{1,0:T(4,128)S(1)} %concatenate.7), channel_id=1, source_target_pairs={{1,0},{2,1},{3,2},{4,3},{5,4},{6,5},{7,6},{8,7},{9,8},{10,9},{11,1... | collective-permute-start | bytes 147464 | tf_op jit(solution)/shard_map/ppermute | solution.py:24
  27.2 4.5 %copy-start.5 = (f32[3,4096]{1,0:T(4,128)}, f32[3,4096]{1,0:T(4,128)S(1)}, u32[]{:S(2)}) copy-start(f32[3,4096]{1,0:T(4,128)S(1)} %collective-permute-done.2.dens_above_ref) | copy-start | bytes 147460
  31.7 0.6 %copy-start.6 = (f32[3,4096]{1,0:T(4,128)}, f32[3,4096]{1,0:T(4,128)S(1)}, u32[]{:S(2)}) copy-start(f32[3,4096]{1,0:T(4,128)S(1)} %collective-permute-done.3.dens_below_ref) | copy-start | bytes 147460
  31.7 0.7 %copy-start.3 = (f32[2,2,4,4096]{3,2,1,0:T(4,128)}, f32[2,2,4,4096]{3,2,1,0:T(4,128)S(1)}, u32[]{:S(2)}) copy-start(f32[2,2,4,4096]{3,2,1,0:T(4,128)S(1)} %collective-permute-done.1.src_below_ref) | copy-start | bytes 786436
  32.4 0.7 %copy-start.4 = (f32[2,2,4,4096]{3,2,1,0:T(4,128)}, f32[2,2,4,4096]{3,2,1,0:T(4,128)S(1)}, u32[]{:S(2)}) copy-start(f32[2,2,4,4096]{3,2,1,0:T(4,128)S(1)} %collective-permute-done.src_above_ref) | copy-start | bytes 786436
  39.8 13.2 %all-to-all-start.1 = ((f32[8,2,128]{2,1,0:T(2,128)}), f32[8,2,128]{2,1,0:T(2,128)S(1)}, u32[]{:S(2)}, u32[]{:S(2)}) async-start(f32[8,2,128]{2,1,0:T(2,128)} %get-tuple-element.9), calls=%async_computation.1 | async-start | bytes 16384 | tf_op jit(solution)/shard_map/all_to_all | solution.py:209

commit v11 on v10

--- a/solution.py
+++ b/solution.py
@@ -95,23 +95,29 @@
     sense_ref[...] = jnp.zeros((rows, cols), jnp.float32)
     for wave in range(waves):
         for run in range(runs):
-            field_e = jnp.zeros((rows, cols), jnp.float32)
-            field_hx = jnp.zeros((rows, cols), jnp.float32)
-            field_hy = jnp.zeros((rows, cols), jnp.float32)
-            current = jnp.zeros((rows, cols), jnp.float32)
+            field_e = field_hx = field_hy = current = None
             for turn in range(ITERS):
-                e_up = jnp.where(row_id < rows - 1, pltpu.roll(field_e, rows - 1, 0), 0.0)
-                e_right = jnp.where(col_id < cols - 1, pltpu.roll(field_e, cols - 1, 1), 0.0)
-                field_hx = field_hx - time_step * (e_right - field_e)
-                field_hy = field_hy + hy_step * (e_up - field_e)
-                current = drude_decay * current + half_density * field_e
-                hy_down = jnp.where(row_id > 0, pltpu.roll(field_hy, 1, 0), 0.0)
-                hx_left = jnp.where(col_id > 0, pltpu.roll(field_hx, 1, 1), 0.0)
-                field_e = (
-                    field_e
-                    + inverse * (field_hy - hy_down - (field_hx - hx_left) - current)
-                    + drive_ref[turn, wave] * source_ref[run, wave]
-                )
+                drive_term = drive_ref[turn, wave] * source_ref[run, wave]
+                if field_e is None:
+                    field_e = drive_term
+                else:
+                    e_up = jnp.where(row_id < rows - 1, pltpu.roll(field_e, rows - 1, 0), 0.0)
+                    e_right = jnp.where(col_id < cols - 1, pltpu.roll(field_e, cols - 1, 1), 0.0)
+                    if field_hx is None:
+                        field_hx = -time_step * (e_right - field_e)
+                        field_hy = hy_step * (e_up - field_e)
+                        current = half_density * field_e
+                    else:
+                        field_hx = field_hx - time_step * (e_right - field_e)
+                        field_hy = field_hy + hy_step * (e_up - field_e)
+                        current = drude_decay * current + half_density * field_e
+                    hy_down = jnp.where(row_id > 0, pltpu.roll(field_hy, 1, 0), 0.0)
+                    hx_left = jnp.where(col_id > 0, pltpu.roll(field_hx, 1, 1), 0.0)
+                    field_e = (
+                        field_e
+                        + inverse * (field_hy - hy_down - (field_hx - hx_left) - current)
+                        + drive_term
+                    )
                 if run == 0:
                     history_ref[turn] = field_e
                 else:

time: 53.9 us -> 53.8 us (level)
  no operation moved by 1% of the time
where the time goes in v11:
time: 53.8 us; the launch traced here: 53.4 us
  starting transfers between devices  26.1 us (49%)
  waiting for transfers between devices  9.28 us (17%)
  Pallas kernels  6.51 us (12%)
  other arithmetic  5.46 us (10%)
  local copies, waits for them, and re-layouts  4.96 us (9%)
  between operations  0.83 us (2%)
    ppermute x4, starting transfers between devices, from_behind(): lax.ppermute(value, axis, [(source, source + steps) for source in range(f...  12.1 us
    all_to_all x1, starting transfers between devices, gather_columns(): pieces = lax.all_to_all(copies, axis, 0, 0, tiled=True)  7.33 us
    all_to_all x1, starting transfers between devices, shards(): lax.all_to_all(pieces.reshape(count, chunks // count, block_rows, span).t...  6.65 us
    pallas_call x1, Pallas kernels, march(): pl.pallas_call(march_kernel, out_shape=(jax.ShapeDtypeStruct((waves, rows...  6.51 us
    all_to_all x1, waiting for transfers between devices, shards(): lax.all_to_all(pieces.reshape(count, chunks // count, block_rows, span).t...  4.76 us
    ppermute x4, waiting for transfers between devices, from_behind(): lax.ppermute(value, axis, [(source, source + steps) for source in range(f...  4.51 us
    slice x1, local copies, waits for them, and re-layouts, shards(): return (final[:, HALO:HALO + cells_x], density_grad)  1.77 us
    unnamed x14, local copies, waits for them, and re-layouts  1.44 us
  transfers between devices with their start and end apart: 6, of which 2 were waited for; matrix products, arithmetic and copies ran while one was open for 14% of the time, Pallas kernels for 0%

profile of v11, /device:TPU:25, one launch (start us, length us, event | category | flops | bytes accessed | tf_op | source)
XLA Modules:
  0.0 53.4 jit_solution(18205876637432667368)
XLA Ops:
  0.6 0.0 copy-start.1
  0.6 1.3 %broadcast_in_dim.55 = f32[8,2,128]{2,1,0:T(2,128)} broadcast(f32[2,128]{1,0:T(2,128)} %param.6), dimensions={1,2} | broadcast | bytes 9216 | tf_op jit(solution)/shard_map/broadcast_in_dim | solution.py:35
  2.0 7.3 %all-to-all-start = ((f32[8,2,128]{2,1,0:T(2,128)}), f32[8,2,128]{2,1,0:T(2,128)S(1)}, u32[]{:S(2)}, u32[]{:S(2)}) async-start(f32[8,2,128]{2,1,0:T(2,128)} %broadcast_in_dim.55), calls=%async_computation | async-start | bytes 16384 | tf_op jit(solution)/shard_map/all_to_all | solution.py:36
  9.3 1.3 %pad_maximum_fusion = (f32[2,2,4,4096]{3,2,1,0:T(4,128)S(1)}, f32[2,2,4,4096]{3,2,1,0:T(4,128)S(1)}) fusion(f32[1,2,8,4096]{3,2,1,0:T(8,128)} %bitcast.43, f32[1,2,8,4096]{3,2,1,0:T(8,128)} %bitcast.42), kind=kLoop, calls=%fused_computation.25 | loop fusion | flops 131072 | bytes 1048576 | tf_op jit(solution)/shard_map/stack | solution.py:177
  10.7 0.0 copy-start.2
  10.7 3.0 %collective-permute-start.1 = (f32[2,2,4,4096]{3,2,1,0:T(4,128)S(1)}, f32[2,2,4,4096]{3,2,1,0:T(4,128)S(1)}, u32[]{:S(2)}, u32[]{:S(2)}) collective-permute-start(f32[2,2,4,4096]{3,2,1,0:T(4,128)S(1)} %get-tuple-element.12), channel_id=1, source_target_pairs={{1,0},{2,1},{3,2},{4,3},{5,4},{6,5},{7,6},{8,7},{9,8},{10,9},{11,1... | collective-permute-start | bytes 786440 | tf_op jit(solution)/shard_map/ppermute | solution.py:24
  13.7 4.8 %collective-permute-start = (f32[2,2,4,4096]{3,2,1,0:T(4,128)S(1)}, f32[2,2,4,4096]{3,2,1,0:T(4,128)S(1)}, u32[]{:S(2)}, u32[]{:S(2)}) collective-permute-start(f32[2,2,4,4096]{3,2,1,0:T(4,128)S(1)} %get-tuple-element.13), channel_id=1, source_target_pairs={{0,1},{1,2},{2,3},{3,4},{4,5},{5,6},{6,7},{7,8},{8,9},{9,10},{10,1... | collective-permute-start | bytes 786440 | tf_op jit(solution)/shard_map/ppermute | solution.py:24
  18.5 0.7 %sine_bitcast_fusion.3 = (f32[1,2]{1,0:T(1,128)S(1)}, f32[1,2]{1,0:T(1,128)S(1)}, f32[1,2]{1,0:T(1,128)S(1)}, f32[1,2]{1,0:T(1,128)S(1)}) fusion(f32[2]{0:T(128)} %param.11), kind=kLoop, calls=%fused_computation.65 | loop fusion | flops 6 | bytes 40 | tf_op jit(solution)/shard_map/stack | solution.py:192
  19.3 0.5 fusion.2
  19.9 0.6 %pad_maximum_fusion.1.drive_ref = f32[4,2]{1,0:T(4,128)} fusion(f32[1,2]{1,0:T(1,128)S(1)} %get-tuple-element.36, f32[1,2]{1,0:T(1,128)S(1)} %get-tuple-element.37, f32[1,2]{1,0:T(1,128)S(1)} %get-tuple-element.35, f32[1,2]{1,0:T(1,128)S(1)} %get-tuple-element.34), kind=kLoop, calls=%fused_computation.59 | loop fusion | flops 24 | bytes 64 | tf_op jit(solution)/shard_map/stack | solution.py:192
  20.5 0.5 select_add_fusion.matched_ref
  21.0 0.0 all-to-all-done
  21.0 0.1 pad_slice_fusion.4
  21.1 0.1 pad_slice_fusion.8
  21.2 0.1 stack.69
  21.3 0.2 fusion.9
  21.6 0.4 multiply_reduce_fusion.1
  22.1 1.9 %collective-permute-start.2 = (f32[3,4096]{1,0:T(4,128)S(1)}, f32[3,4096]{1,0:T(4,128)S(1)}, u32[]{:S(2)}, u32[]{:S(2)}) collective-permute-start(f32[3,4096]{1,0:T(4,128)S(1)} %concatenate.6), channel_id=1, source_target_pairs={{0,1},{1,2},{2,3},{3,4},{4,5},{5,6},{6,7},{7,8},{8,9},{9,10},{10,1... | collective-permute-start | bytes 147464 | tf_op jit(solution)/shard_map/ppermute | solution.py:24
  24.0 2.4 %collective-permute-start.3 = (f32[3,4096]{1,0:T(4,128)S(1)}, f32[3,4096]{1,0:T(4,128)S(1)}, u32[]{:S(2)}, u32[]{:S(2)}) collective-permute-start(f32[3,4096]{1,0:T(4,128)S(1)} %concatenate.7), channel_id=1, source_target_pairs={{1,0},{2,1},{3,2},{4,3},{5,4},{6,5},{7,6},{8,7},{9,8},{10,9},{11,1... | collective-permute-start | bytes 147464 | tf_op jit(solution)/shard_map/ppermute | solution.py:24
  26.4 0.8 %multiply_reduce_fusion.dens_ref = f32[8,4096]{1,0:T(8,128)} fusion(f32[10,8,4096]{2,1,0:T(8,128)S(1)} %select_add_fusion.matched_ref, f32[10,4096]{1,0:T(8,128)S(1)} %mul.44), kind=kLoop, calls=%fused_computation | loop fusion | flops 622592 | bytes 1605632 | tf_op jit(solution)/shard_map/reduce_sum | solution.py:210
  27.2 0.0 collective-permute-done.2.dens_above_ref
  27.2 4.5 %collective-permute-done.3.dens_below_ref = f32[3,4096]{1,0:T(4,128)S(1)} collective-permute-done((f32[3,4096]{1,0:T(4,128)S(1)}, f32[3,4096]{1,0:T(4,128)S(1)}, u32[]{:S(2)}, u32[]{:S(2)}) %collective-permute-start.3) | collective-permute-done | bytes 49184 | tf_op jit(solution)/shard_map/ppermute | solution.py:24
  31.7 0.0 collective-permute-done.1.src_below_ref
  31.7 0.0 collective-permute-done.src_above_ref
  31.7 0.6 %copy-done.6 = f32[3,4096]{1,0:T(4,128)} copy-done((f32[3,4096]{1,0:T(4,128)}, f32[3,4096]{1,0:T(4,128)S(1)}, u32[]{:S(2)}) %copy-start.6) | copy-done | bytes 49176
  32.3 0.1 copy-done.3
  32.4 0.7 %copy-done.4 = f32[2,2,4,4096]{3,2,1,0:T(4,128)} copy-done((f32[2,2,4,4096]{3,2,1,0:T(4,128)}, f32[2,2,4,4096]{3,2,1,0:T(4,128)S(1)}, u32[]{:S(2)}) %copy-start.4) | copy-done | bytes 262168
  33.1 6.5 %shard_map.77 = (f32[2,16,4096]{2,1,0:T(8,128)}, f32[8,2,128]{2,1,0:T(2,128)}) custom-call(f32[4,2]{1,0:T(4,128)} %pad_maximum_fusion.1.drive_ref, f32[2,8,4096]{2,1,0:T(8,128)} %fwd_ref.1, f32[2,8,4096]{2,1,0:T(8,128)} %adj_ref.1, f32[2,2,4,4096]{3,2,1,0:T(4,128)} %copy-done.4, f32[2,2,4,4096]{3,2,1,0:T(4,128)} %copy-done.3, ...), custom_call_target="tpu_custom_call" | custom-call | tf_op jit(solution)/shard_map/pallas_call | solution.py:157
  39.6 6.6 %all-to-all-start.1 = ((f32[8,2,128]{2,1,0:T(2,128)}), f32[8,2,128]{2,1,0:T(2,128)S(1)}, u32[]{:S(2)}, u32[]{:S(2)}) async-start(f32[8,2,128]{2,1,0:T(2,128)} %get-tuple-element.9), calls=%async_computation.1 | async-start | bytes 16384 | tf_op jit(solution)/shard_map/all_to_all | solution.py:215
  46.3 1.8 %slice.107 = f32[2,8,4096]{2,1,0:T(8,128)} slice(f32[2,16,4096]{2,1,0:T(8,128)} %get-tuple-element.8), slice={[0:2], [4:12], [0:4096]} | slice | bytes 524288 | tf_op jit(solution)/shard_map/slice | solution.py:219
  48.1 4.8 %all-to-all-done.1 = f32[8,2,128]{2,1,0:T(2,128)S(1)} async-done(((f32[8,2,128]{2,1,0:T(2,128)}), f32[8,2,128]{2,1,0:T(2,128)S(1)}, u32[]{:S(2)}, u32[]{:S(2)}) %all-to-all-start.1) | async-done | bytes 8224 | tf_op jit(solution)/shard_map/all_to_all | solution.py:215
  52.8 0.6 %reduce_sum.39 = f32[2,128]{1,0:T(2,128)} reduce(f32[8,2,128]{2,1,0:T(2,128)S(1)} %all-to-all-done.1, f32[]{:T(128)} %constant.66.clone.1), dimensions={0}, to_apply=%region_3.4 | reduce | flops 1792 | bytes 9220 | tf_op jit(solution)/shard_map/reduce_sum | solution.py:218
  (20 shorter events, 0.2 us)
Async XLA Ops:
  0.6 18.6 %copy-start.1 = (s32[4,8,4096]{2,1,0:T(8,128)S(1)}, s32[4,8,4096]{2,1,0:T(8,128)}, u32[]{:S(2)}) copy-start(s32[4,8,4096]{2,1,0:T(8,128)} %param.7) | copy-start | bytes 1572868
  2.0 19.0 %all-to-all-start = ((f32[8,2,128]{2,1,0:T(2,128)}), f32[8,2,128]{2,1,0:T(2,128)S(1)}, u32[]{:S(2)}, u32[]{:S(2)}) async-start(f32[8,2,128]{2,1,0:T(2,128)} %broadcast_in_dim.55), calls=%async_computation | async-start | bytes 16384 | tf_op jit(solution)/shard_map/all_to_all | solution.py:36
  10.7 9.2 %copy-start.2 = (bf16[4,8,4096]{2,1,0:T(8,128)(2,1)S(1)}, bf16[4,8,4096]{2,1,0:T(8,128)(2,1)}, u32[]{:S(2)}) copy-start(bf16[4,8,4096]{2,1,0:T(8,128)(2,1)} %param.8) | copy-start | bytes 786436
  10.7 21.0 %collective-permute-start.1 = (f32[2,2,4,4096]{3,2,1,0:T(4,128)S(1)}, f32[2,2,4,4096]{3,2,1,0:T(4,128)S(1)}, u32[]{:S(2)}, u32[]{:S(2)}) collective-permute-start(f32[2,2,4,4096]{3,2,1,0:T(4,128)S(1)} %get-tuple-element.12), channel_id=1, source_target_pairs={{1,0},{2,1},{3,2},{4,3},{5,4},{6,5},{7,6},{8,7},{9,8},{10,9},{11,1... | collective-permute-start | bytes 786440 | tf_op jit(solution)/shard_map/ppermute | solution.py:24
  13.7 18.0 %collective-permute-start = (f32[2,2,4,4096]{3,2,1,0:T(4,128)S(1)}, f32[2,2,4,4096]{3,2,1,0:T(4,128)S(1)}, u32[]{:S(2)}, u32[]{:S(2)}) collective-permute-start(f32[2,2,4,4096]{3,2,1,0:T(4,128)S(1)} %get-tuple-element.13), channel_id=1, source_target_pairs={{0,1},{1,2},{2,3},{3,4},{4,5},{5,6},{6,7},{7,8},{8,9},{9,10},{10,1... | collective-permute-start | bytes 786440 | tf_op jit(solution)/shard_map/ppermute | solution.py:24
  21.0 6.2 %copy-start = (f32[10,8,4096]{2,1,0:T(8,128)}, f32[10,8,4096]{2,1,0:T(8,128)S(1)}, u32[]{:S(2)}) copy-start(f32[10,8,4096]{2,1,0:T(8,128)S(1)} %select_add_fusion.matched_ref) | copy-start | bytes 3932164
  22.1 5.1 %collective-permute-start.2 = (f32[3,4096]{1,0:T(4,128)S(1)}, f32[3,4096]{1,0:T(4,128)S(1)}, u32[]{:S(2)}, u32[]{:S(2)}) collective-permute-start(f32[3,4096]{1,0:T(4,128)S(1)} %concatenate.6), channel_id=1, source_target_pairs={{0,1},{1,2},{2,3},{3,4},{4,5},{5,6},{6,7},{7,8},{8,9},{9,10},{10,1... | collective-permute-start | bytes 147464 | tf_op jit(solution)/shard_map/ppermute | solution.py:24
  24.0 7.7 %collective-permute-start.3 = (f32[3,4096]{1,0:T(4,128)S(1)}, f32[3,4096]{1,0:T(4,128)S(1)}, u32[]{:S(2)}, u32[]{:S(2)}) collective-permute-start(f32[3,4096]{1,0:T(4,128)S(1)} %concatenate.7), channel_id=1, source_target_pairs={{1,0},{2,1},{3,2},{4,3},{5,4},{6,5},{7,6},{8,7},{9,8},{10,9},{11,1... | collective-permute-start | bytes 147464 | tf_op jit(solution)/shard_map/ppermute | solution.py:24
  27.2 4.5 %copy-start.5 = (f32[3,4096]{1,0:T(4,128)}, f32[3,4096]{1,0:T(4,128)S(1)}, u32[]{:S(2)}) copy-start(f32[3,4096]{1,0:T(4,128)S(1)} %collective-permute-done.2.dens_above_ref) | copy-start | bytes 147460
  31.7 0.6 %copy-start.6 = (f32[3,4096]{1,0:T(4,128)}, f32[3,4096]{1,0:T(4,128)S(1)}, u32[]{:S(2)}) copy-start(f32[3,4096]{1,0:T(4,128)S(1)} %collective-permute-done.3.dens_below_ref) | copy-start | bytes 147460
  31.7 0.7 %copy-start.3 = (f32[2,2,4,4096]{3,2,1,0:T(4,128)}, f32[2,2,4,4096]{3,2,1,0:T(4,128)S(1)}, u32[]{:S(2)}) copy-start(f32[2,2,4,4096]{3,2,1,0:T(4,128)S(1)} %collective-permute-done.1.src_below_ref) | copy-start | bytes 786436
  32.4 0.7 %copy-start.4 = (f32[2,2,4,4096]{3,2,1,0:T(4,128)}, f32[2,2,4,4096]{3,2,1,0:T(4,128)S(1)}, u32[]{:S(2)}) copy-start(f32[2,2,4,4096]{3,2,1,0:T(4,128)S(1)} %collective-permute-done.src_above_ref) | copy-start | bytes 786436
  39.6 13.2 %all-to-all-start.1 = ((f32[8,2,128]{2,1,0:T(2,128)}), f32[8,2,128]{2,1,0:T(2,128)S(1)}, u32[]{:S(2)}, u32[]{:S(2)}) async-start(f32[8,2,128]{2,1,0:T(2,128)} %get-tuple-element.9), calls=%async_computation.1 | async-start | bytes 16384 | tf_op jit(solution)/shard_map/all_to_all | solution.py:215

commit v12 on v11

--- a/solution.py
+++ b/solution.py
@@ -8,6 +8,7 @@
 ITERS = 4
 HALO = 4
 FACTOR = 4
+CHUNK = 512
 GRAD_SCALE = 4.0 / 16
 SHIFTS = (-2, -1, 0, 1, 2)
 
@@ -68,7 +69,7 @@
     drive_ref, fwd_ref, adj_ref, src_above_ref, src_below_ref,
     dens_ref, dens_above_ref, dens_below_ref, matched_ref,
     final_ref, pieces_ref,
-    source_ref, density_ref, step_ref, history_ref, sense_ref, gathered_ref,
+    source_ref, density_ref, step_ref, history_ref, sense_ref, gathered_ref, fields_ref,
 ):
     runs, waves, rows, cols = source_ref.shape
     own = fwd_ref.shape[1]
@@ -86,44 +87,61 @@
     step_ref[0:HALO] = jnp.broadcast_to(time_step * dens_above_ref[reach : reach + 1], (HALO, cols))
     step_ref[HALO : HALO + own] = jnp.full((own, cols), time_step, jnp.float32)
     step_ref[HALO + own : rows] = jnp.broadcast_to(time_step * dens_below_ref[0:1], (HALO, cols))
-    row_id = lax.broadcasted_iota(jnp.int32, (rows, cols), 0)
-    col_id = lax.broadcasted_iota(jnp.int32, (rows, cols), 1)
     density = density_ref[...]
-    half_density = drude_gain * density
-    hy_step = step_ref[...]
-    inverse = jnp.where(hy_step > 0.0, time_step / (1.0 + high_contrast * density), 0.0)
+    fields_ref[4] = jnp.where(step_ref[...] > 0.0, time_step / (1.0 + high_contrast * density), 0.0)
+    fields_ref[5] = drude_gain * density
     sense_ref[...] = jnp.zeros((rows, cols), jnp.float32)
+    width = CHUNK
+    count = cols // width
+    row_id = lax.broadcasted_iota(jnp.int32, (rows, width), 0)
     for wave in range(waves):
         for run in range(runs):
-            field_e = field_hx = field_hy = current = None
-            for turn in range(ITERS):
-                drive_term = drive_ref[turn, wave] * source_ref[run, wave]
-                if field_e is None:
-                    field_e = drive_term
-                else:
+            field_e = drive_ref[0, wave] * source_ref[run, wave]
+            fields_ref[0] = field_e
+            if run == 0:
+                history_ref[0] = field_e
+            else:
+                sense_ref[...] += field_e * history_ref[ITERS - 1]
+            for turn in range(1, ITERS):
+
+                def sweep(index, carry, turn=turn, run=run, wave=wave):
+                    at = pl.multiple_of(index * width, width)
+                    ahead = pl.multiple_of(jnp.minimum(index + 1, count - 1) * width, width)
+                    here = pl.ds(at, width)
+                    field_e = fields_ref[0, :, here]
+                    e_next = jnp.where(index + 1 < count, fields_ref[0, :, pl.ds(ahead, 128)], 0.0)
+                    e_right = pltpu.roll(jnp.concatenate([field_e, e_next], axis=1), width + 127, 1)[:, :width]
                     e_up = jnp.where(row_id < rows - 1, pltpu.roll(field_e, rows - 1, 0), 0.0)
-                    e_right = jnp.where(col_id < cols - 1, pltpu.roll(field_e, cols - 1, 1), 0.0)
-                    if field_hx is None:
+                    hy_step = step_ref[:, here]
+                    half_density = fields_ref[5, :, here]
+                    if turn == 1:
                         field_hx = -time_step * (e_right - field_e)
                         field_hy = hy_step * (e_up - field_e)
                         current = half_density * field_e
                     else:
-                        field_hx = field_hx - time_step * (e_right - field_e)
-                        field_hy = field_hy + hy_step * (e_up - field_e)
-                        current = drude_decay * current + half_density * field_e
+                        field_hx = fields_ref[1, :, here] - time_step * (e_right - field_e)
+                        field_hy = fields_ref[2, :, here] + hy_step * (e_up - field_e)
+                        current = drude_decay * fields_ref[3, :, here] + half_density * field_e
+                    hx_left = pltpu.roll(jnp.concatenate([carry, field_hx], axis=1), 1, 1)[:, 128:]
                     hy_down = jnp.where(row_id > 0, pltpu.roll(field_hy, 1, 0), 0.0)
-                    hx_left = jnp.where(col_id > 0, pltpu.roll(field_hx, 1, 1), 0.0)
                     field_e = (
                         field_e
-                        + inverse * (field_hy - hy_down - (field_hx - hx_left) - current)
-                        + drive_term
+                        + fields_ref[4, :, here] * (field_hy - hy_down - (field_hx - hx_left) - current)
+                        + drive_ref[turn, wave] * source_ref[run, wave, :, here]
                     )
-                if run == 0:
-                    history_ref[turn] = field_e
-                else:
-                    sense_ref[...] += field_e * history_ref[ITERS - 1 - turn]
+                    fields_ref[0, :, here] = field_e
+                    fields_ref[1, :, here] = field_hx
+                    fields_ref[2, :, here] = field_hy
+                    fields_ref[3, :, here] = current
+                    if run == 0:
+                        history_ref[turn, :, here] = field_e
+                    else:
+                        sense_ref[:, here] += field_e * history_ref[ITERS - 1 - turn, :, here]
+                    return field_hx[:, width - 128 :]
+
+                lax.fori_loop(0, count, sweep, jnp.zeros((rows, 128), jnp.float32))
             if run == 0:
-                final_ref[wave] = field_e
+                final_ref[wave] = fields_ref[0]
     scaled = GRAD_SCALE * sense_ref[HALO : HALO + own]
     lane = lax.broadcasted_iota(jnp.int32, (1, cols), 1)
     for row in range(block_rows):
@@ -169,6 +187,7 @@
             pltpu.VMEM((ITERS, rows, cols), jnp.float32),
             pltpu.VMEM((rows, cols), jnp.float32),
             pltpu.VMEM((8, cols), jnp.float32),
+            pltpu.VMEM((6, rows, cols), jnp.float32),
         ],
     )(drive, fwd, adj, src_above, src_below, dens, dens_above, dens_below, matched)
 

time: 53.8 us -> 66.4 us (1.23)
  Pallas kernels: 6.51 us -> 19.1 us
    pallas_call x1, Pallas kernels: 6.51 us -> 19.1 us  [march(): pl.pallas_call(march_kernel, out_shape=(jax.ShapeDtypeStruct((waves, rows...]
  transfers between devices with their start and end apart: 6 -> 6, of which waited for: 2 -> 2; matrix products, arithmetic and copies ran while one was open for 14% -> 11% of each run, Pallas kernels for 0% -> 0%
where the time goes in v12:
time: 66.4 us; the launch traced here: 66 us
  starting transfers between devices  26.1 us (39%)
  Pallas kernels  19.1 us (29%)
  waiting for transfers between devices  9.28 us (14%)
  other arithmetic  5.46 us (8%)
  local copies, waits for them, and re-layouts  4.96 us (7%)
  between operations  0.83 us (1%)
    pallas_call x1, Pallas kernels, march(): pl.pallas_call(march_kernel, out_shape=(jax.ShapeDtypeStruct((waves, rows...  19.1 us
    ppermute x4, starting transfers between devices, from_behind(): lax.ppermute(value, axis, [(source, source + steps) for source in range(f...  12.1 us
    all_to_all x1, starting transfers between devices, gather_columns(): pieces = lax.all_to_all(copies, axis, 0, 0, tiled=True)  7.33 us
    all_to_all x1, starting transfers between devices, shards(): lax.all_to_all(pieces.reshape(count, chunks // count, block_rows, span).t...  6.65 us
    all_to_all x1, waiting for transfers between devices, shards(): lax.all_to_all(pieces.reshape(count, chunks // count, block_rows, span).t...  4.76 us
    ppermute x4, waiting for transfers between devices, from_behind(): lax.ppermute(value, axis, [(source, source + steps) for source in range(f...  4.51 us
    slice x1, local copies, waits for them, and re-layouts, shards(): return (final[:, HALO:HALO + cells_x], density_grad)  1.77 us
    unnamed x14, local copies, waits for them, and re-layouts  1.44 us
  transfers between devices with their start and end apart: 6, of which 2 were waited for; matrix products, arithmetic and copies ran while one was open for 11% of the time, Pallas kernels for 0%

profile of v12, /device:TPU:25, one launch (start us, length us, event | category | flops | bytes accessed | tf_op | source)
XLA Modules:
  0.0 66.0 jit_solution(17960148657190674252)
XLA Ops:
  0.6 0.0 copy-start.1
  0.6 1.3 %broadcast_in_dim.55 = f32[8,2,128]{2,1,0:T(2,128)} broadcast(f32[2,128]{1,0:T(2,128)} %param.6), dimensions={1,2} | broadcast | bytes 9216 | tf_op jit(solution)/shard_map/broadcast_in_dim | solution.py:36
  2.0 7.3 %all-to-all-start = ((f32[8,2,128]{2,1,0:T(2,128)}), f32[8,2,128]{2,1,0:T(2,128)S(1)}, u32[]{:S(2)}, u32[]{:S(2)}) async-start(f32[8,2,128]{2,1,0:T(2,128)} %broadcast_in_dim.55), calls=%async_computation | async-start | bytes 16384 | tf_op jit(solution)/shard_map/all_to_all | solution.py:37
  9.3 1.3 %pad_maximum_fusion = (f32[2,2,4,4096]{3,2,1,0:T(4,128)S(1)}, f32[2,2,4,4096]{3,2,1,0:T(4,128)S(1)}) fusion(f32[1,2,8,4096]{3,2,1,0:T(8,128)} %bitcast.43, f32[1,2,8,4096]{3,2,1,0:T(8,128)} %bitcast.42), kind=kLoop, calls=%fused_computation.25 | loop fusion | flops 131072 | bytes 1048576 | tf_op jit(solution)/shard_map/stack | solution.py:196
  10.7 0.0 copy-start.2
  10.7 3.0 %collective-permute-start.1 = (f32[2,2,4,4096]{3,2,1,0:T(4,128)S(1)}, f32[2,2,4,4096]{3,2,1,0:T(4,128)S(1)}, u32[]{:S(2)}, u32[]{:S(2)}) collective-permute-start(f32[2,2,4,4096]{3,2,1,0:T(4,128)S(1)} %get-tuple-element.12), channel_id=1, source_target_pairs={{1,0},{2,1},{3,2},{4,3},{5,4},{6,5},{7,6},{8,7},{9,8},{10,9},{11,1... | collective-permute-start | bytes 786440 | tf_op jit(solution)/shard_map/ppermute | solution.py:25
  13.7 4.8 %collective-permute-start = (f32[2,2,4,4096]{3,2,1,0:T(4,128)S(1)}, f32[2,2,4,4096]{3,2,1,0:T(4,128)S(1)}, u32[]{:S(2)}, u32[]{:S(2)}) collective-permute-start(f32[2,2,4,4096]{3,2,1,0:T(4,128)S(1)} %get-tuple-element.13), channel_id=1, source_target_pairs={{0,1},{1,2},{2,3},{3,4},{4,5},{5,6},{6,7},{7,8},{8,9},{9,10},{10,1... | collective-permute-start | bytes 786440 | tf_op jit(solution)/shard_map/ppermute | solution.py:25
  18.5 0.7 %sine_bitcast_fusion.3 = (f32[1,2]{1,0:T(1,128)S(1)}, f32[1,2]{1,0:T(1,128)S(1)}, f32[1,2]{1,0:T(1,128)S(1)}, f32[1,2]{1,0:T(1,128)S(1)}) fusion(f32[2]{0:T(128)} %param.11), kind=kLoop, calls=%fused_computation.65 | loop fusion | flops 6 | bytes 40 | tf_op jit(solution)/shard_map/stack | solution.py:211
  19.3 0.5 fusion.2
  19.9 0.6 pad_maximum_fusion.1.drive_ref
  20.5 0.5 select_add_fusion.matched_ref
  21.0 0.0 all-to-all-done
  21.0 0.1 pad_slice_fusion.4
  21.1 0.1 pad_slice_fusion.8
  21.2 0.1 stack.69
  21.3 0.2 fusion.9
  21.6 0.4 multiply_reduce_fusion.1
  22.1 1.9 %collective-permute-start.2 = (f32[3,4096]{1,0:T(4,128)S(1)}, f32[3,4096]{1,0:T(4,128)S(1)}, u32[]{:S(2)}, u32[]{:S(2)}) collective-permute-start(f32[3,4096]{1,0:T(4,128)S(1)} %concatenate.6), channel_id=1, source_target_pairs={{0,1},{1,2},{2,3},{3,4},{4,5},{5,6},{6,7},{7,8},{8,9},{9,10},{10,1... | collective-permute-start | bytes 147464 | tf_op jit(solution)/shard_map/ppermute | solution.py:25
  24.0 2.4 %collective-permute-start.3 = (f32[3,4096]{1,0:T(4,128)S(1)}, f32[3,4096]{1,0:T(4,128)S(1)}, u32[]{:S(2)}, u32[]{:S(2)}) collective-permute-start(f32[3,4096]{1,0:T(4,128)S(1)} %concatenate.7), channel_id=1, source_target_pairs={{1,0},{2,1},{3,2},{4,3},{5,4},{6,5},{7,6},{8,7},{9,8},{10,9},{11,1... | collective-permute-start | bytes 147464 | tf_op jit(solution)/shard_map/ppermute | solution.py:25
  26.4 0.8 %multiply_reduce_fusion.dens_ref = f32[8,4096]{1,0:T(8,128)} fusion(f32[10,8,4096]{2,1,0:T(8,128)S(1)} %select_add_fusion.matched_ref, f32[10,4096]{1,0:T(8,128)S(1)} %mul.44), kind=kLoop, calls=%fused_computation | loop fusion | flops 622592 | bytes 1605632 | tf_op jit(solution)/shard_map/reduce_sum | solution.py:229
  27.2 0.0 collective-permute-done.2.dens_above_ref
  27.2 4.5 %collective-permute-done.3.dens_below_ref = f32[3,4096]{1,0:T(4,128)S(1)} collective-permute-done((f32[3,4096]{1,0:T(4,128)S(1)}, f32[3,4096]{1,0:T(4,128)S(1)}, u32[]{:S(2)}, u32[]{:S(2)}) %collective-permute-start.3) | collective-permute-done | bytes 49184 | tf_op jit(solution)/shard_map/ppermute | solution.py:25
  31.7 0.0 collective-permute-done.1.src_below_ref
  31.7 0.0 collective-permute-done.src_above_ref
  31.7 0.6 copy-done.6
  32.3 0.1 copy-done.3
  32.4 0.7 %copy-done.4 = f32[2,2,4,4096]{3,2,1,0:T(4,128)} copy-done((f32[2,2,4,4096]{3,2,1,0:T(4,128)}, f32[2,2,4,4096]{3,2,1,0:T(4,128)S(1)}, u32[]{:S(2)}) %copy-start.4) | copy-done | bytes 262168
  33.1 19.1 %shard_map.77 = (f32[2,16,4096]{2,1,0:T(8,128)}, f32[8,2,128]{2,1,0:T(2,128)}) custom-call(f32[4,2]{1,0:T(4,128)} %pad_maximum_fusion.1.drive_ref, f32[2,8,4096]{2,1,0:T(8,128)} %fwd_ref.1, f32[2,8,4096]{2,1,0:T(8,128)} %adj_ref.1, f32[2,2,4,4096]{3,2,1,0:T(4,128)} %copy-done.4, f32[2,2,4,4096]{3,2,1,0:T(4,128)} %copy-done.3, ...), custom_call_target="tpu_custom_call" | custom-call | tf_op jit(solution)/shard_map/pallas_call | solution.py:175
  52.2 6.6 %all-to-all-start.1 = ((f32[8,2,128]{2,1,0:T(2,128)}), f32[8,2,128]{2,1,0:T(2,128)S(1)}, u32[]{:S(2)}, u32[]{:S(2)}) async-start(f32[8,2,128]{2,1,0:T(2,128)} %get-tuple-element.9), calls=%async_computation.1 | async-start | bytes 16384 | tf_op jit(solution)/shard_map/all_to_all | solution.py:234
  58.9 1.8 %slice.107 = f32[2,8,4096]{2,1,0:T(8,128)} slice(f32[2,16,4096]{2,1,0:T(8,128)} %get-tuple-element.8), slice={[0:2], [4:12], [0:4096]} | slice | bytes 524288 | tf_op jit(solution)/shard_map/slice | solution.py:238
  60.6 4.8 %all-to-all-done.1 = f32[8,2,128]{2,1,0:T(2,128)S(1)} async-done(((f32[8,2,128]{2,1,0:T(2,128)}), f32[8,2,128]{2,1,0:T(2,128)S(1)}, u32[]{:S(2)}, u32[]{:S(2)}) %all-to-all-start.1) | async-done | bytes 8224 | tf_op jit(solution)/shard_map/all_to_all | solution.py:234
  65.4 0.6 reduce_sum.39
  (20 shorter events, 0.2 us)
Async XLA Ops:
  0.6 18.6 %copy-start.1 = (s32[4,8,4096]{2,1,0:T(8,128)S(1)}, s32[4,8,4096]{2,1,0:T(8,128)}, u32[]{:S(2)}) copy-start(s32[4,8,4096]{2,1,0:T(8,128)} %param.7) | copy-start | bytes 1572868
  2.0 19.0 %all-to-all-start = ((f32[8,2,128]{2,1,0:T(2,128)}), f32[8,2,128]{2,1,0:T(2,128)S(1)}, u32[]{:S(2)}, u32[]{:S(2)}) async-start(f32[8,2,128]{2,1,0:T(2,128)} %broadcast_in_dim.55), calls=%async_computation | async-start | bytes 16384 | tf_op jit(solution)/shard_map/all_to_all | solution.py:37
  10.7 9.2 %copy-start.2 = (bf16[4,8,4096]{2,1,0:T(8,128)(2,1)S(1)}, bf16[4,8,4096]{2,1,0:T(8,128)(2,1)}, u32[]{:S(2)}) copy-start(bf16[4,8,4096]{2,1,0:T(8,128)(2,1)} %param.8) | copy-start | bytes 786436
  10.7 21.0 %collective-permute-start.1 = (f32[2,2,4,4096]{3,2,1,0:T(4,128)S(1)}, f32[2,2,4,4096]{3,2,1,0:T(4,128)S(1)}, u32[]{:S(2)}, u32[]{:S(2)}) collective-permute-start(f32[2,2,4,4096]{3,2,1,0:T(4,128)S(1)} %get-tuple-element.12), channel_id=1, source_target_pairs={{1,0},{2,1},{3,2},{4,3},{5,4},{6,5},{7,6},{8,7},{9,8},{10,9},{11,1... | collective-permute-start | bytes 786440 | tf_op jit(solution)/shard_map/ppermute | solution.py:25
  13.7 18.0 %collective-permute-start = (f32[2,2,4,4096]{3,2,1,0:T(4,128)S(1)}, f32[2,2,4,4096]{3,2,1,0:T(4,128)S(1)}, u32[]{:S(2)}, u32[]{:S(2)}) collective-permute-start(f32[2,2,4,4096]{3,2,1,0:T(4,128)S(1)} %get-tuple-element.13), channel_id=1, source_target_pairs={{0,1},{1,2},{2,3},{3,4},{4,5},{5,6},{6,7},{7,8},{8,9},{9,10},{10,1... | collective-permute-start | bytes 786440 | tf_op jit(solution)/shard_map/ppermute | solution.py:25
  21.0 6.2 %copy-start = (f32[10,8,4096]{2,1,0:T(8,128)}, f32[10,8,4096]{2,1,0:T(8,128)S(1)}, u32[]{:S(2)}) copy-start(f32[10,8,4096]{2,1,0:T(8,128)S(1)} %select_add_fusion.matched_ref) | copy-start | bytes 3932164
  22.1 5.1 %collective-permute-start.2 = (f32[3,4096]{1,0:T(4,128)S(1)}, f32[3,4096]{1,0:T(4,128)S(1)}, u32[]{:S(2)}, u32[]{:S(2)}) collective-permute-start(f32[3,4096]{1,0:T(4,128)S(1)} %concatenate.6), channel_id=1, source_target_pairs={{0,1},{1,2},{2,3},{3,4},{4,5},{5,6},{6,7},{7,8},{8,9},{9,10},{10,1... | collective-permute-start | bytes 147464 | tf_op jit(solution)/shard_map/ppermute | solution.py:25
  24.0 7.7 %collective-permute-start.3 = (f32[3,4096]{1,0:T(4,128)S(1)}, f32[3,4096]{1,0:T(4,128)S(1)}, u32[]{:S(2)}, u32[]{:S(2)}) collective-permute-start(f32[3,4096]{1,0:T(4,128)S(1)} %concatenate.7), channel_id=1, source_target_pairs={{1,0},{2,1},{3,2},{4,3},{5,4},{6,5},{7,6},{8,7},{9,8},{10,9},{11,1... | collective-permute-start | bytes 147464 | tf_op jit(solution)/shard_map/ppermute | solution.py:25
  27.2 4.5 %copy-start.5 = (f32[3,4096]{1,0:T(4,128)}, f32[3,4096]{1,0:T(4,128)S(1)}, u32[]{:S(2)}) copy-start(f32[3,4096]{1,0:T(4,128)S(1)} %collective-permute-done.2.dens_above_ref) | copy-start | bytes 147460
  31.7 0.6 copy-start.6
  31.7 0.7 %copy-start.3 = (f32[2,2,4,4096]{3,2,1,0:T(4,128)}, f32[2,2,4,4096]{3,2,1,0:T(4,128)S(1)}, u32[]{:S(2)}) copy-start(f32[2,2,4,4096]{3,2,1,0:T(4,128)S(1)} %collective-permute-done.1.src_below_ref) | copy-start | bytes 786436
  32.4 0.7 %copy-start.4 = (f32[2,2,4,4096]{3,2,1,0:T(4,128)}, f32[2,2,4,4096]{3,2,1,0:T(4,128)S(1)}, u32[]{:S(2)}) copy-start(f32[2,2,4,4096]{3,2,1,0:T(4,128)S(1)} %collective-permute-done.src_above_ref) | copy-start | bytes 786436
  52.2 13.2 %all-to-all-start.1 = ((f32[8,2,128]{2,1,0:T(2,128)}), f32[8,2,128]{2,1,0:T(2,128)S(1)}, u32[]{:S(2)}, u32[]{:S(2)}) async-start(f32[8,2,128]{2,1,0:T(2,128)} %get-tuple-element.9), calls=%async_computation.1 | async-start | bytes 16384 | tf_op jit(solution)/shard_map/all_to_all | solution.py:234

commit v13 on v11

--- a/solution.py
+++ b/solution.py
@@ -1,5 +1,6 @@
 import jax
 import jax.numpy as jnp
+import numpy as np
 from jax import lax
 from jax.experimental import pallas as pl
 from jax.experimental.pallas import tpu as pltpu
@@ -189,8 +190,7 @@
     matched = jnp.zeros((block_rows * len(SHIFTS), cells_x, cells_y), jnp.float32)
     for entry in range(foot_index.shape[0]):
         matched = matched + jnp.where(key[entry][None] == codes, weights[entry][None], 0.0)
-    drive = jnp.stack([jnp.sin(omega * (turn + 1.0)) for turn in range(ITERS)])
-    matched, drive = lax.optimization_barrier((matched, drive))
+    matched = lax.optimization_barrier(matched)
     span = 128
     chunks = block_cols // span
     spread = (
@@ -208,6 +208,7 @@
     above = from_behind(jnp.concatenate([last_rows, present]), "tile", 1)
     below = from_behind(jnp.concatenate([present, first_rows]), "tile", -1)
     density_cell = jnp.sum(matched * candidates[:, None, :], axis=0)
+    drive = jnp.sin(omega[None, :] * np.arange(1.0, ITERS + 1.0, dtype=np.float32)[:, None])
     final, pieces = march(
         drive, source_fwd, source_adj, src_above, src_below, density_cell, above, below, matched, block_rows, chunks
     )

time: 53.8 us -> 53.7 us (level)
  other arithmetic: 5.46 us -> 4.81 us
    another operation x2 -> x0, other arithmetic: 1.33 us -> none  [shards(): drive = jnp.stack([jnp.sin(omega * (turn + 1.0)) for turn in range(ITERS)])]
    sin x0 -> x1, other arithmetic: none -> 0.69 us  [shards(): jnp.sin(omega[None, :] * np.arange(1.0, ITERS + 1.0, dtype=np.float32)[:,...]
    unnamed x14 -> x18, local copies, waits for them, and re-layouts: 1.44 us -> 1.95 us
  transfers between devices with their start and end apart: 6 -> 6, of which waited for: 2 -> 2; matrix products, arithmetic and copies ran while one was open for 14% -> 12% of each run, Pallas kernels for 0% -> 0%
where the time goes in v13:
time: 53.7 us; the launch traced here: 53.3 us
  starting transfers between devices  26.1 us (49%)
  waiting for transfers between devices  9.28 us (17%)
  Pallas kernels  6.51 us (12%)
  local copies, waits for them, and re-layouts  5.47 us (10%)
  other arithmetic  4.81 us (9%)
  between operations  0.84 us (2%)
    ppermute x4, starting transfers between devices, from_behind(): lax.ppermute(value, axis, [(source, source + steps) for source in range(f...  12.1 us
    all_to_all x1, starting transfers between devices, gather_columns(): pieces = lax.all_to_all(copies, axis, 0, 0, tiled=True)  7.33 us
    all_to_all x1, starting transfers between devices, shards(): lax.all_to_all(pieces.reshape(count, chunks // count, block_rows, span).t...  6.65 us
    pallas_call x1, Pallas kernels, march(): pl.pallas_call(march_kernel, out_shape=(jax.ShapeDtypeStruct((waves, rows...  6.51 us
    all_to_all x1, waiting for transfers between devices, shards(): lax.all_to_all(pieces.reshape(count, chunks // count, block_rows, span).t...  4.76 us
    ppermute x4, waiting for transfers between devices, from_behind(): lax.ppermute(value, axis, [(source, source + steps) for source in range(f...  4.51 us
    unnamed x18, local copies, waits for them, and re-layouts  1.95 us
    slice x1, local copies, waits for them, and re-layouts, shards(): return (final[:, HALO:HALO + cells_x], density_grad)  1.77 us
  transfers between devices with their start and end apart: 6, of which 2 were waited for; matrix products, arithmetic and copies ran while one was open for 12% of the time, Pallas kernels for 0%

profile of v13, /device:TPU:25, one launch (start us, length us, event | category | flops | bytes accessed | tf_op | source)
XLA Modules:
  0.0 53.3 jit_solution(11618606250319902878)
XLA Ops:
  0.6 1.3 %broadcast_in_dim.56 = f32[8,2,128]{2,1,0:T(2,128)} broadcast(f32[2,128]{1,0:T(2,128)} %param.7), dimensions={1,2} | broadcast | bytes 9216 | tf_op jit(solution)/shard_map/broadcast_in_dim | solution.py:36
  2.0 7.3 %all-to-all-start = ((f32[8,2,128]{2,1,0:T(2,128)}), f32[8,2,128]{2,1,0:T(2,128)S(1)}, u32[]{:S(2)}, u32[]{:S(2)}) async-start(f32[8,2,128]{2,1,0:T(2,128)} %broadcast_in_dim.56), calls=%async_computation | async-start | bytes 16384 | tf_op jit(solution)/shard_map/all_to_all | solution.py:37
  9.3 1.3 %pad_maximum_fusion = (f32[2,2,4,4096]{3,2,1,0:T(4,128)S(1)}, f32[2,2,4,4096]{3,2,1,0:T(4,128)S(1)}) fusion(f32[1,2,8,4096]{3,2,1,0:T(8,128)} %bitcast.35, f32[1,2,8,4096]{3,2,1,0:T(8,128)} %bitcast.34), kind=kLoop, calls=%fused_computation.27 | loop fusion | flops 131072 | bytes 1048576 | tf_op jit(solution)/shard_map/stack | solution.py:178
  10.7 0.0 copy-start.2
  10.7 3.0 %collective-permute-start.1 = (f32[2,2,4,4096]{3,2,1,0:T(4,128)S(1)}, f32[2,2,4,4096]{3,2,1,0:T(4,128)S(1)}, u32[]{:S(2)}, u32[]{:S(2)}) collective-permute-start(f32[2,2,4,4096]{3,2,1,0:T(4,128)S(1)} %get-tuple-element.16), channel_id=1, source_target_pairs={{1,0},{2,1},{3,2},{4,3},{5,4},{6,5},{7,6},{8,7},{9,8},{10,9},{11,1... | collective-permute-start | bytes 786440 | tf_op jit(solution)/shard_map/ppermute | solution.py:25
  13.7 4.8 %collective-permute-start = (f32[2,2,4,4096]{3,2,1,0:T(4,128)S(1)}, f32[2,2,4,4096]{3,2,1,0:T(4,128)S(1)}, u32[]{:S(2)}, u32[]{:S(2)}) collective-permute-start(f32[2,2,4,4096]{3,2,1,0:T(4,128)S(1)} %get-tuple-element.17), channel_id=1, source_target_pairs={{0,1},{1,2},{2,3},{3,4},{4,5},{5,6},{6,7},{7,8},{8,9},{9,10},{10,1... | collective-permute-start | bytes 786440 | tf_op jit(solution)/shard_map/ppermute | solution.py:25
  18.5 0.5 fusion.2
  19.0 0.0 copy-start.7
  19.1 0.0 copy-start.8
  19.2 0.5 copy-done.7
  19.7 0.0 copy-done.8
  19.7 0.7 %multiply_sine_fusion.drive_ref = f32[4,2]{1,0:T(4,128)} fusion(f32[4]{0:T(128)S(1)} %copy-done.8, f32[2]{0:T(128)S(1)} %copy-done.7), kind=kLoop, calls=%fused_computation.61 | loop fusion | flops 8 | bytes 56 | tf_op jit(solution)/shard_map/sin | solution.py:211
  20.4 0.5 select_add_fusion.matched_ref
  20.9 0.1 pad_slice_fusion.4
  21.0 0.1 pad_slice_fusion.8
  21.1 0.1 stack.49
  21.2 0.2 fusion.11
  21.5 0.4 fusion.8
  21.9 1.9 %collective-permute-start.2 = (f32[3,4096]{1,0:T(4,128)S(1)}, f32[3,4096]{1,0:T(4,128)S(1)}, u32[]{:S(2)}, u32[]{:S(2)}) collective-permute-start(f32[3,4096]{1,0:T(4,128)S(1)} %concatenate.6), channel_id=1, source_target_pairs={{0,1},{1,2},{2,3},{3,4},{4,5},{5,6},{6,7},{7,8},{8,9},{9,10},{10,1... | collective-permute-start | bytes 147464 | tf_op jit(solution)/shard_map/ppermute | solution.py:25
  23.9 2.4 %collective-permute-start.3 = (f32[3,4096]{1,0:T(4,128)S(1)}, f32[3,4096]{1,0:T(4,128)S(1)}, u32[]{:S(2)}, u32[]{:S(2)}) collective-permute-start(f32[3,4096]{1,0:T(4,128)S(1)} %concatenate.7), channel_id=1, source_target_pairs={{1,0},{2,1},{3,2},{4,3},{5,4},{6,5},{7,6},{8,7},{9,8},{10,9},{11,1... | collective-permute-start | bytes 147464 | tf_op jit(solution)/shard_map/ppermute | solution.py:25
  26.3 0.8 %multiply_reduce_fusion.dens_ref = f32[8,4096]{1,0:T(8,128)} fusion(f32[10,8,4096]{2,1,0:T(8,128)S(1)} %select_add_fusion.matched_ref, f32[10,4096]{1,0:T(8,128)S(1)} %mul.51), kind=kLoop, calls=%fused_computation | loop fusion | flops 622592 | bytes 1605632 | tf_op jit(solution)/shard_map/reduce_sum | solution.py:210
  27.0 0.0 collective-permute-done.2.dens_above_ref
  27.1 4.5 %collective-permute-done.3.dens_below_ref = f32[3,4096]{1,0:T(4,128)S(1)} collective-permute-done((f32[3,4096]{1,0:T(4,128)S(1)}, f32[3,4096]{1,0:T(4,128)S(1)}, u32[]{:S(2)}, u32[]{:S(2)}) %collective-permute-start.3) | collective-permute-done | bytes 49184 | tf_op jit(solution)/shard_map/ppermute | solution.py:25
  31.6 0.0 collective-permute-done.1.src_below_ref
  31.6 0.6 %copy-done.6 = f32[3,4096]{1,0:T(4,128)} copy-done((f32[3,4096]{1,0:T(4,128)}, f32[3,4096]{1,0:T(4,128)S(1)}, u32[]{:S(2)}) %copy-start.6) | copy-done | bytes 49176
  32.2 0.1 copy-done.3
  32.3 0.7 %copy-done.4 = f32[2,2,4,4096]{3,2,1,0:T(4,128)} copy-done((f32[2,2,4,4096]{3,2,1,0:T(4,128)}, f32[2,2,4,4096]{3,2,1,0:T(4,128)S(1)}, u32[]{:S(2)}) %copy-start.4) | copy-done | bytes 262168
  33.0 6.5 %shard_map.86 = (f32[2,16,4096]{2,1,0:T(8,128)}, f32[8,2,128]{2,1,0:T(2,128)}) custom-call(f32[4,2]{1,0:T(4,128)} %multiply_sine_fusion.drive_ref, f32[2,8,4096]{2,1,0:T(8,128)} %fwd_ref.1, f32[2,8,4096]{2,1,0:T(8,128)} %adj_ref.1, f32[2,2,4,4096]{3,2,1,0:T(4,128)} %copy-done.4, f32[2,2,4,4096]{3,2,1,0:T(4,128)} %copy-done.3, ...), custom_call_target="tpu_custom_call" | custom-call | tf_op jit(solution)/shard_map/pallas_call | solution.py:158
  39.5 6.6 %all-to-all-start.1 = ((f32[8,2,128]{2,1,0:T(2,128)}), f32[8,2,128]{2,1,0:T(2,128)S(1)}, u32[]{:S(2)}, u32[]{:S(2)}) async-start(f32[8,2,128]{2,1,0:T(2,128)} %get-tuple-element.5), calls=%async_computation.1 | async-start | bytes 16384 | tf_op jit(solution)/shard_map/all_to_all | solution.py:216
  46.2 1.8 %slice.107 = f32[2,8,4096]{2,1,0:T(8,128)} slice(f32[2,16,4096]{2,1,0:T(8,128)} %get-tuple-element.4), slice={[0:2], [4:12], [0:4096]} | slice | bytes 524288 | tf_op jit(solution)/shard_map/slice | solution.py:220
  47.9 4.8 %all-to-all-done.1 = f32[8,2,128]{2,1,0:T(2,128)S(1)} async-done(((f32[8,2,128]{2,1,0:T(2,128)}), f32[8,2,128]{2,1,0:T(2,128)S(1)}, u32[]{:S(2)}, u32[]{:S(2)}) %all-to-all-start.1) | async-done | bytes 8224 | tf_op jit(solution)/shard_map/all_to_all | solution.py:216
  52.7 0.6 %reduce_sum.39 = f32[2,128]{1,0:T(2,128)} reduce(f32[8,2,128]{2,1,0:T(2,128)S(1)} %all-to-all-done.1, f32[]{:T(128)} %constant.65.clone.1), dimensions={0}, to_apply=%region_3.4 | reduce | flops 1792 | bytes 9220 | tf_op jit(solution)/shard_map/reduce_sum | solution.py:219
  (23 shorter events, 0.3 us)
Async XLA Ops:
  0.6 17.9 %copy-start.1 = (s32[4,8,4096]{2,1,0:T(8,128)S(1)}, s32[4,8,4096]{2,1,0:T(8,128)}, u32[]{:S(2)}) copy-start(s32[4,8,4096]{2,1,0:T(8,128)} %param.8) | copy-start | bytes 1572868
  2.0 18.9 %all-to-all-start = ((f32[8,2,128]{2,1,0:T(2,128)}), f32[8,2,128]{2,1,0:T(2,128)S(1)}, u32[]{:S(2)}, u32[]{:S(2)}) async-start(f32[8,2,128]{2,1,0:T(2,128)} %broadcast_in_dim.56), calls=%async_computation | async-start | bytes 16384 | tf_op jit(solution)/shard_map/all_to_all | solution.py:37
  10.7 8.5 %copy-start.2 = (bf16[4,8,4096]{2,1,0:T(8,128)(2,1)S(1)}, bf16[4,8,4096]{2,1,0:T(8,128)(2,1)}, u32[]{:S(2)}) copy-start(bf16[4,8,4096]{2,1,0:T(8,128)(2,1)} %param.9) | copy-start | bytes 786436
  10.7 20.9 %collective-permute-start.1 = (f32[2,2,4,4096]{3,2,1,0:T(4,128)S(1)}, f32[2,2,4,4096]{3,2,1,0:T(4,128)S(1)}, u32[]{:S(2)}, u32[]{:S(2)}) collective-permute-start(f32[2,2,4,4096]{3,2,1,0:T(4,128)S(1)} %get-tuple-element.16), channel_id=1, source_target_pairs={{1,0},{2,1},{3,2},{4,3},{5,4},{6,5},{7,6},{8,7},{9,8},{10,9},{11,1... | collective-permute-start | bytes 786440 | tf_op jit(solution)/shard_map/ppermute | solution.py:25
  13.7 17.9 %collective-permute-start = (f32[2,2,4,4096]{3,2,1,0:T(4,128)S(1)}, f32[2,2,4,4096]{3,2,1,0:T(4,128)S(1)}, u32[]{:S(2)}, u32[]{:S(2)}) collective-permute-start(f32[2,2,4,4096]{3,2,1,0:T(4,128)S(1)} %get-tuple-element.17), channel_id=1, source_target_pairs={{0,1},{1,2},{2,3},{3,4},{4,5},{5,6},{6,7},{7,8},{8,9},{9,10},{10,1... | collective-permute-start | bytes 786440 | tf_op jit(solution)/shard_map/ppermute | solution.py:25
  19.0 0.7 %copy-start.7 = (f32[2]{0:T(128)S(1)}, f32[2]{0:T(128)}, u32[]{:S(2)}) copy-start(f32[2]{0:T(128)} %param.12) | copy-start | bytes 28
  19.1 0.7 %copy-start.8 = (f32[4]{0:T(128)S(1)}, f32[4]{0:T(128)}, u32[]{:S(2)}) copy-start(f32[4]{0:T(128)} %constant.86) | copy-start | bytes 52
  20.9 6.2 %copy-start = (f32[10,8,4096]{2,1,0:T(8,128)}, f32[10,8,4096]{2,1,0:T(8,128)S(1)}, u32[]{:S(2)}) copy-start(f32[10,8,4096]{2,1,0:T(8,128)S(1)} %select_add_fusion.matched_ref) | copy-start | bytes 3932164
  21.9 5.1 %collective-permute-start.2 = (f32[3,4096]{1,0:T(4,128)S(1)}, f32[3,4096]{1,0:T(4,128)S(1)}, u32[]{:S(2)}, u32[]{:S(2)}) collective-permute-start(f32[3,4096]{1,0:T(4,128)S(1)} %concatenate.6), channel_id=1, source_target_pairs={{0,1},{1,2},{2,3},{3,4},{4,5},{5,6},{6,7},{7,8},{8,9},{9,10},{10,1... | collective-permute-start | bytes 147464 | tf_op jit(solution)/shard_map/ppermute | solution.py:25
  23.9 7.7 %collective-permute-start.3 = (f32[3,4096]{1,0:T(4,128)S(1)}, f32[3,4096]{1,0:T(4,128)S(1)}, u32[]{:S(2)}, u32[]{:S(2)}) collective-permute-start(f32[3,4096]{1,0:T(4,128)S(1)} %concatenate.7), channel_id=1, source_target_pairs={{1,0},{2,1},{3,2},{4,3},{5,4},{6,5},{7,6},{8,7},{9,8},{10,9},{11,1... | collective-permute-start | bytes 147464 | tf_op jit(solution)/shard_map/ppermute | solution.py:25
  27.0 4.5 %copy-start.5 = (f32[3,4096]{1,0:T(4,128)}, f32[3,4096]{1,0:T(4,128)S(1)}, u32[]{:S(2)}) copy-start(f32[3,4096]{1,0:T(4,128)S(1)} %collective-permute-done.2.dens_above_ref) | copy-start | bytes 147460
  31.6 0.6 %copy-start.6 = (f32[3,4096]{1,0:T(4,128)}, f32[3,4096]{1,0:T(4,128)S(1)}, u32[]{:S(2)}) copy-start(f32[3,4096]{1,0:T(4,128)S(1)} %collective-permute-done.3.dens_below_ref) | copy-start | bytes 147460
  31.6 0.7 %copy-start.3 = (f32[2,2,4,4096]{3,2,1,0:T(4,128)}, f32[2,2,4,4096]{3,2,1,0:T(4,128)S(1)}, u32[]{:S(2)}) copy-start(f32[2,2,4,4096]{3,2,1,0:T(4,128)S(1)} %collective-permute-done.1.src_below_ref) | copy-start | bytes 786436
  32.3 0.7 %copy-start.4 = (f32[2,2,4,4096]{3,2,1,0:T(4,128)}, f32[2,2,4,4096]{3,2,1,0:T(4,128)S(1)}, u32[]{:S(2)}) copy-start(f32[2,2,4,4096]{3,2,1,0:T(4,128)S(1)} %collective-permute-done.src_above_ref) | copy-start | bytes 786436
  39.5 13.2 %all-to-all-start.1 = ((f32[8,2,128]{2,1,0:T(2,128)}), f32[8,2,128]{2,1,0:T(2,128)S(1)}, u32[]{:S(2)}, u32[]{:S(2)}) async-start(f32[8,2,128]{2,1,0:T(2,128)} %get-tuple-element.5), calls=%async_computation.1 | async-start | bytes 16384 | tf_op jit(solution)/shard_map/all_to_all | solution.py:216

commit v14 on v13

--- a/solution.py
+++ b/solution.py
@@ -1,6 +1,5 @@
 import jax
 import jax.numpy as jnp
-import numpy as np
 from jax import lax
 from jax.experimental import pallas as pl
 from jax.experimental.pallas import tpu as pltpu
@@ -94,11 +93,20 @@
     hy_step = step_ref[...]
     inverse = jnp.where(hy_step > 0.0, time_step / (1.0 + high_contrast * density), 0.0)
     sense_ref[...] = jnp.zeros((rows, cols), jnp.float32)
+    drives = [
+        [
+            jnp.concatenate(
+                [jnp.sin(jnp.full((rows, 128), drive_ref[wave] * (turn + 1.0), jnp.float32))] * (cols // 128), axis=1
+            )
+            for wave in range(waves)
+        ]
+        for turn in range(ITERS)
+    ]
     for wave in range(waves):
         for run in range(runs):
             field_e = field_hx = field_hy = current = None
             for turn in range(ITERS):
-                drive_term = drive_ref[turn, wave] * source_ref[run, wave]
+                drive_term = drives[turn][wave] * source_ref[run, wave]
                 if field_e is None:
                     field_e = drive_term
                 else:
@@ -208,9 +216,8 @@
     above = from_behind(jnp.concatenate([last_rows, present]), "tile", 1)
     below = from_behind(jnp.concatenate([present, first_rows]), "tile", -1)
     density_cell = jnp.sum(matched * candidates[:, None, :], axis=0)
-    drive = jnp.sin(omega[None, :] * np.arange(1.0, ITERS + 1.0, dtype=np.float32)[:, None])
     final, pieces = march(
-        drive, source_fwd, source_adj, src_above, src_below, density_cell, above, below, matched, block_rows, chunks
+        omega, source_fwd, source_adj, src_above, src_below, density_cell, above, below, matched, block_rows, chunks
     )
     count = lax.axis_size("wl")
     density_grad = lax.all_to_all(

time: 53.7 us -> 52.7 us (0.981)
  other arithmetic: 4.81 us -> 4.13 us
    sin x1 -> x0, other arithmetic: 0.69 us -> none  [shards(): jnp.sin(omega[None, :] * np.arange(1.0, ITERS + 1.0, dtype=np.float32)[:,...]
    unnamed x18 -> x14, local copies, waits for them, and re-layouts: 1.95 us -> 1.45 us
  transfers between devices with their start and end apart: 6 -> 6, of which waited for: 2 -> 2; matrix products, arithmetic and copies ran while one was open for 12% -> 11% of each run, Pallas kernels for 0% -> 0%
where the time goes in v14:
time: 52.7 us; the launch traced here: 52.3 us
  starting transfers between devices  26.1 us (50%)
  waiting for transfers between devices  9.28 us (18%)
  Pallas kernels  6.7 us (13%)
  local copies, waits for them, and re-layouts  4.96 us (9%)
  other arithmetic  4.13 us (8%)
  between operations  0.84 us (2%)
    ppermute x4, starting transfers between devices, from_behind(): lax.ppermute(value, axis, [(source, source + steps) for source in range(f...  12.1 us
    all_to_all x1, starting transfers between devices, gather_columns(): pieces = lax.all_to_all(copies, axis, 0, 0, tiled=True)  7.33 us
    pallas_call x1, Pallas kernels, march(): pl.pallas_call(march_kernel, out_shape=(jax.ShapeDtypeStruct((waves, rows...  6.7 us
    all_to_all x1, starting transfers between devices, shards(): lax.all_to_all(pieces.reshape(count, chunks // count, block_rows, span).t...  6.65 us
    all_to_all x1, waiting for transfers between devices, shards(): lax.all_to_all(pieces.reshape(count, chunks // count, block_rows, span).t...  4.76 us
    ppermute x4, waiting for transfers between devices, from_behind(): lax.ppermute(value, axis, [(source, source + steps) for source in range(f...  4.52 us
    slice x1, local copies, waits for them, and re-layouts, shards(): return (final[:, HALO:HALO + cells_x], density_grad)  1.77 us
    unnamed x14, local copies, waits for them, and re-layouts  1.45 us
  transfers between devices with their start and end apart: 6, of which 2 were waited for; matrix products, arithmetic and copies ran while one was open for 11% of the time, Pallas kernels for 0%

profile of v14, /device:TPU:25, one launch (start us, length us, event | category | flops | bytes accessed | tf_op | source)
XLA Modules:
  0.0 52.3 jit_solution(14638121609233168939)
XLA Ops:
  0.6 0.0 copy-start.1
  0.6 1.3 %broadcast_in_dim.55 = f32[8,2,128]{2,1,0:T(2,128)} broadcast(f32[2,128]{1,0:T(2,128)} %param.6), dimensions={1,2} | broadcast | bytes 9216 | tf_op jit(solution)/shard_map/broadcast_in_dim | solution.py:35
  2.0 7.3 %all-to-all-start = ((f32[8,2,128]{2,1,0:T(2,128)}), f32[8,2,128]{2,1,0:T(2,128)S(1)}, u32[]{:S(2)}, u32[]{:S(2)}) async-start(f32[8,2,128]{2,1,0:T(2,128)} %broadcast_in_dim.55), calls=%async_computation | async-start | bytes 16384 | tf_op jit(solution)/shard_map/all_to_all | solution.py:36
  9.3 1.3 %pad_maximum_fusion = (f32[2,2,4,4096]{3,2,1,0:T(4,128)S(1)}, f32[2,2,4,4096]{3,2,1,0:T(4,128)S(1)}) fusion(f32[1,2,8,4096]{3,2,1,0:T(8,128)} %bitcast.35, f32[1,2,8,4096]{3,2,1,0:T(8,128)} %bitcast.34), kind=kLoop, calls=%fused_computation.27 | loop fusion | flops 131072 | bytes 1048576 | tf_op jit(solution)/shard_map/stack | solution.py:186
  10.7 0.0 copy-start.2
  10.7 3.0 %collective-permute-start.1 = (f32[2,2,4,4096]{3,2,1,0:T(4,128)S(1)}, f32[2,2,4,4096]{3,2,1,0:T(4,128)S(1)}, u32[]{:S(2)}, u32[]{:S(2)}) collective-permute-start(f32[2,2,4,4096]{3,2,1,0:T(4,128)S(1)} %get-tuple-element.16), channel_id=1, source_target_pairs={{1,0},{2,1},{3,2},{4,3},{5,4},{6,5},{7,6},{8,7},{9,8},{10,9},{11,1... | collective-permute-start | bytes 786440 | tf_op jit(solution)/shard_map/ppermute | solution.py:24
  13.7 4.8 %collective-permute-start = (f32[2,2,4,4096]{3,2,1,0:T(4,128)S(1)}, f32[2,2,4,4096]{3,2,1,0:T(4,128)S(1)}, u32[]{:S(2)}, u32[]{:S(2)}) collective-permute-start(f32[2,2,4,4096]{3,2,1,0:T(4,128)S(1)} %get-tuple-element.17), channel_id=1, source_target_pairs={{0,1},{1,2},{2,3},{3,4},{4,5},{5,6},{6,7},{7,8},{8,9},{9,10},{10,1... | collective-permute-start | bytes 786440 | tf_op jit(solution)/shard_map/ppermute | solution.py:24
  18.5 0.5 fusion.2
  19.2 0.5 select_add_fusion.matched_ref
  19.7 0.0 copy-start
  19.7 0.0 all-to-all-done
  19.7 0.1 pad_slice_fusion.4
  19.8 0.1 pad_slice_fusion.8
  19.9 0.1 stack.49
  20.0 0.2 fusion.11
  20.3 0.4 fusion.8
  20.7 1.9 %collective-permute-start.2 = (f32[3,4096]{1,0:T(4,128)S(1)}, f32[3,4096]{1,0:T(4,128)S(1)}, u32[]{:S(2)}, u32[]{:S(2)}) collective-permute-start(f32[3,4096]{1,0:T(4,128)S(1)} %concatenate.6), channel_id=1, source_target_pairs={{0,1},{1,2},{2,3},{3,4},{4,5},{5,6},{6,7},{7,8},{8,9},{9,10},{10,1... | collective-permute-start | bytes 147464 | tf_op jit(solution)/shard_map/ppermute | solution.py:24
  22.7 2.4 %collective-permute-start.3 = (f32[3,4096]{1,0:T(4,128)S(1)}, f32[3,4096]{1,0:T(4,128)S(1)}, u32[]{:S(2)}, u32[]{:S(2)}) collective-permute-start(f32[3,4096]{1,0:T(4,128)S(1)} %concatenate.7), channel_id=1, source_target_pairs={{1,0},{2,1},{3,2},{4,3},{5,4},{6,5},{7,6},{8,7},{9,8},{10,9},{11,1... | collective-permute-start | bytes 147464 | tf_op jit(solution)/shard_map/ppermute | solution.py:24
  25.1 0.8 %multiply_reduce_fusion.dens_ref = f32[8,4096]{1,0:T(8,128)} fusion(f32[10,8,4096]{2,1,0:T(8,128)S(1)} %select_add_fusion.matched_ref, f32[10,4096]{1,0:T(8,128)S(1)} %mul.32), kind=kLoop, calls=%fused_computation | loop fusion | flops 622592 | bytes 1605632 | tf_op jit(solution)/shard_map/reduce_sum | solution.py:218
  25.8 0.0 copy-done
  25.8 0.0 collective-permute-done.2.dens_above_ref
  25.8 4.5 %collective-permute-done.3.dens_below_ref = f32[3,4096]{1,0:T(4,128)S(1)} collective-permute-done((f32[3,4096]{1,0:T(4,128)S(1)}, f32[3,4096]{1,0:T(4,128)S(1)}, u32[]{:S(2)}, u32[]{:S(2)}) %collective-permute-start.3) | collective-permute-done | bytes 49184 | tf_op jit(solution)/shard_map/ppermute | solution.py:24
  30.3 0.0 collective-permute-done.1.src_below_ref
  30.4 0.0 collective-permute-done.src_above_ref
  30.4 0.6 %copy-done.6 = f32[3,4096]{1,0:T(4,128)} copy-done((f32[3,4096]{1,0:T(4,128)}, f32[3,4096]{1,0:T(4,128)S(1)}, u32[]{:S(2)}) %copy-start.6) | copy-done | bytes 49176
  31.0 0.1 copy-done.3
  31.1 0.7 %copy-done.4 = f32[2,2,4,4096]{3,2,1,0:T(4,128)} copy-done((f32[2,2,4,4096]{3,2,1,0:T(4,128)}, f32[2,2,4,4096]{3,2,1,0:T(4,128)S(1)}, u32[]{:S(2)}) %copy-start.4) | copy-done | bytes 262168
  31.8 6.7 %shard_map.77 = (f32[2,16,4096]{2,1,0:T(8,128)}, f32[8,2,128]{2,1,0:T(2,128)}) custom-call(f32[2]{0:T(128)} %drive_ref.1, f32[2,8,4096]{2,1,0:T(8,128)} %fwd_ref.1, f32[2,8,4096]{2,1,0:T(8,128)} %adj_ref.1, f32[2,2,4,4096]{3,2,1,0:T(4,128)} %copy-done.4, f32[2,2,4,4096]{3,2,1,0:T(4,128)} %copy-done.3, f32[8,4096]{1,0:T(8,128)} %multiply_reduce_fusion.dens_ref, ...), custom_call_target="tpu_custom_call" | custom-call | tf_op jit(solution)/shard_map/pallas_call | solution.py:166
  38.5 6.6 %all-to-all-start.1 = ((f32[8,2,128]{2,1,0:T(2,128)}), f32[8,2,128]{2,1,0:T(2,128)S(1)}, u32[]{:S(2)}, u32[]{:S(2)}) async-start(f32[8,2,128]{2,1,0:T(2,128)} %get-tuple-element.5), calls=%async_computation.1 | async-start | bytes 16384 | tf_op jit(solution)/shard_map/all_to_all | solution.py:223
  45.1 1.8 %slice.107 = f32[2,8,4096]{2,1,0:T(8,128)} slice(f32[2,16,4096]{2,1,0:T(8,128)} %get-tuple-element.4), slice={[0:2], [4:12], [0:4096]} | slice | bytes 524288 | tf_op jit(solution)/shard_map/slice | solution.py:227
  46.9 4.8 %all-to-all-done.1 = f32[8,2,128]{2,1,0:T(2,128)S(1)} async-done(((f32[8,2,128]{2,1,0:T(2,128)}), f32[8,2,128]{2,1,0:T(2,128)S(1)}, u32[]{:S(2)}, u32[]{:S(2)}) %all-to-all-start.1) | async-done | bytes 8224 | tf_op jit(solution)/shard_map/all_to_all | solution.py:223
  51.7 0.6 %reduce_sum.39 = f32[2,128]{1,0:T(2,128)} reduce(f32[8,2,128]{2,1,0:T(2,128)S(1)} %all-to-all-done.1, f32[]{:T(128)} %constant.63.clone.1), dimensions={0}, to_apply=%region_3.4 | reduce | flops 1792 | bytes 9220 | tf_op jit(solution)/shard_map/reduce_sum | solution.py:226
  (18 shorter events, 0.2 us)
Async XLA Ops:
  0.6 17.9 %copy-start.1 = (s32[4,8,4096]{2,1,0:T(8,128)S(1)}, s32[4,8,4096]{2,1,0:T(8,128)}, u32[]{:S(2)}) copy-start(s32[4,8,4096]{2,1,0:T(8,128)} %param.7) | copy-start | bytes 1572868
  2.0 17.7 %all-to-all-start = ((f32[8,2,128]{2,1,0:T(2,128)}), f32[8,2,128]{2,1,0:T(2,128)S(1)}, u32[]{:S(2)}, u32[]{:S(2)}) async-start(f32[8,2,128]{2,1,0:T(2,128)} %broadcast_in_dim.55), calls=%async_computation | async-start | bytes 16384 | tf_op jit(solution)/shard_map/all_to_all | solution.py:36
  10.7 8.4 %copy-start.2 = (bf16[4,8,4096]{2,1,0:T(8,128)(2,1)S(1)}, bf16[4,8,4096]{2,1,0:T(8,128)(2,1)}, u32[]{:S(2)}) copy-start(bf16[4,8,4096]{2,1,0:T(8,128)(2,1)} %param.8) | copy-start | bytes 786436
  10.7 19.7 %collective-permute-start.1 = (f32[2,2,4,4096]{3,2,1,0:T(4,128)S(1)}, f32[2,2,4,4096]{3,2,1,0:T(4,128)S(1)}, u32[]{:S(2)}, u32[]{:S(2)}) collective-permute-start(f32[2,2,4,4096]{3,2,1,0:T(4,128)S(1)} %get-tuple-element.16), channel_id=1, source_target_pairs={{1,0},{2,1},{3,2},{4,3},{5,4},{6,5},{7,6},{8,7},{9,8},{10,9},{11,1... | collective-permute-start | bytes 786440 | tf_op jit(solution)/shard_map/ppermute | solution.py:24
  13.7 16.7 %collective-permute-start = (f32[2,2,4,4096]{3,2,1,0:T(4,128)S(1)}, f32[2,2,4,4096]{3,2,1,0:T(4,128)S(1)}, u32[]{:S(2)}, u32[]{:S(2)}) collective-permute-start(f32[2,2,4,4096]{3,2,1,0:T(4,128)S(1)} %get-tuple-element.17), channel_id=1, source_target_pairs={{0,1},{1,2},{2,3},{3,4},{4,5},{5,6},{6,7},{7,8},{8,9},{9,10},{10,1... | collective-permute-start | bytes 786440 | tf_op jit(solution)/shard_map/ppermute | solution.py:24
  19.7 6.2 %copy-start = (f32[10,8,4096]{2,1,0:T(8,128)}, f32[10,8,4096]{2,1,0:T(8,128)S(1)}, u32[]{:S(2)}) copy-start(f32[10,8,4096]{2,1,0:T(8,128)S(1)} %select_add_fusion.matched_ref) | copy-start | bytes 3932164
  20.7 5.1 %collective-permute-start.2 = (f32[3,4096]{1,0:T(4,128)S(1)}, f32[3,4096]{1,0:T(4,128)S(1)}, u32[]{:S(2)}, u32[]{:S(2)}) collective-permute-start(f32[3,4096]{1,0:T(4,128)S(1)} %concatenate.6), channel_id=1, source_target_pairs={{0,1},{1,2},{2,3},{3,4},{4,5},{5,6},{6,7},{7,8},{8,9},{9,10},{10,1... | collective-permute-start | bytes 147464 | tf_op jit(solution)/shard_map/ppermute | solution.py:24
  22.7 7.7 %collective-permute-start.3 = (f32[3,4096]{1,0:T(4,128)S(1)}, f32[3,4096]{1,0:T(4,128)S(1)}, u32[]{:S(2)}, u32[]{:S(2)}) collective-permute-start(f32[3,4096]{1,0:T(4,128)S(1)} %concatenate.7), channel_id=1, source_target_pairs={{1,0},{2,1},{3,2},{4,3},{5,4},{6,5},{7,6},{8,7},{9,8},{10,9},{11,1... | collective-permute-start | bytes 147464 | tf_op jit(solution)/shard_map/ppermute | solution.py:24
  25.8 4.5 %copy-start.5 = (f32[3,4096]{1,0:T(4,128)}, f32[3,4096]{1,0:T(4,128)S(1)}, u32[]{:S(2)}) copy-start(f32[3,4096]{1,0:T(4,128)S(1)} %collective-permute-done.2.dens_above_ref) | copy-start | bytes 147460
  30.3 0.6 %copy-start.6 = (f32[3,4096]{1,0:T(4,128)}, f32[3,4096]{1,0:T(4,128)S(1)}, u32[]{:S(2)}) copy-start(f32[3,4096]{1,0:T(4,128)S(1)} %collective-permute-done.3.dens_below_ref) | copy-start | bytes 147460
  30.4 0.7 %copy-start.3 = (f32[2,2,4,4096]{3,2,1,0:T(4,128)}, f32[2,2,4,4096]{3,2,1,0:T(4,128)S(1)}, u32[]{:S(2)}) copy-start(f32[2,2,4,4096]{3,2,1,0:T(4,128)S(1)} %collective-permute-done.1.src_below_ref) | copy-start | bytes 786436
  31.1 0.7 %copy-start.4 = (f32[2,2,4,4096]{3,2,1,0:T(4,128)}, f32[2,2,4,4096]{3,2,1,0:T(4,128)S(1)}, u32[]{:S(2)}) copy-start(f32[2,2,4,4096]{3,2,1,0:T(4,128)S(1)} %collective-permute-done.src_above_ref) | copy-start | bytes 786436
  38.5 13.2 %all-to-all-start.1 = ((f32[8,2,128]{2,1,0:T(2,128)}), f32[8,2,128]{2,1,0:T(2,128)S(1)}, u32[]{:S(2)}, u32[]{:S(2)}) async-start(f32[8,2,128]{2,1,0:T(2,128)} %get-tuple-element.5), calls=%async_computation.1 | async-start | bytes 16384 | tf_op jit(solution)/shard_map/all_to_all | solution.py:223

commit v15 on v14

--- a/solution.py
+++ b/solution.py
@@ -132,7 +132,7 @@
                 else:
                     sense_ref[...] += field_e * history_ref[ITERS - 1 - turn]
             if run == 0:
-                final_ref[wave] = field_e
+                final_ref[wave] = history_ref[ITERS - 1, HALO : HALO + own]
     scaled = GRAD_SCALE * sense_ref[HALO : HALO + own]
     lane = lax.broadcasted_iota(jnp.int32, (1, cols), 1)
     for row in range(block_rows):
@@ -166,7 +166,7 @@
     return pl.pallas_call(
         march_kernel,
         out_shape=(
-            jax.ShapeDtypeStruct((waves, rows, cols), jnp.float32),
+            jax.ShapeDtypeStruct((waves, fwd.shape[1], cols), jnp.float32),
             jax.ShapeDtypeStruct((chunks, block_rows, 128), jnp.float32),
         ),
         in_specs=[pl.BlockSpec(memory_space=smem)] + [pl.BlockSpec(memory_space=vmem)] * 8,
@@ -198,7 +198,6 @@
     matched = jnp.zeros((block_rows * len(SHIFTS), cells_x, cells_y), jnp.float32)
     for entry in range(foot_index.shape[0]):
         matched = matched + jnp.where(key[entry][None] == codes, weights[entry][None], 0.0)
-    matched = lax.optimization_barrier(matched)
     span = 128
     chunks = block_cols // span
     spread = (
@@ -224,7 +223,7 @@
         pieces.reshape(count, chunks // count, block_rows, span).transpose(0, 2, 1, 3).reshape(count, block_rows, -1),
         "wl", 0, 0, tiled=True,
     ).sum(axis=0)
-    return (final[:, HALO : HALO + cells_x], density_grad)
+    return (final, density_grad)
 
 
 def solution(mesh):

time: 52.7 us -> 52.7 us (level)
  blocking collectives: 0 us -> 13.2 us
  starting transfers between devices: 26.1 us -> 19.5 us
  waiting for transfers between devices: 9.28 us -> 5.27 us
  local copies, waits for them, and re-layouts: 4.96 us -> 2.46 us
    all_to_all x0 -> x1, blocking collectives: none -> 13.2 us  [shards(): lax.all_to_all(pieces.reshape(count, chunks // count, block_rows, span).t...]
    all_to_all x1 -> x0, starting transfers between devices: 6.65 us -> none  [shards(): lax.all_to_all(pieces.reshape(count, chunks // count, block_rows, span).t...]
    all_to_all x1 -> x0, waiting for transfers between devices: 4.76 us -> none  [shards(): lax.all_to_all(pieces.reshape(count, chunks // count, block_rows, span).t...]
    slice x1 -> x0, local copies, waits for them, and re-layouts: 1.77 us -> none  [shards(): return (final[:, HALO:HALO + cells_x], density_grad)]
    reduce_sum x1 -> x0, other arithmetic: 0.76 us -> none  [shards(): density_cell = jnp.sum(matched * candidates[:, None, :], axis=0)]
    ppermute x4, waiting for transfers between devices: 4.52 us -> 5.27 us  [from_behind(): lax.ppermute(value, axis, [(source, source + steps) for source in range(f...]
    unnamed x14 -> x12, local copies, waits for them, and re-layouts: 1.45 us -> 0.71 us
    add x1, other arithmetic: 0.47 us -> 1.19 us  [shards(): matched + jnp.where(key[entry][None] == codes, weights[entry][None], 0.0)]
  transfers between devices with their start and end apart: 6 -> 5, of which waited for: 2 -> 1; matrix products, arithmetic and copies ran while one was open for 11% -> 8% of each run, Pallas kernels for 0% -> 0%
where the time goes in v15:
time: 52.7 us; the launch traced here: 52.3 us
  starting transfers between devices  19.5 us (37%)
  blocking collectives  13.2 us (25%)
  Pallas kernels  6.8 us (13%)
  waiting for transfers between devices  5.27 us (10%)
  other arithmetic  4.08 us (8%)
  local copies, waits for them, and re-layouts  2.46 us (5%)
  between operations  0.84 us (2%)
    all_to_all x1, blocking collectives, shards(): lax.all_to_all(pieces.reshape(count, chunks // count, block_rows, span).t...  13.2 us
    ppermute x4, starting transfers between devices, from_behind(): lax.ppermute(value, axis, [(source, source + steps) for source in range(f...  12.1 us
    all_to_all x1, starting transfers between devices, gather_columns(): pieces = lax.all_to_all(copies, axis, 0, 0, tiled=True)  7.33 us
    pallas_call x1, Pallas kernels, march(): pl.pallas_call(march_kernel, out_shape=(jax.ShapeDtypeStruct((waves, fwd....  6.8 us
    ppermute x4, waiting for transfers between devices, from_behind(): lax.ppermute(value, axis, [(source, source + steps) for source in range(f...  5.27 us
    another operation x1, other arithmetic, shards(): sources = jnp.stack([source_fwd, source_adj])  1.35 us
    broadcast_in_dim x1, local copies, waits for them, and re-layouts, gather_columns(): copies = jnp.broadcast_to(value[None], (count,) + value.shape)  1.34 us
    add x1, other arithmetic, shards(): matched + jnp.where(key[entry][None] == codes, weights[entry][None], 0.0)  1.19 us
  transfers between devices with their start and end apart: 5, of which 1 were waited for; matrix products, arithmetic and copies ran while one was open for 8% of the time, Pallas kernels for 0%

profile of v15, /device:TPU:25, one launch (start us, length us, event | category | flops | bytes accessed | tf_op | source)
XLA Modules:
  0.0 52.3 jit_solution(4559115698021150660)
XLA Ops:
  0.6 0.0 copy-start.1
  0.6 1.3 %broadcast_in_dim.55 = f32[8,2,128]{2,1,0:T(2,128)} broadcast(f32[2,128]{1,0:T(2,128)} %param.6), dimensions={1,2} | broadcast | bytes 9216 | tf_op jit(solution)/shard_map/broadcast_in_dim | solution.py:35
  2.0 7.3 %all-to-all-start = ((f32[8,2,128]{2,1,0:T(2,128)}), f32[8,2,128]{2,1,0:T(2,128)S(1)}, u32[]{:S(2)}, u32[]{:S(2)}) async-start(f32[8,2,128]{2,1,0:T(2,128)} %broadcast_in_dim.55), calls=%async_computation | async-start | bytes 16384 | tf_op jit(solution)/shard_map/all_to_all | solution.py:36
  9.3 1.3 %pad_maximum_fusion = (f32[2,2,4,4096]{3,2,1,0:T(4,128)S(1)}, f32[2,2,4,4096]{3,2,1,0:T(4,128)S(1)}) fusion(f32[1,2,8,4096]{3,2,1,0:T(8,128)} %bitcast.35, f32[1,2,8,4096]{3,2,1,0:T(8,128)} %bitcast.34), kind=kLoop, calls=%fused_computation.27 | loop fusion | flops 131072 | bytes 1048576 | tf_op jit(solution)/shard_map/stack | solution.py:186
  10.7 0.0 copy-start.2
  10.7 3.0 %collective-permute-start.1 = (f32[2,2,4,4096]{3,2,1,0:T(4,128)S(1)}, f32[2,2,4,4096]{3,2,1,0:T(4,128)S(1)}, u32[]{:S(2)}, u32[]{:S(2)}) collective-permute-start(f32[2,2,4,4096]{3,2,1,0:T(4,128)S(1)} %get-tuple-element.18), channel_id=1, source_target_pairs={{1,0},{2,1},{3,2},{4,3},{5,4},{6,5},{7,6},{8,7},{9,8},{10,9},{11,1... | collective-permute-start | bytes 786440 | tf_op jit(solution)/shard_map/ppermute | solution.py:24
  13.7 4.8 %collective-permute-start = (f32[2,2,4,4096]{3,2,1,0:T(4,128)S(1)}, f32[2,2,4,4096]{3,2,1,0:T(4,128)}, u32[]{:S(2)}, u32[]{:S(2)}) collective-permute-start(f32[2,2,4,4096]{3,2,1,0:T(4,128)S(1)} %get-tuple-element.19), channel_id=1, source_target_pairs={{0,1},{1,2},{2,3},{3,4},{4,5},{5,6},{6,7},{7,8},{8,9},{9,10},{10,1... | collective-permute-start | bytes 786440 | tf_op jit(solution)/shard_map/ppermute | solution.py:24
  18.5 0.0 copy-done.1
  18.5 0.5 fusion.2
  19.1 0.0 copy-done.2
  19.2 0.0 all-to-all-done
  19.2 0.1 pad_slice_fusion.4
  19.3 0.1 pad_slice_fusion.8
  19.4 0.1 stack.49
  19.5 0.2 fusion.11
  19.8 1.2 %select_add_fusion = (f32[10,8,4096]{2,1,0:T(8,128)S(1)}, f32[8,4096]{1,0:T(8,128)}) fusion(f32[8,4096]{1,0:T(8,128)S(1)} %get-tuple-element.15, s32[8,4096]{1,0:T(8,128)S(1)} %get-tuple-element.11, f32[8,4096]{1,0:T(8,128)S(1)} %get-tuple-element.16, s32[8,4096]{1,0:T(8,128)S(1)} %get-tuple-element.12, f32[8,4096]{1,0:T(8,128)S(1)} %get-tuple-element.17, ...), kind=kLoop, calls=%fused_computation.1 | loop fusion | flops 4227072 | bytes 2654208 | tf_op jit(solution)/shard_map/add | solution.py:200
  21.0 0.0 copy-start
  21.0 0.4 fusion.8
  21.4 1.9 %collective-permute-start.2 = (f32[3,4096]{1,0:T(4,128)S(1)}, f32[3,4096]{1,0:T(4,128)S(1)}, u32[]{:S(2)}, u32[]{:S(2)}) collective-permute-start(f32[3,4096]{1,0:T(4,128)S(1)} %concatenate.6), channel_id=1, source_target_pairs={{0,1},{1,2},{2,3},{3,4},{4,5},{5,6},{6,7},{7,8},{8,9},{9,10},{10,1... | collective-permute-start | bytes 147464 | tf_op jit(solution)/shard_map/ppermute | solution.py:24
  23.4 2.4 %collective-permute-start.3 = (f32[3,4096]{1,0:T(4,128)S(1)}, f32[3,4096]{1,0:T(4,128)S(1)}, u32[]{:S(2)}, u32[]{:S(2)}) collective-permute-start(f32[3,4096]{1,0:T(4,128)S(1)} %concatenate.7), channel_id=1, source_target_pairs={{1,0},{2,1},{3,2},{4,3},{5,4},{6,5},{7,6},{8,7},{9,8},{10,9},{11,1... | collective-permute-start | bytes 147464 | tf_op jit(solution)/shard_map/ppermute | solution.py:24
  25.8 0.0 collective-permute-done.2.dens_above_ref
  25.8 0.0 copy-start.4
  25.8 5.3 %collective-permute-done.3.dens_below_ref = f32[3,4096]{1,0:T(4,128)S(1)} collective-permute-done((f32[3,4096]{1,0:T(4,128)S(1)}, f32[3,4096]{1,0:T(4,128)S(1)}, u32[]{:S(2)}, u32[]{:S(2)}) %collective-permute-start.3) | collective-permute-done | bytes 49184 | tf_op jit(solution)/shard_map/ppermute | solution.py:24
  31.1 0.0 collective-permute-done.1.src_below_ref
  31.1 0.0 collective-permute-done.src_above_ref
  31.1 0.0 copy-done
  31.1 0.0 copy-done.4
  31.1 0.6 %copy-done.5 = f32[3,4096]{1,0:T(4,128)} copy-done((f32[3,4096]{1,0:T(4,128)}, f32[3,4096]{1,0:T(4,128)S(1)}, u32[]{:S(2)}) %copy-start.5) | copy-done | bytes 49176
  31.7 0.1 copy-done.3
  31.8 6.8 %shard_map.77 = (f32[2,8,4096]{2,1,0:T(8,128)}, f32[8,2,128]{2,1,0:T(2,128)}) custom-call(f32[2]{0:T(128)} %drive_ref.1, f32[2,8,4096]{2,1,0:T(8,128)} %fwd_ref.1, f32[2,8,4096]{2,1,0:T(8,128)} %adj_ref.1, f32[2,2,4,4096]{3,2,1,0:T(4,128)} %collective-permute-done.src_above_ref, f32[2,2,4,4096]{3,2,1,0:T(4,128)} %copy-done.3, ...), custom_call_target="tpu_custom_call" | custom-call | tf_op jit(solution)/shard_map/pallas_call | solution.py:166
  38.6 13.2 %all_to_all.10 = f32[8,2,128]{2,1,0:T(2,128)S(1)} all-to-all(f32[8,2,128]{2,1,0:T(2,128)} %get-tuple-element.5), channel_id=1, replica_groups=mesh['wl'=8,'tile'=16] {'wl'}, dimensions={0} | all-to-all | bytes 16384 | tf_op jit(solution)/shard_map/all_to_all | solution.py:222
  51.7 0.6 %reduce_sum.39 = f32[2,128]{1,0:T(2,128)} reduce(f32[8,2,128]{2,1,0:T(2,128)S(1)} %all_to_all.10, f32[]{:T(128)} %constant.63.clone.1), dimensions={0}, to_apply=%region_3.4 | reduce | flops 1792 | bytes 9220 | tf_op jit(solution)/shard_map/reduce_sum | solution.py:225
  (13 shorter events, 0.2 us)
Async XLA Ops:
  0.6 17.9 %copy-start.1 = (s32[4,8,4096]{2,1,0:T(8,128)S(1)}, s32[4,8,4096]{2,1,0:T(8,128)}, u32[]{:S(2)}) copy-start(s32[4,8,4096]{2,1,0:T(8,128)} %param.7) | copy-start | bytes 1572868
  2.0 17.2 %all-to-all-start = ((f32[8,2,128]{2,1,0:T(2,128)}), f32[8,2,128]{2,1,0:T(2,128)S(1)}, u32[]{:S(2)}, u32[]{:S(2)}) async-start(f32[8,2,128]{2,1,0:T(2,128)} %broadcast_in_dim.55), calls=%async_computation | async-start | bytes 16384 | tf_op jit(solution)/shard_map/all_to_all | solution.py:36
  10.7 8.4 %copy-start.2 = (bf16[4,8,4096]{2,1,0:T(8,128)(2,1)S(1)}, bf16[4,8,4096]{2,1,0:T(8,128)(2,1)}, u32[]{:S(2)}) copy-start(bf16[4,8,4096]{2,1,0:T(8,128)(2,1)} %param.8) | copy-start | bytes 786436
  10.7 20.4 %collective-permute-start.1 = (f32[2,2,4,4096]{3,2,1,0:T(4,128)S(1)}, f32[2,2,4,4096]{3,2,1,0:T(4,128)S(1)}, u32[]{:S(2)}, u32[]{:S(2)}) collective-permute-start(f32[2,2,4,4096]{3,2,1,0:T(4,128)S(1)} %get-tuple-element.18), channel_id=1, source_target_pairs={{1,0},{2,1},{3,2},{4,3},{5,4},{6,5},{7,6},{8,7},{9,8},{10,9},{11,1... | collective-permute-start | bytes 786440 | tf_op jit(solution)/shard_map/ppermute | solution.py:24
  13.7 17.4 %collective-permute-start = (f32[2,2,4,4096]{3,2,1,0:T(4,128)S(1)}, f32[2,2,4,4096]{3,2,1,0:T(4,128)}, u32[]{:S(2)}, u32[]{:S(2)}) collective-permute-start(f32[2,2,4,4096]{3,2,1,0:T(4,128)S(1)} %get-tuple-element.19), channel_id=1, source_target_pairs={{0,1},{1,2},{2,3},{3,4},{4,5},{5,6},{6,7},{7,8},{8,9},{9,10},{10,1... | collective-permute-start | bytes 786440 | tf_op jit(solution)/shard_map/ppermute | solution.py:24
  21.0 10.1 %copy-start = (f32[10,8,4096]{2,1,0:T(8,128)}, f32[10,8,4096]{2,1,0:T(8,128)S(1)}, u32[]{:S(2)}) copy-start(f32[10,8,4096]{2,1,0:T(8,128)S(1)} %get-tuple-element.8.matched_ref) | copy-start | bytes 3932164
  21.4 4.3 %collective-permute-start.2 = (f32[3,4096]{1,0:T(4,128)S(1)}, f32[3,4096]{1,0:T(4,128)S(1)}, u32[]{:S(2)}, u32[]{:S(2)}) collective-permute-start(f32[3,4096]{1,0:T(4,128)S(1)} %concatenate.6), channel_id=1, source_target_pairs={{0,1},{1,2},{2,3},{3,4},{4,5},{5,6},{6,7},{7,8},{8,9},{9,10},{10,1... | collective-permute-start | bytes 147464 | tf_op jit(solution)/shard_map/ppermute | solution.py:24
  23.4 7.7 %collective-permute-start.3 = (f32[3,4096]{1,0:T(4,128)S(1)}, f32[3,4096]{1,0:T(4,128)S(1)}, u32[]{:S(2)}, u32[]{:S(2)}) collective-permute-start(f32[3,4096]{1,0:T(4,128)S(1)} %concatenate.7), channel_id=1, source_target_pairs={{1,0},{2,1},{3,2},{4,3},{5,4},{6,5},{7,6},{8,7},{9,8},{10,9},{11,1... | collective-permute-start | bytes 147464 | tf_op jit(solution)/shard_map/ppermute | solution.py:24
  25.8 5.3 %copy-start.4 = (f32[3,4096]{1,0:T(4,128)}, f32[3,4096]{1,0:T(4,128)S(1)}, u32[]{:S(2)}) copy-start(f32[3,4096]{1,0:T(4,128)S(1)} %collective-permute-done.2.dens_above_ref) | copy-start | bytes 147460
  31.1 0.6 %copy-start.5 = (f32[3,4096]{1,0:T(4,128)}, f32[3,4096]{1,0:T(4,128)S(1)}, u32[]{:S(2)}) copy-start(f32[3,4096]{1,0:T(4,128)S(1)} %collective-permute-done.3.dens_below_ref) | copy-start | bytes 147460
  31.1 0.7 %copy-start.3 = (f32[2,2,4,4096]{3,2,1,0:T(4,128)}, f32[2,2,4,4096]{3,2,1,0:T(4,128)S(1)}, u32[]{:S(2)}) copy-start(f32[2,2,4,4096]{3,2,1,0:T(4,128)S(1)} %collective-permute-done.1.src_below_ref) | copy-start | bytes 786436

commit v16 on v15

--- a/solution.py
+++ b/solution.py
@@ -198,6 +198,7 @@
     matched = jnp.zeros((block_rows * len(SHIFTS), cells_x, cells_y), jnp.float32)
     for entry in range(foot_index.shape[0]):
         matched = matched + jnp.where(key[entry][None] == codes, weights[entry][None], 0.0)
+    matched = lax.optimization_barrier(matched)
     span = 128
     chunks = block_cols // span
     spread = (

time: 52.7 us -> 52.7 us (level)
  waiting for transfers between devices: 5.27 us -> 4.52 us
  local copies, waits for them, and re-layouts: 2.46 us -> 3.17 us
    reduce_sum x0 -> x1, other arithmetic: none -> 0.76 us  [shards(): density_cell = jnp.sum(matched * candidates[:, None, :], axis=0)]
    ppermute x4, waiting for transfers between devices: 5.27 us -> 4.52 us  [from_behind(): lax.ppermute(value, axis, [(source, source + steps) for source in range(f...]
    add x1, other arithmetic: 1.19 us -> 0.47 us  [shards(): matched + jnp.where(key[entry][None] == codes, weights[entry][None], 0.0)]
    unnamed x12 -> x14, local copies, waits for them, and re-layouts: 0.71 us -> 1.43 us
where the time goes in v16:
time: 52.7 us; the launch traced here: 52.3 us
  starting transfers between devices  19.5 us (37%)
  blocking collectives  13.2 us (25%)
  Pallas kernels  6.8 us (13%)
  waiting for transfers between devices  4.52 us (9%)
  other arithmetic  4.12 us (8%)
  local copies, waits for them, and re-layouts  3.17 us (6%)
  between operations  0.84 us (2%)
    all_to_all x1, blocking collectives, shards(): lax.all_to_all(pieces.reshape(count, chunks // count, block_rows, span).t...  13.2 us
    ppermute x4, starting transfers between devices, from_behind(): lax.ppermute(value, axis, [(source, source + steps) for source in range(f...  12.1 us
    all_to_all x1, starting transfers between devices, gather_columns(): pieces = lax.all_to_all(copies, axis, 0, 0, tiled=True)  7.33 us
    pallas_call x1, Pallas kernels, march(): pl.pallas_call(march_kernel, out_shape=(jax.ShapeDtypeStruct((waves, fwd....  6.8 us
    ppermute x4, waiting for transfers between devices, from_behind(): lax.ppermute(value, axis, [(source, source + steps) for source in range(f...  4.52 us
    unnamed x14, local copies, waits for them, and re-layouts  1.43 us
    another operation x1, other arithmetic, shards(): sources = jnp.stack([source_fwd, source_adj])  1.35 us
    broadcast_in_dim x1, local copies, waits for them, and re-layouts, gather_columns(): copies = jnp.broadcast_to(value[None], (count,) + value.shape)  1.34 us
  transfers between devices with their start and end apart: 5, of which 1 were waited for; matrix products, arithmetic and copies ran while one was open for 8% of the time, Pallas kernels for 0%

profile of v16, /device:TPU:25, one launch (start us, length us, event | category | flops | bytes accessed | tf_op | source)
XLA Modules:
  0.0 52.3 jit_solution(9613898130175905240)
XLA Ops:
  0.6 0.0 copy-start.1
  0.6 1.3 %broadcast_in_dim.55 = f32[8,2,128]{2,1,0:T(2,128)} broadcast(f32[2,128]{1,0:T(2,128)} %param.6), dimensions={1,2} | broadcast | bytes 9216 | tf_op jit(solution)/shard_map/broadcast_in_dim | solution.py:35
  2.0 7.3 %all-to-all-start = ((f32[8,2,128]{2,1,0:T(2,128)}), f32[8,2,128]{2,1,0:T(2,128)S(1)}, u32[]{:S(2)}, u32[]{:S(2)}) async-start(f32[8,2,128]{2,1,0:T(2,128)} %broadcast_in_dim.55), calls=%async_computation | async-start | bytes 16384 | tf_op jit(solution)/shard_map/all_to_all | solution.py:36
  9.3 1.3 %pad_maximum_fusion = (f32[2,2,4,4096]{3,2,1,0:T(4,128)S(1)}, f32[2,2,4,4096]{3,2,1,0:T(4,128)S(1)}) fusion(f32[1,2,8,4096]{3,2,1,0:T(8,128)} %bitcast.35, f32[1,2,8,4096]{3,2,1,0:T(8,128)} %bitcast.34), kind=kLoop, calls=%fused_computation.27 | loop fusion | flops 131072 | bytes 1048576 | tf_op jit(solution)/shard_map/stack | solution.py:186
  10.7 0.0 copy-start.2
  10.7 3.0 %collective-permute-start.1 = (f32[2,2,4,4096]{3,2,1,0:T(4,128)S(1)}, f32[2,2,4,4096]{3,2,1,0:T(4,128)S(1)}, u32[]{:S(2)}, u32[]{:S(2)}) collective-permute-start(f32[2,2,4,4096]{3,2,1,0:T(4,128)S(1)} %get-tuple-element.16), channel_id=1, source_target_pairs={{1,0},{2,1},{3,2},{4,3},{5,4},{6,5},{7,6},{8,7},{9,8},{10,9},{11,1... | collective-permute-start | bytes 786440 | tf_op jit(solution)/shard_map/ppermute | solution.py:24
  13.7 4.8 %collective-permute-start = (f32[2,2,4,4096]{3,2,1,0:T(4,128)S(1)}, f32[2,2,4,4096]{3,2,1,0:T(4,128)S(1)}, u32[]{:S(2)}, u32[]{:S(2)}) collective-permute-start(f32[2,2,4,4096]{3,2,1,0:T(4,128)S(1)} %get-tuple-element.17), channel_id=1, source_target_pairs={{0,1},{1,2},{2,3},{3,4},{4,5},{5,6},{6,7},{7,8},{8,9},{9,10},{10,1... | collective-permute-start | bytes 786440 | tf_op jit(solution)/shard_map/ppermute | solution.py:24
  18.5 0.0 copy-done.1
  18.5 0.5 fusion.2
  19.1 0.0 copy-done.2
  19.2 0.5 select_add_fusion.matched_ref
  19.7 0.0 copy-start
  19.7 0.0 all-to-all-done
  19.7 0.1 pad_slice_fusion.4
  19.8 0.1 pad_slice_fusion.8
  19.9 0.1 stack.49
  20.0 0.2 fusion.11
  20.3 0.4 fusion.8
  20.7 1.9 %collective-permute-start.2 = (f32[3,4096]{1,0:T(4,128)S(1)}, f32[3,4096]{1,0:T(4,128)S(1)}, u32[]{:S(2)}, u32[]{:S(2)}) collective-permute-start(f32[3,4096]{1,0:T(4,128)S(1)} %concatenate.6), channel_id=1, source_target_pairs={{0,1},{1,2},{2,3},{3,4},{4,5},{5,6},{6,7},{7,8},{8,9},{9,10},{10,1... | collective-permute-start | bytes 147464 | tf_op jit(solution)/shard_map/ppermute | solution.py:24
  22.6 2.4 %collective-permute-start.3 = (f32[3,4096]{1,0:T(4,128)S(1)}, f32[3,4096]{1,0:T(4,128)S(1)}, u32[]{:S(2)}, u32[]{:S(2)}) collective-permute-start(f32[3,4096]{1,0:T(4,128)S(1)} %concatenate.7), channel_id=1, source_target_pairs={{1,0},{2,1},{3,2},{4,3},{5,4},{6,5},{7,6},{8,7},{9,8},{10,9},{11,1... | collective-permute-start | bytes 147464 | tf_op jit(solution)/shard_map/ppermute | solution.py:24
  25.1 0.8 %multiply_reduce_fusion.dens_ref = f32[8,4096]{1,0:T(8,128)} fusion(f32[10,8,4096]{2,1,0:T(8,128)S(1)} %select_add_fusion.matched_ref, f32[10,4096]{1,0:T(8,128)S(1)} %mul.32), kind=kLoop, calls=%fused_computation | loop fusion | flops 622592 | bytes 1605632 | tf_op jit(solution)/shard_map/reduce_sum | solution.py:218
  25.8 0.0 copy-done
  25.8 0.0 collective-permute-done.2.dens_above_ref
  25.8 4.5 %collective-permute-done.3.dens_below_ref = f32[3,4096]{1,0:T(4,128)S(1)} collective-permute-done((f32[3,4096]{1,0:T(4,128)S(1)}, f32[3,4096]{1,0:T(4,128)S(1)}, u32[]{:S(2)}, u32[]{:S(2)}) %collective-permute-start.3) | collective-permute-done | bytes 49184 | tf_op jit(solution)/shard_map/ppermute | solution.py:24
  30.3 0.0 collective-permute-done.1.src_below_ref
  30.4 0.0 collective-permute-done.src_above_ref
  30.4 0.6 %copy-done.6 = f32[3,4096]{1,0:T(4,128)} copy-done((f32[3,4096]{1,0:T(4,128)}, f32[3,4096]{1,0:T(4,128)S(1)}, u32[]{:S(2)}) %copy-start.6) | copy-done | bytes 49176
  31.0 0.1 copy-done.3
  31.1 0.7 %copy-done.4 = f32[2,2,4,4096]{3,2,1,0:T(4,128)} copy-done((f32[2,2,4,4096]{3,2,1,0:T(4,128)}, f32[2,2,4,4096]{3,2,1,0:T(4,128)S(1)}, u32[]{:S(2)}) %copy-start.4) | copy-done | bytes 262168
  31.8 6.8 %shard_map.77 = (f32[2,8,4096]{2,1,0:T(8,128)}, f32[8,2,128]{2,1,0:T(2,128)}) custom-call(f32[2]{0:T(128)} %drive_ref.1, f32[2,8,4096]{2,1,0:T(8,128)} %fwd_ref.1, f32[2,8,4096]{2,1,0:T(8,128)} %adj_ref.1, f32[2,2,4,4096]{3,2,1,0:T(4,128)} %copy-done.4, f32[2,2,4,4096]{3,2,1,0:T(4,128)} %copy-done.3, f32[8,4096]{1,0:T(8,128)} %multiply_reduce_fusion.dens_ref, ...), custom_call_target="tpu_custom_call" | custom-call | tf_op jit(solution)/shard_map/pallas_call | solution.py:166
  38.6 13.2 %all_to_all.10 = f32[8,2,128]{2,1,0:T(2,128)S(1)} all-to-all(f32[8,2,128]{2,1,0:T(2,128)} %get-tuple-element.5), channel_id=1, replica_groups=mesh['wl'=8,'tile'=16] {'wl'}, dimensions={0} | all-to-all | bytes 16384 | tf_op jit(solution)/shard_map/all_to_all | solution.py:223
  51.8 0.6 %reduce_sum.39 = f32[2,128]{1,0:T(2,128)} reduce(f32[8,2,128]{2,1,0:T(2,128)S(1)} %all_to_all.10, f32[]{:T(128)} %constant.63.clone.1), dimensions={0}, to_apply=%region_3.4 | reduce | flops 1792 | bytes 9220 | tf_op jit(solution)/shard_map/reduce_sum | solution.py:226
  (16 shorter events, 0.2 us)
Async XLA Ops:
  0.6 17.9 %copy-start.1 = (s32[4,8,4096]{2,1,0:T(8,128)S(1)}, s32[4,8,4096]{2,1,0:T(8,128)}, u32[]{:S(2)}) copy-start(s32[4,8,4096]{2,1,0:T(8,128)} %param.7) | copy-start | bytes 1572868
  2.0 17.7 %all-to-all-start = ((f32[8,2,128]{2,1,0:T(2,128)}), f32[8,2,128]{2,1,0:T(2,128)S(1)}, u32[]{:S(2)}, u32[]{:S(2)}) async-start(f32[8,2,128]{2,1,0:T(2,128)} %broadcast_in_dim.55), calls=%async_computation | async-start | bytes 16384 | tf_op jit(solution)/shard_map/all_to_all | solution.py:36
  10.7 8.4 %copy-start.2 = (bf16[4,8,4096]{2,1,0:T(8,128)(2,1)S(1)}, bf16[4,8,4096]{2,1,0:T(8,128)(2,1)}, u32[]{:S(2)}) copy-start(bf16[4,8,4096]{2,1,0:T(8,128)(2,1)} %param.8) | copy-start | bytes 786436
  10.7 19.7 %collective-permute-start.1 = (f32[2,2,4,4096]{3,2,1,0:T(4,128)S(1)}, f32[2,2,4,4096]{3,2,1,0:T(4,128)S(1)}, u32[]{:S(2)}, u32[]{:S(2)}) collective-permute-start(f32[2,2,4,4096]{3,2,1,0:T(4,128)S(1)} %get-tuple-element.16), channel_id=1, source_target_pairs={{1,0},{2,1},{3,2},{4,3},{5,4},{6,5},{7,6},{8,7},{9,8},{10,9},{11,1... | collective-permute-start | bytes 786440 | tf_op jit(solution)/shard_map/ppermute | solution.py:24
  13.7 16.7 %collective-permute-start = (f32[2,2,4,4096]{3,2,1,0:T(4,128)S(1)}, f32[2,2,4,4096]{3,2,1,0:T(4,128)S(1)}, u32[]{:S(2)}, u32[]{:S(2)}) collective-permute-start(f32[2,2,4,4096]{3,2,1,0:T(4,128)S(1)} %get-tuple-element.17), channel_id=1, source_target_pairs={{0,1},{1,2},{2,3},{3,4},{4,5},{5,6},{6,7},{7,8},{8,9},{9,10},{10,1... | collective-permute-start | bytes 786440 | tf_op jit(solution)/shard_map/ppermute | solution.py:24
  19.7 6.2 %copy-start = (f32[10,8,4096]{2,1,0:T(8,128)}, f32[10,8,4096]{2,1,0:T(8,128)S(1)}, u32[]{:S(2)}) copy-start(f32[10,8,4096]{2,1,0:T(8,128)S(1)} %select_add_fusion.matched_ref) | copy-start | bytes 3932164
  20.7 5.1 %collective-permute-start.2 = (f32[3,4096]{1,0:T(4,128)S(1)}, f32[3,4096]{1,0:T(4,128)S(1)}, u32[]{:S(2)}, u32[]{:S(2)}) collective-permute-start(f32[3,4096]{1,0:T(4,128)S(1)} %concatenate.6), channel_id=1, source_target_pairs={{0,1},{1,2},{2,3},{3,4},{4,5},{5,6},{6,7},{7,8},{8,9},{9,10},{10,1... | collective-permute-start | bytes 147464 | tf_op jit(solution)/shard_map/ppermute | solution.py:24
  22.6 7.7 %collective-permute-start.3 = (f32[3,4096]{1,0:T(4,128)S(1)}, f32[3,4096]{1,0:T(4,128)S(1)}, u32[]{:S(2)}, u32[]{:S(2)}) collective-permute-start(f32[3,4096]{1,0:T(4,128)S(1)} %concatenate.7), channel_id=1, source_target_pairs={{1,0},{2,1},{3,2},{4,3},{5,4},{6,5},{7,6},{8,7},{9,8},{10,9},{11,1... | collective-permute-start | bytes 147464 | tf_op jit(solution)/shard_map/ppermute | solution.py:24
  25.8 4.5 %copy-start.5 = (f32[3,4096]{1,0:T(4,128)}, f32[3,4096]{1,0:T(4,128)S(1)}, u32[]{:S(2)}) copy-start(f32[3,4096]{1,0:T(4,128)S(1)} %collective-permute-done.2.dens_above_ref) | copy-start | bytes 147460
  30.3 0.6 %copy-start.6 = (f32[3,4096]{1,0:T(4,128)}, f32[3,4096]{1,0:T(4,128)S(1)}, u32[]{:S(2)}) copy-start(f32[3,4096]{1,0:T(4,128)S(1)} %collective-permute-done.3.dens_below_ref) | copy-start | bytes 147460
  30.3 0.7 %copy-start.3 = (f32[2,2,4,4096]{3,2,1,0:T(4,128)}, f32[2,2,4,4096]{3,2,1,0:T(4,128)S(1)}, u32[]{:S(2)}) copy-start(f32[2,2,4,4096]{3,2,1,0:T(4,128)S(1)} %collective-permute-done.1.src_below_ref) | copy-start | bytes 786436
  31.1 0.7 %copy-start.4 = (f32[2,2,4,4096]{3,2,1,0:T(4,128)}, f32[2,2,4,4096]{3,2,1,0:T(4,128)S(1)}, u32[]{:S(2)}) copy-start(f32[2,2,4,4096]{3,2,1,0:T(4,128)S(1)} %collective-permute-done.src_above_ref) | copy-start | bytes 786436

commit v17 on v15

--- a/solution.py
+++ b/solution.py
@@ -76,9 +76,12 @@
     block_rows = pieces_ref.shape[1]
     for wave in range(waves):
         for run, own_ref in enumerate((fwd_ref, adj_ref)):
-            source_ref[run, wave, 0:HALO] = src_above_ref[run, wave]
+            reach_src = src_above_ref.shape[2]
+            source_ref[run, wave, 0 : HALO - reach_src] = jnp.zeros((HALO - reach_src, cols), jnp.float32)
+            source_ref[run, wave, HALO - reach_src : HALO] = src_above_ref[run, wave]
             source_ref[run, wave, HALO : HALO + own] = own_ref[wave]
-            source_ref[run, wave, HALO + own : rows] = src_below_ref[run, wave]
+            source_ref[run, wave, HALO + own : HALO + own + reach_src] = src_below_ref[run, wave]
+            source_ref[run, wave, HALO + own + reach_src : rows] = jnp.zeros((HALO - reach_src, cols), jnp.float32)
     density_ref[...] = jnp.zeros((rows, cols), jnp.float32)
     density_ref[HALO - reach : HALO] = dens_above_ref[0:reach]
     density_ref[HALO : HALO + own] = dens_ref[...]
@@ -184,8 +187,8 @@
 
 def shards(density, foot_index, foot_weight, source_fwd, source_adj, omega):
     sources = jnp.stack([source_fwd, source_adj])
-    src_above = from_behind(sources[:, :, -HALO:], "tile", 1)
-    src_below = from_behind(sources[:, :, :HALO], "tile", -1)
+    src_above = from_behind(sources[:, :, -(ITERS - 1):], "tile", 1)
+    src_below = from_behind(sources[:, :, : ITERS - 1], "tile", -1)
     strip = gather_columns(density, "wl")
     block_rows, block_cols = strip.shape
     cells_x, cells_y = foot_index.shape[1:]

time: 52.7 us -> 52.7 us (level)
  no operation moved by 1% of the time
where the time goes in v17:
time: 52.7 us; the launch traced here: 52.3 us
  starting transfers between devices  19.5 us (37%)
  blocking collectives  13.2 us (25%)
  Pallas kernels  6.82 us (13%)
  waiting for transfers between devices  5.27 us (10%)
  other arithmetic  4.08 us (8%)
  local copies, waits for them, and re-layouts  2.46 us (5%)
  between operations  0.84 us (2%)
    all_to_all x1, blocking collectives, shards(): lax.all_to_all(pieces.reshape(count, chunks // count, block_rows, span).t...  13.2 us
    ppermute x4, starting transfers between devices, from_behind(): lax.ppermute(value, axis, [(source, source + steps) for source in range(f...  12.1 us
    all_to_all x1, starting transfers between devices, gather_columns(): pieces = lax.all_to_all(copies, axis, 0, 0, tiled=True)  7.33 us
    pallas_call x1, Pallas kernels, march(): pl.pallas_call(march_kernel, out_shape=(jax.ShapeDtypeStruct((waves, fwd....  6.82 us
    ppermute x4, waiting for transfers between devices, from_behind(): lax.ppermute(value, axis, [(source, source + steps) for source in range(f...  5.27 us
    another operation x1, other arithmetic, shards(): sources = jnp.stack([source_fwd, source_adj])  1.35 us
    broadcast_in_dim x1, local copies, waits for them, and re-layouts, gather_columns(): copies = jnp.broadcast_to(value[None], (count,) + value.shape)  1.34 us
    add x1, other arithmetic, shards(): matched + jnp.where(key[entry][None] == codes, weights[entry][None], 0.0)  1.19 us
  transfers between devices with their start and end apart: 5, of which 1 were waited for; matrix products, arithmetic and copies ran while one was open for 8% of the time, Pallas kernels for 0%

profile of v17, /device:TPU:25, one launch (start us, length us, event | category | flops | bytes accessed | tf_op | source)
XLA Modules:
  0.0 52.3 jit_solution(4665461445901159360)
XLA Ops:
  0.6 0.0 copy-start.1
  0.6 1.3 %broadcast_in_dim.55 = f32[8,2,128]{2,1,0:T(2,128)} broadcast(f32[2,128]{1,0:T(2,128)} %param.6), dimensions={1,2} | broadcast | bytes 9216 | tf_op jit(solution)/shard_map/broadcast_in_dim | solution.py:35
  2.0 7.3 %all-to-all-start = ((f32[8,2,128]{2,1,0:T(2,128)}), f32[8,2,128]{2,1,0:T(2,128)S(1)}, u32[]{:S(2)}, u32[]{:S(2)}) async-start(f32[8,2,128]{2,1,0:T(2,128)} %broadcast_in_dim.55), calls=%async_computation | async-start | bytes 16384 | tf_op jit(solution)/shard_map/all_to_all | solution.py:36
  9.3 1.3 %pad_maximum_fusion = (f32[2,2,3,4096]{3,2,1,0:T(4,128)S(1)}, f32[2,2,3,4096]{3,2,1,0:T(4,128)S(1)}) fusion(f32[1,2,8,4096]{3,2,1,0:T(8,128)} %bitcast.35, f32[1,2,8,4096]{3,2,1,0:T(8,128)} %bitcast.34), kind=kLoop, calls=%fused_computation.27 | loop fusion | flops 98304 | bytes 917504 | tf_op jit(solution)/shard_map/stack | solution.py:189
  10.7 0.0 copy-start.2
  10.7 3.0 %collective-permute-start.1 = (f32[2,2,3,4096]{3,2,1,0:T(4,128)S(1)}, f32[2,2,3,4096]{3,2,1,0:T(4,128)S(1)}, u32[]{:S(2)}, u32[]{:S(2)}) collective-permute-start(f32[2,2,3,4096]{3,2,1,0:T(4,128)S(1)} %get-tuple-element.18), channel_id=1, source_target_pairs={{1,0},{2,1},{3,2},{4,3},{5,4},{6,5},{7,6},{8,7},{9,8},{10,9},{11,1... | collective-permute-start | bytes 589832 | tf_op jit(solution)/shard_map/ppermute | solution.py:24
  13.7 4.8 %collective-permute-start = (f32[2,2,3,4096]{3,2,1,0:T(4,128)S(1)}, f32[2,2,3,4096]{3,2,1,0:T(4,128)}, u32[]{:S(2)}, u32[]{:S(2)}) collective-permute-start(f32[2,2,3,4096]{3,2,1,0:T(4,128)S(1)} %get-tuple-element.19), channel_id=1, source_target_pairs={{0,1},{1,2},{2,3},{3,4},{4,5},{5,6},{6,7},{7,8},{8,9},{9,10},{10,1... | collective-permute-start | bytes 589832 | tf_op jit(solution)/shard_map/ppermute | solution.py:24
  18.5 0.0 copy-done.1
  18.5 0.5 fusion.2
  19.1 0.0 copy-done.2
  19.2 0.0 all-to-all-done
  19.2 0.1 pad_slice_fusion.4
  19.3 0.1 pad_slice_fusion.8
  19.4 0.1 stack.49
  19.5 0.2 fusion.11
  19.8 1.2 %select_add_fusion = (f32[10,8,4096]{2,1,0:T(8,128)S(1)}, f32[8,4096]{1,0:T(8,128)}) fusion(f32[8,4096]{1,0:T(8,128)S(1)} %get-tuple-element.15, s32[8,4096]{1,0:T(8,128)S(1)} %get-tuple-element.11, f32[8,4096]{1,0:T(8,128)S(1)} %get-tuple-element.16, s32[8,4096]{1,0:T(8,128)S(1)} %get-tuple-element.12, f32[8,4096]{1,0:T(8,128)S(1)} %get-tuple-element.17, ...), kind=kLoop, calls=%fused_computation.1 | loop fusion | flops 4227072 | bytes 2654208 | tf_op jit(solution)/shard_map/add | solution.py:203
  21.0 0.0 copy-start
  21.0 0.4 fusion.8
  21.4 1.9 %collective-permute-start.2 = (f32[3,4096]{1,0:T(4,128)S(1)}, f32[3,4096]{1,0:T(4,128)S(1)}, u32[]{:S(2)}, u32[]{:S(2)}) collective-permute-start(f32[3,4096]{1,0:T(4,128)S(1)} %concatenate.6), channel_id=1, source_target_pairs={{0,1},{1,2},{2,3},{3,4},{4,5},{5,6},{6,7},{7,8},{8,9},{9,10},{10,1... | collective-permute-start | bytes 147464 | tf_op jit(solution)/shard_map/ppermute | solution.py:24
  23.4 2.4 %collective-permute-start.3 = (f32[3,4096]{1,0:T(4,128)S(1)}, f32[3,4096]{1,0:T(4,128)S(1)}, u32[]{:S(2)}, u32[]{:S(2)}) collective-permute-start(f32[3,4096]{1,0:T(4,128)S(1)} %concatenate.7), channel_id=1, source_target_pairs={{1,0},{2,1},{3,2},{4,3},{5,4},{6,5},{7,6},{8,7},{9,8},{10,9},{11,1... | collective-permute-start | bytes 147464 | tf_op jit(solution)/shard_map/ppermute | solution.py:24
  25.8 0.0 collective-permute-done.2.dens_above_ref
  25.8 0.0 copy-start.4
  25.8 5.3 %collective-permute-done.3.dens_below_ref = f32[3,4096]{1,0:T(4,128)S(1)} collective-permute-done((f32[3,4096]{1,0:T(4,128)S(1)}, f32[3,4096]{1,0:T(4,128)S(1)}, u32[]{:S(2)}, u32[]{:S(2)}) %collective-permute-start.3) | collective-permute-done | bytes 49184 | tf_op jit(solution)/shard_map/ppermute | solution.py:24
  31.1 0.0 collective-permute-done.1.src_below_ref
  31.1 0.0 collective-permute-done.src_above_ref
  31.1 0.0 copy-done
  31.1 0.0 copy-done.4
  31.1 0.6 %copy-done.5 = f32[3,4096]{1,0:T(4,128)} copy-done((f32[3,4096]{1,0:T(4,128)}, f32[3,4096]{1,0:T(4,128)S(1)}, u32[]{:S(2)}) %copy-start.5) | copy-done | bytes 49176
  31.7 0.1 copy-done.3
  31.8 6.8 %shard_map.77 = (f32[2,8,4096]{2,1,0:T(8,128)}, f32[8,2,128]{2,1,0:T(2,128)}) custom-call(f32[2]{0:T(128)} %drive_ref.1, f32[2,8,4096]{2,1,0:T(8,128)} %fwd_ref.1, f32[2,8,4096]{2,1,0:T(8,128)} %adj_ref.1, f32[2,2,3,4096]{3,2,1,0:T(4,128)} %collective-permute-done.src_above_ref, f32[2,2,3,4096]{3,2,1,0:T(4,128)} %copy-done.3, ...), custom_call_target="tpu_custom_call" | custom-call | tf_op jit(solution)/shard_map/pallas_call | solution.py:169
  38.6 13.2 %all_to_all.10 = f32[8,2,128]{2,1,0:T(2,128)S(1)} all-to-all(f32[8,2,128]{2,1,0:T(2,128)} %get-tuple-element.5), channel_id=1, replica_groups=mesh['wl'=8,'tile'=16] {'wl'}, dimensions={0} | all-to-all | bytes 16384 | tf_op jit(solution)/shard_map/all_to_all | solution.py:225
  51.8 0.6 %reduce_sum.39 = f32[2,128]{1,0:T(2,128)} reduce(f32[8,2,128]{2,1,0:T(2,128)S(1)} %all_to_all.10, f32[]{:T(128)} %constant.63.clone.1), dimensions={0}, to_apply=%region_3.4 | reduce | flops 1792 | bytes 9220 | tf_op jit(solution)/shard_map/reduce_sum | solution.py:228
  (13 shorter events, 0.2 us)
Async XLA Ops:
  0.6 17.9 %copy-start.1 = (s32[4,8,4096]{2,1,0:T(8,128)S(1)}, s32[4,8,4096]{2,1,0:T(8,128)}, u32[]{:S(2)}) copy-start(s32[4,8,4096]{2,1,0:T(8,128)} %param.7) | copy-start | bytes 1572868
  2.0 17.2 %all-to-all-start = ((f32[8,2,128]{2,1,0:T(2,128)}), f32[8,2,128]{2,1,0:T(2,128)S(1)}, u32[]{:S(2)}, u32[]{:S(2)}) async-start(f32[8,2,128]{2,1,0:T(2,128)} %broadcast_in_dim.55), calls=%async_computation | async-start | bytes 16384 | tf_op jit(solution)/shard_map/all_to_all | solution.py:36
  10.7 8.4 %copy-start.2 = (bf16[4,8,4096]{2,1,0:T(8,128)(2,1)S(1)}, bf16[4,8,4096]{2,1,0:T(8,128)(2,1)}, u32[]{:S(2)}) copy-start(bf16[4,8,4096]{2,1,0:T(8,128)(2,1)} %param.8) | copy-start | bytes 786436
  10.7 20.4 %collective-permute-start.1 = (f32[2,2,3,4096]{3,2,1,0:T(4,128)S(1)}, f32[2,2,3,4096]{3,2,1,0:T(4,128)S(1)}, u32[]{:S(2)}, u32[]{:S(2)}) collective-permute-start(f32[2,2,3,4096]{3,2,1,0:T(4,128)S(1)} %get-tuple-element.18), channel_id=1, source_target_pairs={{1,0},{2,1},{3,2},{4,3},{5,4},{6,5},{7,6},{8,7},{9,8},{10,9},{11,1... | collective-permute-start | bytes 589832 | tf_op jit(solution)/shard_map/ppermute | solution.py:24
  13.7 17.4 %collective-permute-start = (f32[2,2,3,4096]{3,2,1,0:T(4,128)S(1)}, f32[2,2,3,4096]{3,2,1,0:T(4,128)}, u32[]{:S(2)}, u32[]{:S(2)}) collective-permute-start(f32[2,2,3,4096]{3,2,1,0:T(4,128)S(1)} %get-tuple-element.19), channel_id=1, source_target_pairs={{0,1},{1,2},{2,3},{3,4},{4,5},{5,6},{6,7},{7,8},{8,9},{9,10},{10,1... | collective-permute-start | bytes 589832 | tf_op jit(solution)/shard_map/ppermute | solution.py:24
  21.0 10.1 %copy-start = (f32[10,8,4096]{2,1,0:T(8,128)}, f32[10,8,4096]{2,1,0:T(8,128)S(1)}, u32[]{:S(2)}) copy-start(f32[10,8,4096]{2,1,0:T(8,128)S(1)} %get-tuple-element.8.matched_ref) | copy-start | bytes 3932164
  21.4 4.3 %collective-permute-start.2 = (f32[3,4096]{1,0:T(4,128)S(1)}, f32[3,4096]{1,0:T(4,128)S(1)}, u32[]{:S(2)}, u32[]{:S(2)}) collective-permute-start(f32[3,4096]{1,0:T(4,128)S(1)} %concatenate.6), channel_id=1, source_target_pairs={{0,1},{1,2},{2,3},{3,4},{4,5},{5,6},{6,7},{7,8},{8,9},{9,10},{10,1... | collective-permute-start | bytes 147464 | tf_op jit(solution)/shard_map/ppermute | solution.py:24
  23.4 7.7 %collective-permute-start.3 = (f32[3,4096]{1,0:T(4,128)S(1)}, f32[3,4096]{1,0:T(4,128)S(1)}, u32[]{:S(2)}, u32[]{:S(2)}) collective-permute-start(f32[3,4096]{1,0:T(4,128)S(1)} %concatenate.7), channel_id=1, source_target_pairs={{1,0},{2,1},{3,2},{4,3},{5,4},{6,5},{7,6},{8,7},{9,8},{10,9},{11,1... | collective-permute-start | bytes 147464 | tf_op jit(solution)/shard_map/ppermute | solution.py:24
  25.8 5.3 %copy-start.4 = (f32[3,4096]{1,0:T(4,128)}, f32[3,4096]{1,0:T(4,128)S(1)}, u32[]{:S(2)}) copy-start(f32[3,4096]{1,0:T(4,128)S(1)} %collective-permute-done.2.dens_above_ref) | copy-start | bytes 147460
  31.1 0.6 %copy-start.5 = (f32[3,4096]{1,0:T(4,128)}, f32[3,4096]{1,0:T(4,128)S(1)}, u32[]{:S(2)}) copy-start(f32[3,4096]{1,0:T(4,128)S(1)} %collective-permute-done.3.dens_below_ref) | copy-start | bytes 147460
  31.1 0.7 %copy-start.3 = (f32[2,2,3,4096]{3,2,1,0:T(4,128)}, f32[2,2,3,4096]{3,2,1,0:T(4,128)S(1)}, u32[]{:S(2)}) copy-start(f32[2,2,3,4096]{3,2,1,0:T(4,128)S(1)} %collective-permute-done.1.src_below_ref) | copy-start | bytes 589828

commit v18 on v15

--- a/solution.py
+++ b/solution.py
@@ -110,7 +110,7 @@
                 if field_e is None:
                     field_e = drive_term
                 else:
-                    e_up = jnp.where(row_id < rows - 1, pltpu.roll(field_e, rows - 1, 0), 0.0)
+                    e_up = pltpu.roll(field_e, rows - 1, 0)
                     e_right = jnp.where(col_id < cols - 1, pltpu.roll(field_e, cols - 1, 1), 0.0)
                     if field_hx is None:
                         field_hx = -time_step * (e_right - field_e)
@@ -120,7 +120,7 @@
                         field_hx = field_hx - time_step * (e_right - field_e)
                         field_hy = field_hy + hy_step * (e_up - field_e)
                         current = drude_decay * current + half_density * field_e
-                    hy_down = jnp.where(row_id > 0, pltpu.roll(field_hy, 1, 0), 0.0)
+                    hy_down = pltpu.roll(field_hy, 1, 0)
                     hx_left = jnp.where(col_id > 0, pltpu.roll(field_hx, 1, 1), 0.0)
                     field_e = (
                         field_e

time: 52.7 us -> 52.6 us (level)
  no operation moved by 1% of the time
where the time goes in v18:
time: 52.6 us; the launch traced here: 52.2 us
  starting transfers between devices  19.5 us (37%)
  blocking collectives  13.2 us (25%)
  Pallas kernels  6.71 us (13%)
  waiting for transfers between devices  5.27 us (10%)
  other arithmetic  4.08 us (8%)
  local copies, waits for them, and re-layouts  2.46 us (5%)
  between operations  0.84 us (2%)
    all_to_all x1, blocking collectives, shards(): lax.all_to_all(pieces.reshape(count, chunks // count, block_rows, span).t...  13.2 us
    ppermute x4, starting transfers between devices, from_behind(): lax.ppermute(value, axis, [(source, source + steps) for source in range(f...  12.1 us
    all_to_all x1, starting transfers between devices, gather_columns(): pieces = lax.all_to_all(copies, axis, 0, 0, tiled=True)  7.33 us
    pallas_call x1, Pallas kernels, march(): pl.pallas_call(march_kernel, out_shape=(jax.ShapeDtypeStruct((waves, fwd....  6.71 us
    ppermute x4, waiting for transfers between devices, from_behind(): lax.ppermute(value, axis, [(source, source + steps) for source in range(f...  5.27 us
    another operation x1, other arithmetic, shards(): sources = jnp.stack([source_fwd, source_adj])  1.35 us
    broadcast_in_dim x1, local copies, waits for them, and re-layouts, gather_columns(): copies = jnp.broadcast_to(value[None], (count,) + value.shape)  1.34 us
    add x1, other arithmetic, shards(): matched + jnp.where(key[entry][None] == codes, weights[entry][None], 0.0)  1.19 us
  transfers between devices with their start and end apart: 5, of which 1 were waited for; matrix products, arithmetic and copies ran while one was open for 8% of the time, Pallas kernels for 0%

profile of v18, /device:TPU:25, one launch (start us, length us, event | category | flops | bytes accessed | tf_op | source)
XLA Modules:
  0.0 52.2 jit_solution(5979686529752666301)
XLA Ops:
  0.6 0.0 copy-start.1
  0.6 1.3 %broadcast_in_dim.55 = f32[8,2,128]{2,1,0:T(2,128)} broadcast(f32[2,128]{1,0:T(2,128)} %param.6), dimensions={1,2} | broadcast | bytes 9216 | tf_op jit(solution)/shard_map/broadcast_in_dim | solution.py:35
  2.0 7.3 %all-to-all-start = ((f32[8,2,128]{2,1,0:T(2,128)}), f32[8,2,128]{2,1,0:T(2,128)S(1)}, u32[]{:S(2)}, u32[]{:S(2)}) async-start(f32[8,2,128]{2,1,0:T(2,128)} %broadcast_in_dim.55), calls=%async_computation | async-start | bytes 16384 | tf_op jit(solution)/shard_map/all_to_all | solution.py:36
  9.3 1.3 %pad_maximum_fusion = (f32[2,2,4,4096]{3,2,1,0:T(4,128)S(1)}, f32[2,2,4,4096]{3,2,1,0:T(4,128)S(1)}) fusion(f32[1,2,8,4096]{3,2,1,0:T(8,128)} %bitcast.35, f32[1,2,8,4096]{3,2,1,0:T(8,128)} %bitcast.34), kind=kLoop, calls=%fused_computation.27 | loop fusion | flops 131072 | bytes 1048576 | tf_op jit(solution)/shard_map/stack | solution.py:186
  10.7 0.0 copy-start.2
  10.7 3.0 %collective-permute-start.1 = (f32[2,2,4,4096]{3,2,1,0:T(4,128)S(1)}, f32[2,2,4,4096]{3,2,1,0:T(4,128)S(1)}, u32[]{:S(2)}, u32[]{:S(2)}) collective-permute-start(f32[2,2,4,4096]{3,2,1,0:T(4,128)S(1)} %get-tuple-element.18), channel_id=1, source_target_pairs={{1,0},{2,1},{3,2},{4,3},{5,4},{6,5},{7,6},{8,7},{9,8},{10,9},{11,1... | collective-permute-start | bytes 786440 | tf_op jit(solution)/shard_map/ppermute | solution.py:24
  13.7 4.8 %collective-permute-start = (f32[2,2,4,4096]{3,2,1,0:T(4,128)S(1)}, f32[2,2,4,4096]{3,2,1,0:T(4,128)}, u32[]{:S(2)}, u32[]{:S(2)}) collective-permute-start(f32[2,2,4,4096]{3,2,1,0:T(4,128)S(1)} %get-tuple-element.19), channel_id=1, source_target_pairs={{0,1},{1,2},{2,3},{3,4},{4,5},{5,6},{6,7},{7,8},{8,9},{9,10},{10,1... | collective-permute-start | bytes 786440 | tf_op jit(solution)/shard_map/ppermute | solution.py:24
  18.5 0.0 copy-done.1
  18.5 0.5 fusion.2
  19.1 0.0 copy-done.2
  19.2 0.0 all-to-all-done
  19.2 0.1 pad_slice_fusion.4
  19.3 0.1 pad_slice_fusion.8
  19.4 0.1 stack.49
  19.5 0.2 fusion.11
  19.8 1.2 %select_add_fusion = (f32[10,8,4096]{2,1,0:T(8,128)S(1)}, f32[8,4096]{1,0:T(8,128)}) fusion(f32[8,4096]{1,0:T(8,128)S(1)} %get-tuple-element.15, s32[8,4096]{1,0:T(8,128)S(1)} %get-tuple-element.11, f32[8,4096]{1,0:T(8,128)S(1)} %get-tuple-element.16, s32[8,4096]{1,0:T(8,128)S(1)} %get-tuple-element.12, f32[8,4096]{1,0:T(8,128)S(1)} %get-tuple-element.17, ...), kind=kLoop, calls=%fused_computation.1 | loop fusion | flops 4227072 | bytes 2654208 | tf_op jit(solution)/shard_map/add | solution.py:200
  21.0 0.0 copy-start
  21.0 0.4 fusion.8
  21.4 1.9 %collective-permute-start.2 = (f32[3,4096]{1,0:T(4,128)S(1)}, f32[3,4096]{1,0:T(4,128)S(1)}, u32[]{:S(2)}, u32[]{:S(2)}) collective-permute-start(f32[3,4096]{1,0:T(4,128)S(1)} %concatenate.6), channel_id=1, source_target_pairs={{0,1},{1,2},{2,3},{3,4},{4,5},{5,6},{6,7},{7,8},{8,9},{9,10},{10,1... | collective-permute-start | bytes 147464 | tf_op jit(solution)/shard_map/ppermute | solution.py:24
  23.4 2.4 %collective-permute-start.3 = (f32[3,4096]{1,0:T(4,128)S(1)}, f32[3,4096]{1,0:T(4,128)S(1)}, u32[]{:S(2)}, u32[]{:S(2)}) collective-permute-start(f32[3,4096]{1,0:T(4,128)S(1)} %concatenate.7), channel_id=1, source_target_pairs={{1,0},{2,1},{3,2},{4,3},{5,4},{6,5},{7,6},{8,7},{9,8},{10,9},{11,1... | collective-permute-start | bytes 147464 | tf_op jit(solution)/shard_map/ppermute | solution.py:24
  25.8 0.0 collective-permute-done.2.dens_above_ref
  25.8 0.0 copy-start.4
  25.8 5.3 %collective-permute-done.3.dens_below_ref = f32[3,4096]{1,0:T(4,128)S(1)} collective-permute-done((f32[3,4096]{1,0:T(4,128)S(1)}, f32[3,4096]{1,0:T(4,128)S(1)}, u32[]{:S(2)}, u32[]{:S(2)}) %collective-permute-start.3) | collective-permute-done | bytes 49184 | tf_op jit(solution)/shard_map/ppermute | solution.py:24
  31.1 0.0 collective-permute-done.1.src_below_ref
  31.1 0.0 collective-permute-done.src_above_ref
  31.1 0.0 copy-done
  31.1 0.0 copy-done.4
  31.1 0.6 %copy-done.5 = f32[3,4096]{1,0:T(4,128)} copy-done((f32[3,4096]{1,0:T(4,128)}, f32[3,4096]{1,0:T(4,128)S(1)}, u32[]{:S(2)}) %copy-start.5) | copy-done | bytes 49176
  31.7 0.1 copy-done.3
  31.8 6.7 %shard_map.77 = (f32[2,8,4096]{2,1,0:T(8,128)}, f32[8,2,128]{2,1,0:T(2,128)}) custom-call(f32[2]{0:T(128)} %drive_ref.1, f32[2,8,4096]{2,1,0:T(8,128)} %fwd_ref.1, f32[2,8,4096]{2,1,0:T(8,128)} %adj_ref.1, f32[2,2,4,4096]{3,2,1,0:T(4,128)} %collective-permute-done.src_above_ref, f32[2,2,4,4096]{3,2,1,0:T(4,128)} %copy-done.3, ...), custom_call_target="tpu_custom_call" | custom-call | tf_op jit(solution)/shard_map/pallas_call | solution.py:166
  38.5 13.2 %all_to_all.10 = f32[8,2,128]{2,1,0:T(2,128)S(1)} all-to-all(f32[8,2,128]{2,1,0:T(2,128)} %get-tuple-element.5), channel_id=1, replica_groups=mesh['wl'=8,'tile'=16] {'wl'}, dimensions={0} | all-to-all | bytes 16384 | tf_op jit(solution)/shard_map/all_to_all | solution.py:222
  51.7 0.6 %reduce_sum.39 = f32[2,128]{1,0:T(2,128)} reduce(f32[8,2,128]{2,1,0:T(2,128)S(1)} %all_to_all.10, f32[]{:T(128)} %constant.63.clone.1), dimensions={0}, to_apply=%region_3.4 | reduce | flops 1792 | bytes 9220 | tf_op jit(solution)/shard_map/reduce_sum | solution.py:225
  (13 shorter events, 0.2 us)
Async XLA Ops:
  0.6 17.9 %copy-start.1 = (s32[4,8,4096]{2,1,0:T(8,128)S(1)}, s32[4,8,4096]{2,1,0:T(8,128)}, u32[]{:S(2)}) copy-start(s32[4,8,4096]{2,1,0:T(8,128)} %param.7) | copy-start | bytes 1572868
  2.0 17.2 %all-to-all-start = ((f32[8,2,128]{2,1,0:T(2,128)}), f32[8,2,128]{2,1,0:T(2,128)S(1)}, u32[]{:S(2)}, u32[]{:S(2)}) async-start(f32[8,2,128]{2,1,0:T(2,128)} %broadcast_in_dim.55), calls=%async_computation | async-start | bytes 16384 | tf_op jit(solution)/shard_map/all_to_all | solution.py:36
  10.7 8.4 %copy-start.2 = (bf16[4,8,4096]{2,1,0:T(8,128)(2,1)S(1)}, bf16[4,8,4096]{2,1,0:T(8,128)(2,1)}, u32[]{:S(2)}) copy-start(bf16[4,8,4096]{2,1,0:T(8,128)(2,1)} %param.8) | copy-start | bytes 786436
  10.7 20.4 %collective-permute-start.1 = (f32[2,2,4,4096]{3,2,1,0:T(4,128)S(1)}, f32[2,2,4,4096]{3,2,1,0:T(4,128)S(1)}, u32[]{:S(2)}, u32[]{:S(2)}) collective-permute-start(f32[2,2,4,4096]{3,2,1,0:T(4,128)S(1)} %get-tuple-element.18), channel_id=1, source_target_pairs={{1,0},{2,1},{3,2},{4,3},{5,4},{6,5},{7,6},{8,7},{9,8},{10,9},{11,1... | collective-permute-start | bytes 786440 | tf_op jit(solution)/shard_map/ppermute | solution.py:24
  13.7 17.4 %collective-permute-start = (f32[2,2,4,4096]{3,2,1,0:T(4,128)S(1)}, f32[2,2,4,4096]{3,2,1,0:T(4,128)}, u32[]{:S(2)}, u32[]{:S(2)}) collective-permute-start(f32[2,2,4,4096]{3,2,1,0:T(4,128)S(1)} %get-tuple-element.19), channel_id=1, source_target_pairs={{0,1},{1,2},{2,3},{3,4},{4,5},{5,6},{6,7},{7,8},{8,9},{9,10},{10,1... | collective-permute-start | bytes 786440 | tf_op jit(solution)/shard_map/ppermute | solution.py:24
  21.0 10.1 %copy-start = (f32[10,8,4096]{2,1,0:T(8,128)}, f32[10,8,4096]{2,1,0:T(8,128)S(1)}, u32[]{:S(2)}) copy-start(f32[10,8,4096]{2,1,0:T(8,128)S(1)} %get-tuple-element.8.matched_ref) | copy-start | bytes 3932164
  21.4 4.3 %collective-permute-start.2 = (f32[3,4096]{1,0:T(4,128)S(1)}, f32[3,4096]{1,0:T(4,128)S(1)}, u32[]{:S(2)}, u32[]{:S(2)}) collective-permute-start(f32[3,4096]{1,0:T(4,128)S(1)} %concatenate.6), channel_id=1, source_target_pairs={{0,1},{1,2},{2,3},{3,4},{4,5},{5,6},{6,7},{7,8},{8,9},{9,10},{10,1... | collective-permute-start | bytes 147464 | tf_op jit(solution)/shard_map/ppermute | solution.py:24
  23.4 7.7 %collective-permute-start.3 = (f32[3,4096]{1,0:T(4,128)S(1)}, f32[3,4096]{1,0:T(4,128)S(1)}, u32[]{:S(2)}, u32[]{:S(2)}) collective-permute-start(f32[3,4096]{1,0:T(4,128)S(1)} %concatenate.7), channel_id=1, source_target_pairs={{1,0},{2,1},{3,2},{4,3},{5,4},{6,5},{7,6},{8,7},{9,8},{10,9},{11,1... | collective-permute-start | bytes 147464 | tf_op jit(solution)/shard_map/ppermute | solution.py:24
  25.8 5.3 %copy-start.4 = (f32[3,4096]{1,0:T(4,128)}, f32[3,4096]{1,0:T(4,128)S(1)}, u32[]{:S(2)}) copy-start(f32[3,4096]{1,0:T(4,128)S(1)} %collective-permute-done.2.dens_above_ref) | copy-start | bytes 147460
  31.1 0.6 %copy-start.5 = (f32[3,4096]{1,0:T(4,128)}, f32[3,4096]{1,0:T(4,128)S(1)}, u32[]{:S(2)}) copy-start(f32[3,4096]{1,0:T(4,128)S(1)} %collective-permute-done.3.dens_below_ref) | copy-start | bytes 147460
  31.1 0.7 %copy-start.3 = (f32[2,2,4,4096]{3,2,1,0:T(4,128)}, f32[2,2,4,4096]{3,2,1,0:T(4,128)S(1)}, u32[]{:S(2)}) copy-start(f32[2,2,4,4096]{3,2,1,0:T(4,128)S(1)} %collective-permute-done.1.src_below_ref) | copy-start | bytes 786436
